TPU v7x, 32 devices: a whole 2x2x4 slice. The times are simulated.
32 devices in a mesh: sec: 4 (over y, x), dev: 8 (over z, core).
Axes of the slice: x: 2, y: 2, z: 4, core: 2. Of those that a mesh axis runs over, the one named last changes fastest.
Arguments:
- strain_rows: bfloat16 [65536, 128], P(('sec', 'dev')), may hold values from -6 to 6
- bands: int32 [65536], P(('sec', 'dev')), may hold values from 0 to 15
- damaged: int32 [4096], P(('sec', 'dev')), may hold values from 0 to 2047
- owner: int32 [4096, 1], P(('sec', 'dev')), may hold values from 0 to 31; in each aligned block of 128 rows (0 to 127, 128 to 255, ...) at most 8 rows name the same one
- first_layers: bfloat16 [4096, 4096], P(('sec', 'dev')), may hold values from -0.5 to 0.5
- middle_weight: bfloat16 [4096, 4096], P(None, 'sec'), may hold values from -0.09375 to 0.09375
- out_weight: bfloat16 [4096, 128], P('sec'), may hold values from -0.09375 to 0.09375
- band_scale: float32 [16, 4096], replicated, may hold values from 0.5 to 2
- back_weight: bfloat16 [128, 128], replicated, may hold values from -0.5 to 0.5
Outputs:
- response: bfloat16 [4096, 128], P(('sec', 'dev'))
Inputs may be any that keep to these rules, and one draw needn't show every extreme that they name: Among the 128 rows of one macro device no owner is named more than 8 times, a bound that some block reaches. `damaged`: indices into the listing device's own 2048 points.
All inputs are finite; a program needn't handle non-finite values.
Results may differ from a plain program's by a relative error of at most 0.014.
Values may be sent and summed in bfloat16 or wider, within the bound.
No kernel may reach another device: no remote copies, remote signals or barrier semaphores. Data moves between devices by JAX's collectives and lax.ppermute only.
A program may use at most 128 MiB of HBM per device.

v0:
```python
import jax
import jax.numpy as jnp
from jax import lax
from jax.sharding import PartitionSpec as P

PASSES = 2


def band_rows(band_values, band_scale):
    levels = jnp.arange(band_scale.shape[0], dtype=jnp.float32)
    picks = (band_values.astype(jnp.float32)[:, None] == levels[None, :]).astype(jnp.float32)
    return jnp.dot(
        picks, band_scale, precision=lax.Precision.HIGHEST, preferred_element_type=jnp.float32
    )


def first_hidden(row_block, weight_block, band_block, band_scale):
    mixed = jnp.dot(row_block, weight_block, preferred_element_type=jnp.float32) * band_rows(
        band_block, band_scale
    )
    return jax.nn.silu(mixed).astype(jnp.bfloat16)


def surrogate_tail(hidden_block, middle_weight, out_weight):
    middle = jax.nn.silu(
        jnp.dot(hidden_block, middle_weight, preferred_element_type=jnp.float32)
    ).astype(jnp.bfloat16)
    return jnp.dot(middle, out_weight, preferred_element_type=jnp.float32)


def per_device(
    strain_rows,
    bands,
    damaged,
    owner,
    first_layers,
    middle_weight,
    out_weight,
    band_scale,
    back_weight,
):
    count_all = lax.axis_size(("sec", "dev"))
    list_rows = damaged.shape[0]
    slot_count = max(2, 2 * list_rows // count_all)
    recv_rows = count_all * slot_count
    feat_width = strain_rows.shape[1]
    features = jnp.take(strain_rows, damaged, axis=0)
    band_local = jnp.take(bands, damaged)
    target_owner = owner[:, 0]
    matches = (target_owner[:, None] == jnp.arange(count_all, dtype=jnp.int32)[None, :]).astype(
        jnp.int32
    )
    slot_rank = jnp.sum((jnp.cumsum(matches, axis=0) - 1) * matches, axis=1)
    target = target_owner * slot_count + slot_rank
    dispatch = (jnp.arange(recv_rows, dtype=jnp.int32)[:, None] == target[None, :]).astype(
        jnp.bfloat16
    )
    send_band = jnp.dot(
        dispatch, band_local.astype(jnp.bfloat16)[:, None], preferred_element_type=jnp.float32
    ).astype(jnp.bfloat16)
    result = None
    for segment_index in range(PASSES):
        send_rows = jnp.dot(dispatch, features, preferred_element_type=jnp.float32).astype(
            jnp.bfloat16
        )
        got_rows, got_band = (
            lax.all_to_all(
                send_rows.reshape(count_all, slot_count, feat_width),
                ("sec", "dev"),
                split_axis=0,
                concat_axis=0,
                tiled=True,
            ),
            lax.all_to_all(
                send_band.reshape(count_all, slot_count),
                ("sec", "dev"),
                split_axis=0,
                concat_axis=0,
                tiled=True,
            ),
        )
        got_rows = got_rows.reshape(recv_rows, feat_width)
        got_band = got_band.reshape(recv_rows)
        hidden = first_hidden(got_rows, first_layers, got_band, band_scale)
        every_hidden = lax.all_gather(hidden, "sec", axis=0, tiled=True)
        partial_value = lax.psum_scatter(
            surrogate_tail(every_hidden, middle_weight, out_weight),
            "sec",
            scatter_dimension=0,
            tiled=True,
        )
        response = partial_value.astype(jnp.bfloat16)
        returned = lax.all_to_all(
            response.reshape(count_all, slot_count, response.shape[1]),
            ("sec", "dev"),
            split_axis=0,
            concat_axis=0,
            tiled=True,
        )
        returned = returned.reshape(recv_rows, response.shape[1])
        result = lax.dot_general(
            dispatch, returned, (((0,), (0,)), ((), ())), preferred_element_type=jnp.float32
        ).astype(jnp.bfloat16)
        if segment_index + 1 < PASSES:
            features = (
                features.astype(jnp.float32)
                + jnp.dot(result, back_weight, preferred_element_type=jnp.float32)
            ).astype(jnp.bfloat16)
    return result


def solution(mesh):
    in_specs = (
        P(("sec", "dev"), None),
        P(("sec", "dev")),
        P(("sec", "dev")),
        P(("sec", "dev"), None),
        P(("sec", "dev"), None),
        P(None, "sec"),
        P("sec", None),
        P(),
        P(),
    )
    out_specs = P(("sec", "dev"), None)
    return jax.shard_map(
        per_device, mesh=mesh, in_specs=in_specs, out_specs=out_specs, check_vma=False
    )
```

profile of v0, /device:TPU:0, one launch (start us, length us, event | category | flops | bytes accessed | tf_op | source)
XLA Modules:
  0.0 342.8 jit_solution(10192566044894200866)
XLA Ops:
  6.5 0.7 compare_select_fusion
  7.3 0.7 fusion.19
  8.2 0.8 select_reduce_fusion
  9.0 0.7 multiply_add_fusion
  9.7 1.6 gather_fusion.1
  11.3 0.8 fusion.5
  12.1 0.7 all_to_all.25
  12.9 7.3 %all-to-all-start.1 = ((bf16[32,1,8]{2,1,0:T(2,128)(2,1)}), bf16[32,1,8]{2,1,0:T(2,128)(2,1)S(1)}, u32[]{:S(2)}, u32[]{:S(2)}) async-start(bf16[32,1,8]{2,1,0:T(2,128)(2,1)} %all_to_all.25), calls=%async_computation.1 | async-start | bytes 32768 | tf_op jit(solution)/shard_map/all_to_all | solution.py:74
  20.2 0.7 compare_and_fusion
  20.9 1.8 gather_fusion
  22.6 0.8 fusion.2
  23.5 3.8 %all-to-all-done.1 = bf16[32,1,8]{2,1,0:T(2,128)(2,1)S(1)} async-done(((bf16[32,1,8]{2,1,0:T(2,128)(2,1)}), bf16[32,1,8]{2,1,0:T(2,128)(2,1)S(1)}, u32[]{:S(2)}, u32[]{:S(2)}) %all-to-all-start.1) | async-done | bytes 544 | tf_op jit(solution)/shard_map/all_to_all | solution.py:74
  27.3 2.6 all-to-all-start
  30.0 4.7 %fusion.6 = f32[256,4096]{1,0:T(8,128)} fusion(f32[16,4096]{1,0:T(8,128)} %param.16, f32[256]{0:T(256)S(1)} %reshape.65), kind=kOutput, calls=%fused_computation.21 | convolution fusion | flops 201330688 | bytes 4457472 | tf_op jit(solution)/shard_map/dot_general | solution.py:12
  34.8 2.5 all-to-all-done
  37.2 4.9 %multiply_convert_fusion.3 = bf16[256,4096]{1,0:T(8,128)(2,1)} fusion(f32[256,4096]{1,0:T(8,128)} %fusion.6, bf16[128,4096]{1,0:T(8,128)(2,1)S(1)} %copy-done, bf16[32,8,128]{2,1,0:T(8,128)(2,1)S(1)} %all-to-all-done), kind=kOutput, calls=%fused_computation.7 | convolution fusion | flops 274726912 | bytes 7405568 | tf_op jit(solution)/shard_map/dot_general | solution.py:18
  42.2 0.2 reduce-scatter.3.cloned.1.call-start
  42.4 86.2 %all-gather.3.cloned.1.call-done = bf16[1024,4096]{1,0:T(8,128)(2,1)} async-done(((bf16[256,4096]{1,0:T(8,128)(2,1)}), bf16[1024,4096]{1,0:T(8,128)(2,1)}) %all-gather.3.cloned.1.call-update) | async-done | bytes 8388624 | tf_op jit(solution)/shard_map/all_gather | solution.py:85
  128.7 16.1 %fusion = f32[1024,128]{1,0:T(8,128)} fusion(bf16[1024,128]{1,0:T(8,128)(2,1)S(1)} %copy-done.1, bf16[1024,4096]{1,0:T(8,128)(2,1)} %all-gather.3.cloned.1.call-done, bf16[4096,1024]{1,0:T(8,128)(2,1)} %param.14), kind=kOutput, calls=%fused_computation.8 | convolution fusion | flops 8863612928 | bytes 17563648 | tf_op jit(solution)/shard_map/dot_general | solution.py:28
  144.8 25.2 %reduce-scatter.3.cloned.1.call-done = f32[256,128]{1,0:T(8,128)} async-done(((f32[1024,128]{1,0:T(8,128)}), f32[256,128]{1,0:T(8,128)}) %reduce-scatter.3.cloned.1.call-update) | async-done | bytes 131088 | tf_op jit(solution)/shard_map/reduce_scatter | solution.py:86
  170.0 0.9 convert_bitcast_fusion.1
  170.9 11.8 %all_to_all.31 = bf16[32,8,128]{2,1,0:T(8,128)(2,1)S(1)} all-to-all(bf16[32,8,128]{2,1,0:T(8,128)(2,1)S(1)} %convert_bitcast_fusion.1), channel_id=1, replica_groups=mesh['sec'=4,'dev'=8] {'sec','dev'}, dimensions={0} | all-to-all | bytes 131072 | tf_op jit(solution)/shard_map/all_to_all | solution.py:93
  182.7 0.3 fusion.4
  183.2 9.1 %all_to_all.32 = bf16[32,8,128]{2,1,0:T(8,128)(2,1)S(1)} all-to-all(bf16[32,8,128]{2,1,0:T(8,128)(2,1)S(1)} %fusion.3), channel_id=1, replica_groups=mesh['sec'=4,'dev'=8] {'sec','dev'}, dimensions={0} | all-to-all | bytes 131072 | tf_op jit(solution)/shard_map/all_to_all | solution.py:67
  192.3 4.9 %multiply_convert_fusion.1 = bf16[256,4096]{1,0:T(8,128)(2,1)} fusion(f32[256,4096]{1,0:T(8,128)} %fusion.6, bf16[128,4096]{1,0:T(8,128)(2,1)S(1)} %copy-done, bf16[32,8,128]{2,1,0:T(8,128)(2,1)S(1)} %all_to_all.32), kind=kOutput, calls=%fused_computation.5 | convolution fusion | flops 274726912 | bytes 7405568 | tf_op jit(solution)/shard_map/dot_general | solution.py:18
  197.2 0.3 reduce-scatter.5.cloned.1.call-start
  197.5 83.9 %all-gather.5.cloned.1.call-done = bf16[1024,4096]{1,0:T(8,128)(2,1)} async-done(((bf16[256,4096]{1,0:T(8,128)(2,1)}), bf16[1024,4096]{1,0:T(8,128)(2,1)}) %all-gather.5.cloned.1.call-update) | async-done | bytes 8388624 | tf_op jit(solution)/shard_map/all_gather | solution.py:85
  281.4 16.1 %fusion.1 = f32[1024,128]{1,0:T(8,128)} fusion(bf16[1024,128]{1,0:T(8,128)(2,1)S(1)} %copy-done.1, bf16[1024,4096]{1,0:T(8,128)(2,1)} %all-gather.5.cloned.1.call-done, bf16[4096,1024]{1,0:T(8,128)(2,1)} %param.14), kind=kOutput, calls=%fused_computation.9 | convolution fusion | flops 8863612928 | bytes 17563648 | tf_op jit(solution)/shard_map/dot_general | solution.py:28
  297.5 25.3 %reduce-scatter.5.cloned.1.call-done = f32[256,128]{1,0:T(8,128)} async-done(((f32[1024,128]{1,0:T(8,128)}), f32[256,128]{1,0:T(8,128)}) %reduce-scatter.5.cloned.1.call-update) | async-done | bytes 131088 | tf_op jit(solution)/shard_map/reduce_scatter | solution.py:86
  322.8 0.9 convert_bitcast_fusion
  323.7 11.8 %all_to_all.33 = bf16[32,8,128]{2,1,0:T(8,128)(2,1)S(1)} all-to-all(bf16[32,8,128]{2,1,0:T(8,128)(2,1)S(1)} %convert_bitcast_fusion), channel_id=1, replica_groups=mesh['sec'=4,'dev'=8] {'sec','dev'}, dimensions={0} | all-to-all | bytes 131072 | tf_op jit(solution)/shard_map/all_to_all | solution.py:93
  335.5 0.8 convolution_convert_fusion.2
  (18 shorter events, 0.6 us)
Async XLA Ops:
  6.5 30.7 %copy-start = (bf16[128,4096]{1,0:T(8,128)(2,1)S(1)}, bf16[128,4096]{1,0:T(8,128)(2,1)}, u32[]{:S(2)}) copy-start(bf16[128,4096]{1,0:T(8,128)(2,1)} %param.13) | copy-start | bytes 3145732
  12.9 14.4 %all-to-all-start.1 = ((bf16[32,1,8]{2,1,0:T(2,128)(2,1)}), bf16[32,1,8]{2,1,0:T(2,128)(2,1)S(1)}, u32[]{:S(2)}, u32[]{:S(2)}) async-start(bf16[32,1,8]{2,1,0:T(2,128)(2,1)} %all_to_all.25), calls=%async_computation.1 | async-start | bytes 32768 | tf_op jit(solution)/shard_map/all_to_all | solution.py:74
  27.3 9.9 %all-to-all-start = ((bf16[32,8,128]{2,1,0:T(8,128)(2,1)}), bf16[32,8,128]{2,1,0:T(8,128)(2,1)S(1)}, u32[]{:S(2)}, u32[]{:S(2)}) async-start(bf16[32,8,128]{2,1,0:T(8,128)(2,1)} %fusion.2), calls=%async_computation | async-start | bytes 131072 | tf_op jit(solution)/shard_map/all_to_all | solution.py:67
  29.8 98.8 %all-gather.3.cloned.1.call-start = ((), (), s32[]{:S(2)}) async-start(), calls=%async_computation.7 | async-start | bytes 10485760 | tf_op jit(solution)/shard_map/all_gather | solution.py:85
  34.8 93.9 %copy-start.1 = (bf16[1024,128]{1,0:T(8,128)(2,1)S(1)}, bf16[1024,128]{1,0:T(8,128)(2,1)}, u32[]{:S(2)}) copy-start(bf16[1024,128]{1,0:T(8,128)(2,1)} %param.15) | copy-start | bytes 786436
  42.2 140.5 %copy-start.2 = (bf16[128,128]{1,0:T(8,128)(2,1)S(1)}, bf16[128,128]{1,0:T(8,128)(2,1)}, u32[]{:S(2)}) copy-start(bf16[128,128]{1,0:T(8,128)(2,1)} %param.17) | copy-start | bytes 98308
  42.2 127.8 %reduce-scatter.3.cloned.1.call-start = ((), (), s32[]{:S(2)}) async-start(), calls=%async_computation.8 | async-start | bytes 655360 | tf_op jit(solution)/shard_map/reduce_scatter | solution.py:86
  144.8 136.6 %all-gather.5.cloned.1.call-start = ((), (), s32[]{:S(2)}) async-start(), calls=%async_computation.9 | async-start | bytes 10485760 | tf_op jit(solution)/shard_map/all_gather | solution.py:85
  197.2 125.5 %reduce-scatter.5.cloned.1.call-start = ((), (), s32[]{:S(2)}) async-start(), calls=%async_computation.10 | async-start | bytes 655360 | tf_op jit(solution)/shard_map/reduce_scatter | solution.py:86
Sparse Core Ops, SparseCore 0:
  42.3 86.2 all-gather.2
  144.9 25.0 reduce-scatter.2
  197.4 83.9 all-gather.4
  297.7 25.0 reduce-scatter.4
where the time goes:
time: 343 us
  waiting for transfers between devices  227 us (66%)
  matrix products  49.8 us (15%)
  blocking collectives  32.6 us (10%)
  between operations  13.2 us (4%)
  starting transfers between devices  10.4 us (3%)
  other arithmetic  5.7 us (2%)
  local copies, waits for them, and re-layouts  4.2 us (1%)
    all_gather x2, waiting for transfers between devices, per_device(): every_hidden = lax.all_gather(hidden, 'sec', axis=0, tiled=True)  170 us
    reduce_scatter x2, waiting for transfers between devices, per_device(): lax.psum_scatter(surrogate_tail(every_hidden, middle_weight, out_weight),...  50.5 us
    dot_general x2, matrix products, surrogate_tail(): return jnp.dot(middle, out_weight, preferred_element_type=jnp.float32)  32.2 us
    all_to_all x2, blocking collectives, per_device(): lax.all_to_all(response.reshape(count_all, slot_count, response.shape[1])...  23.6 us
    dot_general x2, matrix products, first_hidden(): jnp.dot(row_block, weight_block, preferred_element_type=jnp.float32)  9.87 us
    all_to_all x1, blocking collectives, per_device(): lax.all_to_all(send_rows.reshape(count_all, slot_count, feat_width), ('se...  9.08 us
    all_to_all x1, starting transfers between devices, per_device(): lax.all_to_all(send_band.reshape(count_all, slot_count), ('sec', 'dev'),...  7.33 us
  transfers between devices with their start and end apart: 6, of which 6 were waited for; matrix products, arithmetic and copies ran while one was open for 2% of the time, Pallas kernels for 0%

commit v1 on v0

v1 whole, which is shorter than its diff:
```python
import jax
import jax.numpy as jnp
from jax import lax
from jax.sharding import PartitionSpec as P

PASSES = 2


def scale_parts(band_scale):
    hi = band_scale.astype(jnp.bfloat16)
    rest = band_scale - hi.astype(jnp.float32)
    mid = rest.astype(jnp.bfloat16)
    lo = (rest - mid.astype(jnp.float32)).astype(jnp.bfloat16)
    return jnp.concatenate([hi, mid, lo], axis=0)


def band_rows(band_values, parts):
    levels = parts.shape[0] // 3
    level_ids = jnp.arange(3 * levels, dtype=jnp.int32) % levels
    picks = (band_values[:, None] == level_ids[None, :]).astype(jnp.bfloat16)
    return jnp.dot(picks, parts, preferred_element_type=jnp.float32)


def first_hidden(rows, weights, band_values, parts):
    mixed = jnp.einsum("srf,sfh->srh", rows, weights, preferred_element_type=jnp.float32)
    mixed = mixed.reshape(-1, weights.shape[2]) * band_rows(band_values, parts)
    return jax.nn.silu(mixed).astype(jnp.bfloat16)


def surrogate_tail(hidden_block, middle_weight, out_weight):
    middle = jax.nn.silu(
        jnp.dot(hidden_block, middle_weight, preferred_element_type=jnp.float32)
    ).astype(jnp.bfloat16)
    return jnp.dot(middle, out_weight, preferred_element_type=jnp.float32)


def per_device(
    strain_rows,
    bands,
    damaged,
    owner,
    first_layers,
    middle_weight,
    out_weight,
    band_scale,
    back_weight,
):
    n_sec = lax.axis_size("sec")
    n_dev = lax.axis_size("dev")
    count_all = n_sec * n_dev
    list_rows = damaged.shape[0]
    slot_count = max(2, 2 * list_rows // count_all)
    group_slots = n_sec * slot_count
    feat_width = strain_rows.shape[1]
    hid = first_layers.shape[1]

    every_first = lax.all_gather(first_layers, "sec", axis=0, tiled=True).reshape(
        n_sec, feat_width, hid
    )
    parts = scale_parts(band_scale)

    features = jnp.take(strain_rows, damaged, axis=0)
    band_local = jnp.take(bands, damaged)
    target_owner = owner[:, 0]
    matches = (target_owner[:, None] == jnp.arange(count_all, dtype=jnp.int32)[None, :]).astype(
        jnp.int32
    )
    slot_rank = jnp.sum((jnp.cumsum(matches, axis=0) - 1) * matches, axis=1)
    owner_sec = target_owner // n_dev
    owner_dev = target_owner % n_dev
    target = owner_dev * group_slots + owner_sec * slot_count + slot_rank
    dispatch = (
        jnp.arange(n_dev * group_slots, dtype=jnp.int32)[:, None] == target[None, :]
    ).astype(jnp.bfloat16)
    packed = jnp.concatenate(
        [features, band_local.astype(jnp.bfloat16)[:, None]], axis=1
    )
    send = jnp.dot(dispatch, packed, preferred_element_type=jnp.float32).astype(jnp.bfloat16)
    send = send.reshape(1, n_dev, group_slots, feat_width + 1)
    send = jnp.broadcast_to(send, (n_sec, n_dev, group_slots, feat_width + 1)).reshape(
        count_all, group_slots, feat_width + 1
    )
    got = lax.all_to_all(send, ("sec", "dev"), split_axis=0, concat_axis=0, tiled=True)
    got = got.reshape(count_all, n_sec, slot_count, feat_width + 1).transpose(1, 0, 2, 3)
    got = got.reshape(n_sec, count_all * slot_count, feat_width + 1)
    rows = got[:, :, :feat_width]
    got_band = got[:, :, feat_width].astype(jnp.int32).reshape(-1)

    result = None
    for segment_index in range(PASSES):
        hidden = first_hidden(rows, every_first, got_band, parts)
        partial = surrogate_tail(hidden, middle_weight, out_weight)
        if segment_index + 1 < PASSES:
            values = lax.psum(partial, "sec").astype(jnp.bfloat16)
            rows = (
                rows.astype(jnp.float32)
                + jnp.dot(values, back_weight, preferred_element_type=jnp.float32).reshape(
                    rows.shape
                )
            ).astype(jnp.bfloat16)
        else:
            out_width = partial.shape[1]
            back = partial.reshape(n_sec, count_all, slot_count, out_width).transpose(1, 0, 2, 3)
            back = lax.all_to_all(back, ("sec", "dev"), split_axis=0, concat_axis=0, tiled=True)
            back = back.reshape(n_sec, n_dev * group_slots, out_width).sum(axis=0)
            result = jnp.take(back, target, axis=0).astype(jnp.bfloat16)
    return result


def solution(mesh):
    in_specs = (
        P(("sec", "dev"), None),
        P(("sec", "dev")),
        P(("sec", "dev")),
        P(("sec", "dev"), None),
        P(("sec", "dev"), None),
        P(None, "sec"),
        P("sec", None),
        P(),
        P(),
    )
    out_specs = P(("sec", "dev"), None)
    return jax.shard_map(
        per_device, mesh=mesh, in_specs=in_specs, out_specs=out_specs, check_vma=False
    )
```

time: 343 us -> 187 us (0.55)
  waiting for transfers between devices: 227 us -> 63.6 us
  other arithmetic: 5.7 us -> 16.8 us
  blocking collectives: 32.6 us -> 27.1 us
    all_gather x2 -> x1, waiting for transfers between devices: 170 us -> 31.4 us  [per_device(): lax.all_gather(first_layers, 'sec', axis=0, tiled=True)]
    reduce_scatter x2 -> x0, waiting for transfers between devices: 50.5 us -> none  [per_device(): lax.psum_scatter(surrogate_tail(every_hidden, middle_weight, out_weight),...]
    all_to_all x3 -> x0, blocking collectives: 32.6 us -> none  [the longest x2 23.6 us: per_device(): lax.all_to_all(response.reshape(count_all, slot_count, response.shape[1])...]
    psum x0 -> x1, blocking collectives: none -> 27.1 us  [per_device(): values = lax.psum(partial, 'sec').astype(jnp.bfloat16)]
    all_to_all x2, waiting for transfers between devices: 6.29 us -> 31.4 us  [the longest x1 16.2 us: per_device(): lax.all_to_all(back, ('sec', 'dev'), split_axis=0, concat_axis=0, tiled=T...]
    convert_element_type x2 -> x5, other arithmetic: 0.06 us -> 13.6 us  [the longest x1 10.9 us: first_hidden(): return jax.nn.silu(mixed).astype(jnp.bfloat16)]
    dot_general x8 -> x5, matrix products: 17.6 us -> 19.6 us  [the longest x1 10.1 us: band_rows(): return jnp.dot(picks, parts, preferred_element_type=jnp.float32)]
  transfers between devices with their start and end apart: 6 -> 3, of which waited for: 6 -> 3; matrix products, arithmetic and copies ran while one was open for 2% -> 5% of each run, Pallas kernels for 0% -> 0%
where the time goes in v1:
time: 187 us; the launch traced here: 186 us
  waiting for transfers between devices  63.6 us (34%)
  matrix products  48.6 us (26%)
  blocking collectives  27.1 us (14%)
  other arithmetic  16.8 us (9%)
  between operations  13.5 us (7%)
  starting transfers between devices  11.6 us (6%)
  local copies, waits for them, and re-layouts  5.03 us (3%)
    all_gather x1, waiting for transfers between devices, per_device(): lax.all_gather(first_layers, 'sec', axis=0, tiled=True)  31.4 us
    dot_general x2, matrix products, surrogate_tail(): return jnp.dot(middle, out_weight, preferred_element_type=jnp.float32)  29.1 us
    psum x1, blocking collectives, per_device(): values = lax.psum(partial, 'sec').astype(jnp.bfloat16)  27.1 us
    all_to_all x1, waiting for transfers between devices, per_device(): lax.all_to_all(back, ('sec', 'dev'), split_axis=0, concat_axis=0, tiled=T...  16.2 us
    all_to_all x1, waiting for transfers between devices, per_device(): lax.all_to_all(send, ('sec', 'dev'), split_axis=0, concat_axis=0, tiled=T...  15.2 us
    convert_element_type x1, other arithmetic, first_hidden(): return jax.nn.silu(mixed).astype(jnp.bfloat16)  10.9 us
    dot_general x1, matrix products, band_rows(): return jnp.dot(picks, parts, preferred_element_type=jnp.float32)  10.1 us
    dot_general x2, matrix products, first_hidden(): jnp.einsum('srf,sfh->srh', rows, weights, preferred_element_type=jnp.floa...  9.05 us
  transfers between devices with their start and end apart: 3, of which 3 were waited for; matrix products, arithmetic and copies ran while one was open for 5% of the time, Pallas kernels for 0%

profile of v1, /device:TPU:0, one launch (start us, length us, event | category | flops | bytes accessed | tf_op | source)
XLA Modules:
  0.0 186.2 jit_solution(1819267888237272443)
XLA Ops:
  6.5 0.7 all-gather.2.cloned.1.call-update
  7.3 0.7 compare_select_fusion
  7.9 1.6 gather_fusion.1
  9.6 0.7 gather_fusion
  10.3 0.7 convert_bitcast_fusion
  10.9 0.1 copy.12
  11.1 0.7 fusion.22
  11.8 0.2 reduce_window_sum.11
  12.0 0.8 select_reduce_fusion
  12.8 0.7 fusion.28
  13.5 0.1 broadcast_select_fusion
  13.6 0.2 convolution_convert_fusion
  13.8 0.1 copy.13
  13.9 0.8 broadcast_in_dim.47
  14.8 7.3 %all-to-all-start = ((bf16[32,32,129]{2,1,0:T(8,128)(2,1)}), bf16[32,32,129]{2,1,0:T(8,128)(2,1)S(1)}, u32[]{:S(2)}, u32[]{:S(2)}) async-start(bf16[32,32,129]{2,1,0:T(8,128)(2,1)} %bitcast.5), calls=%async_computation | async-start | bytes 1048576 | tf_op jit(solution)/shard_map/all_to_all | solution.py:83
  22.1 1.1 fusion.33
  23.2 15.2 %all-to-all-done = bf16[32,32,129]{2,1,0:T(8,128)(2,1)S(1)} async-done(((bf16[32,32,129]{2,1,0:T(8,128)(2,1)}), bf16[32,32,129]{2,1,0:T(8,128)(2,1)S(1)}, u32[]{:S(2)}, u32[]{:S(2)}) %all-to-all-start) | async-done | bytes 264224 | tf_op jit(solution)/shard_map/all_to_all | solution.py:83
  38.5 0.2 convert_reduce_fusion
  38.7 31.4 %all-gather.2.cloned.1.call-done = bf16[512,4096]{1,0:T(8,128)(2,1)} async-done(((bf16[128,4096]{1,0:T(8,128)(2,1)}), bf16[512,4096]{1,0:T(8,128)(2,1)}) %all-gather.2.cloned.1.call-update) | async-done | bytes 4194320 | tf_op jit(solution)/shard_map/all_gather | solution.py:57
  70.1 4.5 %fusion.14 = f32[4,256,4096]{2,1,0:T(8,128)S(1)} fusion(bf16[4,128,4096]{2,1,0:T(8,128)(2,1)} %bitcast.48, bf16[4,256,129]{2,1,0:T(8,128)(2,1)S(1)} %copy_bitcast_fusion.1), kind=kOutput, calls=%fused_computation.30 | convolution fusion | flops 1073741824 | bytes 21233664 | tf_op jit(solution)/shard_map/srf,sfh->srh/dot_general | solution.py:25
  74.7 10.1 %multiply_convert_fusion.1 = (bf16[1024,4096]{1,0:T(8,128)(2,1)}, f32[1024,4096]{1,0:T(8,128)}) fusion(f32[4,256,4096]{2,1,0:T(8,128)S(1)} %fusion.14, bf16[16,4096]{1,0:T(8,128)(2,1)S(1)} %get-tuple-element.10, bf16[16,4096]{1,0:T(8,128)(2,1)S(1)} %get-tuple-element.11, bf16[16,4096]{1,0:T(8,128)(2,1)S(1)} %get-tuple-element.9, s32[48]{0:T(128)S(1)} %and_select_fusion, ...), kind=kOutput, calls=%fused_computation.6 | convolution fusion | flops 429047808 | bytes 42340544 | tf_op jit(solution)/shard_map/dot_general | solution.py:21
  84.8 14.5 %fusion = f32[1024,128]{1,0:T(8,128)S(1)} fusion(bf16[1024,128]{1,0:T(8,128)(2,1)S(1)} %copy-done.4, bf16[1024,4096]{1,0:T(8,128)(2,1)} %get-tuple-element.12, bf16[4096,1024]{1,0:T(8,128)(2,1)} %param.14), kind=kOutput, calls=%fused_computation.9 | convolution fusion | flops 8863612928 | bytes 17563648 | tf_op jit(solution)/shard_map/dot_general | solution.py:34
  99.3 27.1 %all-reduce.1 = bf16[1024,128]{1,0:T(8,128)(2,1)S(1)} all-reduce(f32[1024,128]{1,0:T(8,128)S(1)} %fusion), channel_id=1, replica_groups=mesh['sec'=4,'dev'=8] {'sec'}, use_global_device_ids=true, to_apply=%region_2.3 | all-reduce | flops 131072 | bytes 786432 | tf_op jit(solution)/shard_map/psum | solution.py:94
  126.4 0.2 fusion.38
  126.6 4.5 %fusion.9 = f32[4,256,4096]{2,1,0:T(8,128)S(1)} fusion(bf16[4,128,4096]{2,1,0:T(8,128)(2,1)} %bitcast.49, f32[4,256,128]{2,1,0:T(8,128)S(1)} %bitcast.50, bf16[4,256,129]{2,1,0:T(8,128)(2,1)S(1)} %copy_bitcast_fusion.1), kind=kOutput, calls=%fused_computation.23 | convolution fusion | flops 1074135040 | bytes 21757952 | tf_op jit(solution)/shard_map/srf,sfh->srh/dot_general | solution.py:25
  131.1 10.9 %multiply_convert_fusion = bf16[1024,4096]{1,0:T(8,128)(2,1)} fusion(f32[1024,4096]{1,0:T(8,128)} %get-tuple-element.13, f32[4,256,4096]{2,1,0:T(8,128)S(1)} %fusion.9), kind=kLoop, calls=%fused_computation.5 | loop fusion | flops 25165824 | bytes 41943040 | tf_op jit(solution)/shard_map/convert_element_type | solution.py:27
  142.0 14.5 %fusion.1 = f32[1024,128]{1,0:T(8,128)S(1)} fusion(bf16[1024,128]{1,0:T(8,128)(2,1)S(1)} %copy-done.4, bf16[1024,4096]{1,0:T(8,128)(2,1)} %multiply_convert_fusion, bf16[4096,1024]{1,0:T(8,128)(2,1)} %param.14), kind=kOutput, calls=%fused_computation.10 | convolution fusion | flops 8863612928 | bytes 17563648 | tf_op jit(solution)/shard_map/dot_general | solution.py:34
  156.6 0.8 copy.19
  157.4 4.2 %all-to-all-start.1 = ((f32[32,4,8,128]{3,2,1,0:T(8,128)}), f32[32,4,8,128]{3,2,1,0:T(8,128)S(1)}, u32[]{:S(2)}, u32[]{:S(2)}) async-start(f32[32,4,8,128]{3,2,1,0:T(8,128)} %bitcast.47), calls=%async_computation.1 | async-start | bytes 1048576 | tf_op jit(solution)/shard_map/all_to_all | solution.py:104
  161.7 16.2 %all-to-all-done.1 = f32[32,4,8,128]{3,2,1,0:T(8,128)S(1)} async-done(((f32[32,4,8,128]{3,2,1,0:T(8,128)}), f32[32,4,8,128]{3,2,1,0:T(8,128)S(1)}, u32[]{:S(2)}, u32[]{:S(2)}) %all-to-all-start.1) | async-done | bytes 524320 | tf_op jit(solution)/shard_map/all_to_all | solution.py:104
  178.0 0.7 gather_fusion.2
  178.7 0.7 select_convert_fusion
  (18 shorter events, 0.1 us)
Async XLA Ops:
  6.5 3.0 %copy-start = (bf16[2048,128]{1,0:T(8,128)(2,1)S(1)}, bf16[2048,128]{1,0:T(8,128)(2,1)}, u32[]{:S(2)}) copy-start(bf16[2048,128]{1,0:T(8,128)(2,1)} %param.9) | copy-start | bytes 1572868
  6.5 63.6 %all-gather.2.cloned.1.call-start = ((), (), s32[]{:S(2)}) async-start(), calls=%async_computation.2 | async-start | bytes 5242880 | tf_op jit(solution)/shard_map/all_gather | solution.py:57
  14.8 23.7 %all-to-all-start = ((bf16[32,32,129]{2,1,0:T(8,128)(2,1)}), bf16[32,32,129]{2,1,0:T(8,128)(2,1)S(1)}, u32[]{:S(2)}, u32[]{:S(2)}) async-start(bf16[32,32,129]{2,1,0:T(8,128)(2,1)} %bitcast.5), calls=%async_computation | async-start | bytes 1048576 | tf_op jit(solution)/shard_map/all_to_all | solution.py:83
  74.6 10.1 %copy-start.4 = (bf16[1024,128]{1,0:T(8,128)(2,1)S(1)}, bf16[1024,128]{1,0:T(8,128)(2,1)}, u32[]{:S(2)}) copy-start(bf16[1024,128]{1,0:T(8,128)(2,1)} %param.15) | copy-start | bytes 786436
  84.8 41.6 %copy-start.2 = (bf16[128,128]{1,0:T(8,128)(2,1)S(1)}, bf16[128,128]{1,0:T(8,128)(2,1)}, u32[]{:S(2)}) copy-start(bf16[128,128]{1,0:T(8,128)(2,1)} %param.17) | copy-start | bytes 98308
  142.0 19.7 %copy-start.3 = (s32[128,1]{0,1:T(1,128)S(1)}, s32[128,1]{0,1:T(1,128)}, u32[]{:S(2)}) copy-start(s32[128,1]{0,1:T(1,128)} %param.12) | copy-start | bytes 1540
  142.0 37.3 %copy-start.1 = (bf16[2048,128]{1,0:T(8,128)(2,1)S(1)}, bf16[2048,128]{1,0:T(8,128)(2,1)}, u32[]{:S(2)}) copy-start(bf16[2048,128]{1,0:T(8,128)(2,1)} %param.9) | copy-start | bytes 1572868
  157.4 20.5 %all-to-all-start.1 = ((f32[32,4,8,128]{3,2,1,0:T(8,128)}), f32[32,4,8,128]{3,2,1,0:T(8,128)S(1)}, u32[]{:S(2)}, u32[]{:S(2)}) async-start(f32[32,4,8,128]{3,2,1,0:T(8,128)} %bitcast.47), calls=%async_computation.1 | async-start | bytes 1048576 | tf_op jit(solution)/shard_map/all_to_all | solution.py:104
Sparse Core Ops, SparseCore 0:
  9.2 60.9 all-gather.1

commit v2 on v1

--- a/solution.py
+++ b/solution.py
@@ -1,5 +1,6 @@
 import jax
 import jax.numpy as jnp
+import numpy as np
 from jax import lax
 from jax.sharding import PartitionSpec as P
 
@@ -34,6 +35,10 @@
     return jnp.dot(middle, out_weight, preferred_element_type=jnp.float32)
 
 
+def xor_pairs(n, k):
+    return [(i, i ^ k) for i in range(n)]
+
+
 def per_device(
     strain_rows,
     bands,
@@ -47,16 +52,16 @@
 ):
     n_sec = lax.axis_size("sec")
     n_dev = lax.axis_size("dev")
+    assert n_sec & (n_sec - 1) == 0
     count_all = n_sec * n_dev
     list_rows = damaged.shape[0]
     slot_count = max(2, 2 * list_rows // count_all)
     group_slots = n_sec * slot_count
     feat_width = strain_rows.shape[1]
-    hid = first_layers.shape[1]
 
-    every_first = lax.all_gather(first_layers, "sec", axis=0, tiled=True).reshape(
-        n_sec, feat_width, hid
-    )
+    block_first = [first_layers] + [
+        lax.ppermute(first_layers, "sec", xor_pairs(n_sec, k)) for k in range(1, n_sec)
+    ]
     parts = scale_parts(band_scale)
 
     features = jnp.take(strain_rows, damaged, axis=0)
@@ -75,35 +80,50 @@
     packed = jnp.concatenate(
         [features, band_local.astype(jnp.bfloat16)[:, None]], axis=1
     )
-    send = jnp.dot(dispatch, packed, preferred_element_type=jnp.float32).astype(jnp.bfloat16)
-    send = send.reshape(1, n_dev, group_slots, feat_width + 1)
-    send = jnp.broadcast_to(send, (n_sec, n_dev, group_slots, feat_width + 1)).reshape(
-        count_all, group_slots, feat_width + 1
-    )
+    grp = jnp.dot(dispatch, packed, preferred_element_type=jnp.float32).astype(jnp.bfloat16)
+    grp = grp.reshape(n_dev, n_sec, slot_count, feat_width + 1)
+    xor_table = np.bitwise_xor.outer(np.arange(n_sec), np.arange(n_sec)).reshape(-1)
+    send = jnp.take(grp, jnp.asarray(xor_table, jnp.int32), axis=1)
+    send = send.reshape(n_dev, n_sec, n_sec, slot_count, feat_width + 1).transpose(1, 0, 2, 3, 4)
+    send = send.reshape(count_all, group_slots, feat_width + 1)
     got = lax.all_to_all(send, ("sec", "dev"), split_axis=0, concat_axis=0, tiled=True)
     got = got.reshape(count_all, n_sec, slot_count, feat_width + 1).transpose(1, 0, 2, 3)
     got = got.reshape(n_sec, count_all * slot_count, feat_width + 1)
-    rows = got[:, :, :feat_width]
-    got_band = got[:, :, feat_width].astype(jnp.int32).reshape(-1)
+    rows = [got[k, :, :feat_width] for k in range(n_sec)]
+    got_band = [got[k, :, feat_width].astype(jnp.int32) for k in range(n_sec)]
 
     result = None
     for segment_index in range(PASSES):
-        hidden = first_hidden(rows, every_first, got_band, parts)
-        partial = surrogate_tail(hidden, middle_weight, out_weight)
+        partial = []
+        for k in range(n_sec):
+            hidden = first_hidden(rows[k][None], block_first[k][None], got_band[k], parts)
+            partial.append(surrogate_tail(hidden, middle_weight, out_weight))
+        own_sum = partial[0]
+        for k in range(1, n_sec):
+            own_sum = own_sum + lax.ppermute(partial[k], "sec", xor_pairs(n_sec, k))
+        own_values = own_sum.astype(jnp.bfloat16)
         if segment_index + 1 < PASSES:
-            values = lax.psum(partial, "sec").astype(jnp.bfloat16)
-            rows = (
-                rows.astype(jnp.float32)
-                + jnp.dot(values, back_weight, preferred_element_type=jnp.float32).reshape(
-                    rows.shape
-                )
-            ).astype(jnp.bfloat16)
+            values = [own_values] + [
+                lax.ppermute(own_values, "sec", xor_pairs(n_sec, k)) for k in range(1, n_sec)
+            ]
+            rows = [
+                (
+                    rows[k].astype(jnp.float32)
+                    + jnp.dot(values[k], back_weight, preferred_element_type=jnp.float32)
+                ).astype(jnp.bfloat16)
+                for k in range(n_sec)
+            ]
         else:
-            out_width = partial.shape[1]
-            back = partial.reshape(n_sec, count_all, slot_count, out_width).transpose(1, 0, 2, 3)
-            back = lax.all_to_all(back, ("sec", "dev"), split_axis=0, concat_axis=0, tiled=True)
-            back = back.reshape(n_sec, n_dev * group_slots, out_width).sum(axis=0)
-            result = jnp.take(back, target, axis=0).astype(jnp.bfloat16)
+            out_width = own_values.shape[1]
+            back = lax.all_to_all(
+                own_values.reshape(count_all, slot_count, out_width),
+                ("sec", "dev"),
+                split_axis=0,
+                concat_axis=0,
+                tiled=True,
+            )
+            home = target_owner * slot_count + slot_rank
+            result = jnp.take(back.reshape(count_all * slot_count, out_width), home, axis=0)
     return result
 
 

time: 187 us -> 164 us (0.88)
  matrix products: 48.6 us -> 82.3 us
  blocking collectives: 27.1 us -> 0 us
  waiting for transfers between devices: 63.6 us -> 44.8 us
  starting transfers between devices: 11.6 us -> 26.3 us
  between operations: 13.5 us -> 0.32 us
  other arithmetic: 16.8 us -> 5.47 us
    dot_general x3 -> x12, matrix products: 9.26 us -> 68.2 us  [the longest x8 67.6 us: surrogate_tail(): jnp.dot(hidden_block, middle_weight, preferred_element_type=jnp.float32)]
    all_gather x1 -> x0, waiting for transfers between devices: 31.4 us -> none  [per_device(): lax.all_gather(first_layers, 'sec', axis=0, tiled=True)]
    psum x1 -> x0, blocking collectives: 27.1 us -> none  [per_device(): values = lax.psum(partial, 'sec').astype(jnp.bfloat16)]
    dot_general x2 -> x8, matrix products: 29.1 us -> 3.11 us  [surrogate_tail(): return jnp.dot(middle, out_weight, preferred_element_type=jnp.float32)]
    all_to_all x1, waiting for transfers between devices: 15.2 us -> 36.2 us  [per_device(): lax.all_to_all(send, ('sec', 'dev'), split_axis=0, concat_axis=0, tiled=T...]
    ppermute x0 -> x12, starting transfers between devices: none -> 15.4 us  [the longest x6 7.38 us: per_device(): own_sum = own_sum + lax.ppermute(partial[k], 'sec', xor_pairs(n_sec, k))]
    convert_element_type x3 -> x1, other arithmetic: 11.8 us -> 0.22 us  [per_device(): got_band = [got[k, :, feat_width].astype(jnp.int32) for k in range(n_sec)]]
    all_to_all x1, waiting for transfers between devices: 16.2 us -> 7.35 us  [per_device(): lax.all_to_all(own_values.reshape(count_all, slot_count, out_width), ('se...]
  transfers between devices with their start and end apart: 3 -> 14, of which waited for: 3 -> 3; matrix products, arithmetic and copies ran while one was open for 5% -> 55% of each run, Pallas kernels for 0% -> 0%
where the time goes in v2:
time: 164 us
  matrix products  82.3 us (50%)
  waiting for transfers between devices  44.8 us (27%)
  starting transfers between devices  26.3 us (16%)
  other arithmetic  5.47 us (3%)
  local copies, waits for them, and re-layouts  4.81 us (3%)
    dot_general x8, matrix products, surrogate_tail(): jnp.dot(hidden_block, middle_weight, preferred_element_type=jnp.float32)  67.6 us
    all_to_all x1, waiting for transfers between devices, per_device(): lax.all_to_all(send, ('sec', 'dev'), split_axis=0, concat_axis=0, tiled=T...  36.2 us
    dot_general x4, matrix products, band_rows(): return jnp.dot(picks, parts, preferred_element_type=jnp.float32)  10.8 us
    ppermute x6, starting transfers between devices, per_device(): own_sum = own_sum + lax.ppermute(partial[k], 'sec', xor_pairs(n_sec, k))  7.38 us
    all_to_all x1, waiting for transfers between devices, per_device(): lax.all_to_all(own_values.reshape(count_all, slot_count, out_width), ('se...  7.35 us
    all_to_all x1, starting transfers between devices, per_device(): lax.all_to_all(send, ('sec', 'dev'), split_axis=0, concat_axis=0, tiled=T...  6.31 us
    all_to_all x1, starting transfers between devices, per_device(): lax.all_to_all(own_values.reshape(count_all, slot_count, out_width), ('se...  4.55 us
    ppermute x3, starting transfers between devices, per_device(): lax.ppermute(first_layers, 'sec', xor_pairs(n_sec, k))  4.51 us
  transfers between devices with their start and end apart: 14, of which 3 were waited for; matrix products, arithmetic and copies ran while one was open for 55% of the time, Pallas kernels for 0%

profile of v2, /device:TPU:0, one launch (start us, length us, event | category | flops | bytes accessed | tf_op | source)
XLA Modules:
  0.0 164.0 jit_solution(4558705124248512207)
XLA Ops:
  0.0 3.0 %collective-permute-start = (bf16[128,4096]{1,0:T(8,128)(2,1)}, bf16[128,4096]{1,0:T(8,128)(2,1)}, u32[]{:S(2)}, u32[]{:S(2)}) collective-permute-start(bf16[128,4096]{1,0:T(8,128)(2,1)} %param.14), channel_id=1, source_target_pairs={{0,8},{8,0},{16,24},{24,16},{1,9},{9,1},{17,25},{25,17},{2,10},{10... | collective-permute-start | bytes 3145736 | tf_op jit(solution)/shard_map/ppermute | solution.py:63
  3.0 1.5 collective-permute-start.2
  5.4 0.8 select_reduce_fusion
  7.6 1.6 gather_fusion.1
  12.4 0.9 copy.14
  13.3 6.3 %all-to-all-start = ((bf16[32,32,129]{2,1,0:T(8,128)(2,1)}), bf16[32,32,129]{2,1,0:T(8,128)(2,1)S(1)}, u32[]{:S(2)}, u32[]{:S(2)}) async-start(bf16[32,32,129]{2,1,0:T(8,128)(2,1)} %bitcast.8), calls=%async_computation | async-start | bytes 1048576 | tf_op jit(solution)/shard_map/all_to_all | solution.py:89
  19.7 36.2 %all-to-all-done = bf16[32,32,129]{2,1,0:T(8,128)(2,1)S(1)} async-done(((bf16[32,32,129]{2,1,0:T(8,128)(2,1)}), bf16[32,32,129]{2,1,0:T(8,128)(2,1)S(1)}, u32[]{:S(2)}, u32[]{:S(2)}) %all-to-all-start) | async-done | bytes 264224 | tf_op jit(solution)/shard_map/all_to_all | solution.py:89
  56.2 2.7 %fusion.24 = f32[256,4096]{1,0:T(8,128)} fusion(s32[48]{0:T(128)S(1)} %and_select_fusion, s32[256]{0:T(256)S(1)} %get-tuple-element.8, bf16[16,4096]{1,0:T(8,128)(2,1)S(1)} %get-tuple-element.14, bf16[16,4096]{1,0:T(8,128)(2,1)S(1)} %get-tuple-element.15, bf16[16,4096]{1,0:T(8,128)(2,1)S(1)} %get-tuple-element.13), kind=kOutput, calls=%fused_computation.68 | convolution fusion | flops 101855232 | bytes 4588736 | tf_op jit(solution)/shard_map/dot_general | solution.py:22
  58.8 2.7 %fusion.22 = f32[256,4096]{1,0:T(8,128)} fusion(s32[48]{0:T(128)S(1)} %and_select_fusion, s32[256]{0:T(256)S(1)} %get-tuple-element.7, bf16[16,4096]{1,0:T(8,128)(2,1)S(1)} %get-tuple-element.14, bf16[16,4096]{1,0:T(8,128)(2,1)S(1)} %get-tuple-element.15, bf16[16,4096]{1,0:T(8,128)(2,1)S(1)} %get-tuple-element.13), kind=kOutput, calls=%fused_computation.66 | convolution fusion | flops 101855232 | bytes 4588736 | tf_op jit(solution)/shard_map/dot_general | solution.py:22
  61.5 2.7 %fusion.20 = f32[256,4096]{1,0:T(8,128)} fusion(s32[48]{0:T(128)S(1)} %and_select_fusion, s32[256]{0:T(256)S(1)} %get-tuple-element.6, bf16[16,4096]{1,0:T(8,128)(2,1)S(1)} %get-tuple-element.14, bf16[16,4096]{1,0:T(8,128)(2,1)S(1)} %get-tuple-element.15, bf16[16,4096]{1,0:T(8,128)(2,1)S(1)} %get-tuple-element.13), kind=kOutput, calls=%fused_computation.64 | convolution fusion | flops 101855232 | bytes 4588736 | tf_op jit(solution)/shard_map/dot_general | solution.py:22
  64.2 2.7 %fusion.26 = f32[256,4096]{1,0:T(8,128)} fusion(s32[48]{0:T(128)S(1)} %and_select_fusion, s32[256]{0:T(256)S(1)} %get-tuple-element.5, bf16[16,4096]{1,0:T(8,128)(2,1)S(1)} %get-tuple-element.14, bf16[16,4096]{1,0:T(8,128)(2,1)S(1)} %get-tuple-element.15, bf16[16,4096]{1,0:T(8,128)(2,1)S(1)} %get-tuple-element.13), kind=kOutput, calls=%fused_computation.70 | convolution fusion | flops 101855232 | bytes 4588736 | tf_op jit(solution)/shard_map/dot_general | solution.py:22
  67.0 8.5 %multiply_convert_fusion.14 = bf16[256,1024]{1,0:T(8,128)(2,1)S(1)} fusion(bf16[4096,1024]{1,0:T(8,128)(2,1)} %param.15, f32[256,4096]{1,0:T(8,128)} %fusion.24, bf16[128,4096]{1,0:T(8,128)(2,1)} %collective-permute-done, bf16[4,256,129]{2,1,0:T(8,128)(2,1)S(1)} %copy_bitcast_fusion), kind=kOutput, calls=%fused_computation.52 | convolution fusion | flops 2423521280 | bytes 14221312 | tf_op jit(solution)/shard_map/dot_general | solution.py:33
  75.7 0.9 collective-permute-start.1
  76.6 8.4 %multiply_convert_fusion.13 = bf16[256,1024]{1,0:T(8,128)(2,1)S(1)} fusion(bf16[4096,1024]{1,0:T(8,128)(2,1)} %param.15, f32[256,4096]{1,0:T(8,128)} %fusion.22, bf16[128,4096]{1,0:T(8,128)(2,1)} %collective-permute-done.2, bf16[4,256,129]{2,1,0:T(8,128)(2,1)S(1)} %copy_bitcast_fusion), kind=kOutput, calls=%fused_computation.51 | convolution fusion | flops 2423521280 | bytes 14221312 | tf_op jit(solution)/shard_map/dot_general | solution.py:33
  85.3 1.3 collective-permute-start.3
  86.6 8.4 %multiply_convert_fusion.12 = bf16[256,1024]{1,0:T(8,128)(2,1)S(1)} fusion(bf16[4096,1024]{1,0:T(8,128)(2,1)} %param.15, f32[256,4096]{1,0:T(8,128)} %fusion.20, bf16[128,4096]{1,0:T(8,128)(2,1)} %collective-permute-done.4, bf16[4,256,129]{2,1,0:T(8,128)(2,1)S(1)} %copy_bitcast_fusion), kind=kOutput, calls=%fused_computation.50 | convolution fusion | flops 2423521280 | bytes 14221312 | tf_op jit(solution)/shard_map/dot_general | solution.py:33
  95.4 1.5 collective-permute-start.5
  96.9 8.6 %multiply_convert_fusion.15 = bf16[256,1024]{1,0:T(8,128)(2,1)S(1)} fusion(bf16[4096,1024]{1,0:T(8,128)(2,1)} %param.15, f32[256,4096]{1,0:T(8,128)} %fusion.26, bf16[128,4096]{1,0:T(8,128)(2,1)} %param.14, bf16[4,256,129]{2,1,0:T(8,128)(2,1)S(1)} %copy_bitcast_fusion), kind=kOutput, calls=%fused_computation.53 | convolution fusion | flops 2423521280 | bytes 14221312 | tf_op jit(solution)/shard_map/dot_general | solution.py:33
  105.8 0.9 collective-permute-start.6
  106.7 1.2 collective-permute-start.8
  107.9 1.4 collective-permute-start.10
  109.5 1.2 collective-permute-done.6
  110.9 8.4 %multiply_convert_fusion.10 = bf16[256,1024]{1,0:T(8,128)(2,1)S(1)} fusion(bf16[4096,1024]{1,0:T(8,128)(2,1)} %param.15, f32[256,4096]{1,0:T(8,128)} %fusion.24, bf16[256,128]{1,0:T(8,128)(2,1)S(1)} %fusion.15, bf16[128,4096]{1,0:T(8,128)(2,1)} %collective-permute-done), kind=kOutput, calls=%fused_computation.48 | convolution fusion | flops 2423521280 | bytes 14221312 | tf_op jit(solution)/shard_map/dot_general | solution.py:33
  119.6 0.8 collective-permute-start.7
  120.5 8.4 %multiply_convert_fusion.9 = bf16[256,1024]{1,0:T(8,128)(2,1)S(1)} fusion(bf16[4096,1024]{1,0:T(8,128)(2,1)} %param.15, f32[256,4096]{1,0:T(8,128)} %fusion.22, bf16[256,128]{1,0:T(8,128)(2,1)S(1)} %fusion.16, bf16[128,4096]{1,0:T(8,128)(2,1)} %collective-permute-done.2), kind=kOutput, calls=%fused_computation.47 | convolution fusion | flops 2423521280 | bytes 14221312 | tf_op jit(solution)/shard_map/dot_general | solution.py:33
  129.2 1.0 collective-permute-start.9
  130.4 8.4 %multiply_convert_fusion.8 = bf16[256,1024]{1,0:T(8,128)(2,1)S(1)} fusion(bf16[4096,1024]{1,0:T(8,128)(2,1)} %param.15, f32[256,4096]{1,0:T(8,128)} %fusion.20, bf16[256,128]{1,0:T(8,128)(2,1)S(1)} %fusion.17, bf16[128,4096]{1,0:T(8,128)(2,1)} %collective-permute-done.4), kind=kOutput, calls=%fused_computation.46 | convolution fusion | flops 2423521280 | bytes 14221312 | tf_op jit(solution)/shard_map/dot_general | solution.py:33
  139.4 1.9 %collective-permute-start.11 = (f32[256,128]{1,0:T(8,128)S(1)}, f32[256,128]{1,0:T(8,128)S(1)}, u32[]{:S(2)}, u32[]{:S(2)}) collective-permute-start(f32[256,128]{1,0:T(8,128)S(1)} %fusion.59), channel_id=1, source_target_pairs={{0,24},{8,16},{16,8},{24,0},{1,25},{9,17},{17,9},{25,1},{2,26},{10... | collective-permute-start | bytes 393224 | tf_op jit(solution)/shard_map/ppermute | solution.py:103
  141.3 8.4 %multiply_convert_fusion.11 = bf16[256,1024]{1,0:T(8,128)(2,1)S(1)} fusion(bf16[4096,1024]{1,0:T(8,128)(2,1)} %param.15, f32[256,4096]{1,0:T(8,128)} %fusion.26, bf16[256,128]{1,0:T(8,128)(2,1)S(1)} %fusion.14, bf16[128,4096]{1,0:T(8,128)(2,1)} %param.14), kind=kOutput, calls=%fused_computation.49 | convolution fusion | flops 2423521280 | bytes 14221312 | tf_op jit(solution)/shard_map/dot_general | solution.py:33
  149.7 0.9 fusion.18
  150.6 4.5 %all-to-all-start.1 = ((bf16[32,8,128]{2,1,0:T(8,128)(2,1)}), bf16[32,8,128]{2,1,0:T(8,128)(2,1)S(1)}, u32[]{:S(2)}, u32[]{:S(2)}) async-start(bf16[32,8,128]{2,1,0:T(8,128)(2,1)} %fusion.18), calls=%async_computation.1 | async-start | bytes 131072 | tf_op jit(solution)/shard_map/all_to_all | solution.py:118
  155.2 7.3 %all-to-all-done.1 = bf16[32,8,128]{2,1,0:T(8,128)(2,1)S(1)} async-done(((bf16[32,8,128]{2,1,0:T(8,128)(2,1)}), bf16[32,8,128]{2,1,0:T(8,128)(2,1)S(1)}, u32[]{:S(2)}, u32[]{:S(2)}) %all-to-all-start.1) | async-done | bytes 65568 | tf_op jit(solution)/shard_map/all_to_all | solution.py:118
  (54 shorter events, 10.0 us)
Async XLA Ops:
  0.0 9.9 %copy-start = (bf16[2048,128]{1,0:T(8,128)(2,1)S(1)}, bf16[2048,128]{1,0:T(8,128)(2,1)}, u32[]{:S(2)}) copy-start(bf16[2048,128]{1,0:T(8,128)(2,1)} %param.10) | copy-start | bytes 1572868
  0.0 19.6 %copy-start.3 = (f32[16,4096]{1,0:T(8,128)S(1)}, f32[16,4096]{1,0:T(8,128)}, u32[]{:S(2)}) copy-start(f32[16,4096]{1,0:T(8,128)} %param.17) | copy-start | bytes 786436
  0.0 67.0 %collective-permute-start = (bf16[128,4096]{1,0:T(8,128)(2,1)}, bf16[128,4096]{1,0:T(8,128)(2,1)}, u32[]{:S(2)}, u32[]{:S(2)}) collective-permute-start(bf16[128,4096]{1,0:T(8,128)(2,1)} %param.14), channel_id=1, source_target_pairs={{0,8},{8,0},{16,24},{24,16},{1,9},{9,1},{17,25},{25,17},{2,10},{10... | collective-permute-start | bytes 3145736 | tf_op jit(solution)/shard_map/ppermute | solution.py:63
  3.0 73.6 %collective-permute-start.2 = (bf16[128,4096]{1,0:T(8,128)(2,1)}, bf16[128,4096]{1,0:T(8,128)(2,1)}, u32[]{:S(2)}, u32[]{:S(2)}) collective-permute-start(bf16[128,4096]{1,0:T(8,128)(2,1)} %param.14), channel_id=1, source_target_pairs={{0,16},{8,24},{16,0},{24,8},{1,17},{9,25},{17,1},{25,9},{2,18},{10... | collective-permute-start | bytes 3145736 | tf_op jit(solution)/shard_map/ppermute | solution.py:63
  4.5 82.1 %collective-permute-start.4 = (bf16[128,4096]{1,0:T(8,128)(2,1)}, bf16[128,4096]{1,0:T(8,128)(2,1)}, u32[]{:S(2)}, u32[]{:S(2)}) collective-permute-start(bf16[128,4096]{1,0:T(8,128)(2,1)} %param.14), channel_id=1, source_target_pairs={{0,24},{8,16},{16,8},{24,0},{1,25},{9,17},{17,9},{25,1},{2,26},{10... | collective-permute-start | bytes 3145736 | tf_op jit(solution)/shard_map/ppermute | solution.py:63
  13.3 42.6 %all-to-all-start = ((bf16[32,32,129]{2,1,0:T(8,128)(2,1)}), bf16[32,32,129]{2,1,0:T(8,128)(2,1)S(1)}, u32[]{:S(2)}, u32[]{:S(2)}) async-start(bf16[32,32,129]{2,1,0:T(8,128)(2,1)} %bitcast.8), calls=%async_computation | async-start | bytes 1048576 | tf_op jit(solution)/shard_map/all_to_all | solution.py:89
  67.0 8.5 %copy-start.1 = (bf16[1024,128]{1,0:T(8,128)(2,1)S(1)}, bf16[1024,128]{1,0:T(8,128)(2,1)}, u32[]{:S(2)}) copy-start(bf16[1024,128]{1,0:T(8,128)(2,1)} %param.16) | copy-start | bytes 786436
  75.7 29.7 %collective-permute-start.1 = (f32[256,128]{1,0:T(8,128)S(1)}, f32[256,128]{1,0:T(8,128)S(1)}, u32[]{:S(2)}, u32[]{:S(2)}) collective-permute-start(f32[256,128]{1,0:T(8,128)S(1)} %fusion.54), channel_id=1, source_target_pairs={{0,8},{8,0},{16,24},{24,16},{1,9},{9,1},{17,25},{25,17},{2,10},{10... | collective-permute-start | bytes 393224 | tf_op jit(solution)/shard_map/ppermute | solution.py:103
  85.3 20.2 %collective-permute-start.3 = (f32[256,128]{1,0:T(8,128)S(1)}, f32[256,128]{1,0:T(8,128)S(1)}, u32[]{:S(2)}, u32[]{:S(2)}) collective-permute-start(f32[256,128]{1,0:T(8,128)S(1)} %fusion.55), channel_id=1, source_target_pairs={{0,16},{8,24},{16,0},{24,8},{1,17},{9,25},{17,1},{25,9},{2,18},{10... | collective-permute-start | bytes 393224 | tf_op jit(solution)/shard_map/ppermute | solution.py:103
  95.4 14.0 %copy-start.2 = (bf16[128,128]{1,0:T(8,128)(2,1)S(1)}, bf16[128,128]{1,0:T(8,128)(2,1)}, u32[]{:S(2)}) copy-start(bf16[128,128]{1,0:T(8,128)(2,1)} %param.18) | copy-start | bytes 98308
  95.4 10.1 %collective-permute-start.5 = (f32[256,128]{1,0:T(8,128)S(1)}, f32[256,128]{1,0:T(8,128)S(1)}, u32[]{:S(2)}, u32[]{:S(2)}) collective-permute-start(f32[256,128]{1,0:T(8,128)S(1)} %fusion.56), channel_id=1, source_target_pairs={{0,24},{8,16},{16,8},{24,0},{1,25},{9,17},{17,9},{25,1},{2,26},{10... | collective-permute-start | bytes 393224 | tf_op jit(solution)/shard_map/ppermute | solution.py:103
  105.8 4.9 %collective-permute-start.6 = (bf16[256,128]{1,0:T(8,128)(2,1)S(1)}, bf16[256,128]{1,0:T(8,128)(2,1)S(1)}, u32[]{:S(2)}, u32[]{:S(2)}) collective-permute-start(bf16[256,128]{1,0:T(8,128)(2,1)S(1)} %fusion.13), channel_id=1, source_target_pairs={{0,8},{8,0},{16,24},{24,16},{1,9},{9,1},{17,25},{25,17},{2,10},{10... | collective-permute-start | bytes 196616 | tf_op jit(solution)/shard_map/ppermute | solution.py:107
  106.7 13.7 %collective-permute-start.8 = (bf16[256,128]{1,0:T(8,128)(2,1)S(1)}, bf16[256,128]{1,0:T(8,128)(2,1)S(1)}, u32[]{:S(2)}, u32[]{:S(2)}) collective-permute-start(bf16[256,128]{1,0:T(8,128)(2,1)S(1)} %fusion.13), channel_id=1, source_target_pairs={{0,16},{8,24},{16,0},{24,8},{1,17},{9,25},{17,1},{25,9},{2,18},{10... | collective-permute-start | bytes 196616 | tf_op jit(solution)/shard_map/ppermute | solution.py:107
  107.9 22.4 %collective-permute-start.10 = (bf16[256,128]{1,0:T(8,128)(2,1)S(1)}, bf16[256,128]{1,0:T(8,128)(2,1)S(1)}, u32[]{:S(2)}, u32[]{:S(2)}) collective-permute-start(bf16[256,128]{1,0:T(8,128)(2,1)S(1)} %fusion.13), channel_id=1, source_target_pairs={{0,24},{8,16},{16,8},{24,0},{1,25},{9,17},{17,9},{25,1},{2,26},{10... | collective-permute-start | bytes 196616 | tf_op jit(solution)/shard_map/ppermute | solution.py:107
  119.6 30.1 %collective-permute-start.7 = (f32[256,128]{1,0:T(8,128)S(1)}, f32[256,128]{1,0:T(8,128)S(1)}, u32[]{:S(2)}, u32[]{:S(2)}) collective-permute-start(f32[256,128]{1,0:T(8,128)S(1)} %fusion.57), channel_id=1, source_target_pairs={{0,8},{8,0},{16,24},{24,16},{1,9},{9,1},{17,25},{25,17},{2,10},{10... | collective-permute-start | bytes 393224 | tf_op jit(solution)/shard_map/ppermute | solution.py:103
  129.2 20.5 %collective-permute-start.9 = (f32[256,128]{1,0:T(8,128)S(1)}, f32[256,128]{1,0:T(8,128)S(1)}, u32[]{:S(2)}, u32[]{:S(2)}) collective-permute-start(f32[256,128]{1,0:T(8,128)S(1)} %fusion.58), channel_id=1, source_target_pairs={{0,16},{8,24},{16,0},{24,8},{1,17},{9,25},{17,1},{25,9},{2,18},{10... | collective-permute-start | bytes 393224 | tf_op jit(solution)/shard_map/ppermute | solution.py:103
  139.4 15.8 %copy-start.4 = (s32[128,1]{0,1:T(1,128)S(1)}, s32[128,1]{0,1:T(1,128)}, u32[]{:S(2)}) copy-start(s32[128,1]{0,1:T(1,128)} %param.13) | copy-start | bytes 1540
  139.4 10.3 %collective-permute-start.11 = (f32[256,128]{1,0:T(8,128)S(1)}, f32[256,128]{1,0:T(8,128)S(1)}, u32[]{:S(2)}, u32[]{:S(2)}) collective-permute-start(f32[256,128]{1,0:T(8,128)S(1)} %fusion.59), channel_id=1, source_target_pairs={{0,24},{8,16},{16,8},{24,0},{1,25},{9,17},{17,9},{25,1},{2,26},{10... | collective-permute-start | bytes 393224 | tf_op jit(solution)/shard_map/ppermute | solution.py:103
  150.6 11.9 %all-to-all-start.1 = ((bf16[32,8,128]{2,1,0:T(8,128)(2,1)}), bf16[32,8,128]{2,1,0:T(8,128)(2,1)S(1)}, u32[]{:S(2)}, u32[]{:S(2)}) async-start(bf16[32,8,128]{2,1,0:T(8,128)(2,1)} %fusion.18), calls=%async_computation.1 | async-start | bytes 131072 | tf_op jit(solution)/shard_map/all_to_all | solution.py:118

commit v3 on v2

--- a/solution.py
+++ b/solution.py
@@ -96,7 +96,9 @@
     for segment_index in range(PASSES):
         partial = []
         for k in range(n_sec):
-            hidden = first_hidden(rows[k][None], block_first[k][None], got_band[k], parts)
+            hidden = lax.optimization_barrier(
+                first_hidden(rows[k][None], block_first[k][None], got_band[k], parts)
+            )
             partial.append(surrogate_tail(hidden, middle_weight, out_weight))
         own_sum = partial[0]
         for k in range(1, n_sec):

time: 164 us -> 186 us (1.13)
  matrix products: 82.3 us -> 103 us
    dot_general x8, matrix products: 3.11 us -> 53.3 us  [surrogate_tail(): return jnp.dot(middle, out_weight, preferred_element_type=jnp.float32)]
    dot_general x12 -> x8, matrix products: 68.2 us -> 40.5 us  [first_hidden(): jnp.einsum('srf,sfh->srh', rows, weights, preferred_element_type=jnp.floa...]
  transfers between devices with their start and end apart: 14 -> 14, of which waited for: 3 -> 3; matrix products, arithmetic and copies ran while one was open for 55% -> 53% of each run, Pallas kernels for 0% -> 0%
where the time goes in v3:
time: 186 us
  matrix products  103 us (55%)
  waiting for transfers between devices  44.9 us (24%)
  starting transfers between devices  26.3 us (14%)
  local copies, waits for them, and re-layouts  5.77 us (3%)
  other arithmetic  5.47 us (3%)
    dot_general x8, matrix products, surrogate_tail(): return jnp.dot(middle, out_weight, preferred_element_type=jnp.float32)  53.3 us
    dot_general x8, matrix products, first_hidden(): jnp.einsum('srf,sfh->srh', rows, weights, preferred_element_type=jnp.floa...  40.5 us
    all_to_all x1, waiting for transfers between devices, per_device(): lax.all_to_all(send, ('sec', 'dev'), split_axis=0, concat_axis=0, tiled=T...  36.2 us
    dot_general x4, matrix products, band_rows(): return jnp.dot(picks, parts, preferred_element_type=jnp.float32)  9.25 us
    ppermute x6, starting transfers between devices, per_device(): own_sum = own_sum + lax.ppermute(partial[k], 'sec', xor_pairs(n_sec, k))  7.37 us
    all_to_all x1, waiting for transfers between devices, per_device(): lax.all_to_all(own_values.reshape(count_all, slot_count, out_width), ('se...  7.35 us
    all_to_all x1, starting transfers between devices, per_device(): lax.all_to_all(send, ('sec', 'dev'), split_axis=0, concat_axis=0, tiled=T...  6.31 us
    all_to_all x1, starting transfers between devices, per_device(): lax.all_to_all(own_values.reshape(count_all, slot_count, out_width), ('se...  4.55 us
  transfers between devices with their start and end apart: 14, of which 3 were waited for; matrix products, arithmetic and copies ran while one was open for 53% of the time, Pallas kernels for 0%

profile of v3, /device:TPU:0, one launch (start us, length us, event | category | flops | bytes accessed | tf_op | source)
XLA Modules:
  0.0 185.9 jit_solution(9581777097781287646)
XLA Ops:
  0.0 3.0 %collective-permute-start = (bf16[128,4096]{1,0:T(8,128)(2,1)}, bf16[128,4096]{1,0:T(8,128)(2,1)}, u32[]{:S(2)}, u32[]{:S(2)}) collective-permute-start(bf16[128,4096]{1,0:T(8,128)(2,1)} %param.14), channel_id=1, source_target_pairs={{0,8},{8,0},{16,24},{24,16},{1,9},{9,1},{17,25},{25,17},{2,10},{10... | collective-permute-start | bytes 3145736 | tf_op jit(solution)/shard_map/ppermute | solution.py:63
  3.0 1.5 collective-permute-start.2
  7.6 1.6 gather_fusion.1
  13.3 6.3 %all-to-all-start = ((bf16[32,32,129]{2,1,0:T(8,128)(2,1)}), bf16[32,32,129]{2,1,0:T(8,128)(2,1)S(1)}, u32[]{:S(2)}, u32[]{:S(2)}) async-start(bf16[32,32,129]{2,1,0:T(8,128)(2,1)} %bitcast.8), calls=%async_computation | async-start | bytes 1048576 | tf_op jit(solution)/shard_map/all_to_all | solution.py:89
  19.7 36.2 %all-to-all-done = bf16[32,32,129]{2,1,0:T(8,128)(2,1)S(1)} async-done(((bf16[32,32,129]{2,1,0:T(8,128)(2,1)}), bf16[32,32,129]{2,1,0:T(8,128)(2,1)S(1)}, u32[]{:S(2)}, u32[]{:S(2)}) %all-to-all-start) | async-done | bytes 264224 | tf_op jit(solution)/shard_map/all_to_all | solution.py:89
  56.9 3.1 %fusion.24 = f32[256,4096]{1,0:T(8,128)} fusion(s32[48]{0:T(128)S(1)} %and_select_fusion, s32[256]{0:T(256)S(1)} %get-tuple-element.7, bf16[16,4096]{1,0:T(8,128)(2,1)S(1)} %get-tuple-element.14, bf16[16,4096]{1,0:T(8,128)(2,1)S(1)} %get-tuple-element.15, bf16[16,4096]{1,0:T(8,128)(2,1)S(1)} %get-tuple-element.13), kind=kOutput, calls=%fused_computation.68 | convolution fusion | flops 101855232 | bytes 4588736 | tf_op jit(solution)/shard_map/dot_general | solution.py:22
  60.0 2.7 %fusion.22 = f32[256,4096]{1,0:T(8,128)} fusion(s32[48]{0:T(128)S(1)} %and_select_fusion, s32[256]{0:T(256)S(1)} %get-tuple-element.6, bf16[16,4096]{1,0:T(8,128)(2,1)S(1)} %get-tuple-element.14, bf16[16,4096]{1,0:T(8,128)(2,1)S(1)} %get-tuple-element.15, bf16[16,4096]{1,0:T(8,128)(2,1)S(1)} %get-tuple-element.13), kind=kOutput, calls=%fused_computation.66 | convolution fusion | flops 101855232 | bytes 4588736 | tf_op jit(solution)/shard_map/dot_general | solution.py:22
  62.7 2.7 %fusion.28 = f32[256,4096]{1,0:T(8,128)} fusion(s32[48]{0:T(128)S(1)} %and_select_fusion, s32[256]{0:T(256)S(1)} %get-tuple-element.5, bf16[16,4096]{1,0:T(8,128)(2,1)S(1)} %get-tuple-element.14, bf16[16,4096]{1,0:T(8,128)(2,1)S(1)} %get-tuple-element.15, bf16[16,4096]{1,0:T(8,128)(2,1)S(1)} %get-tuple-element.13), kind=kOutput, calls=%fused_computation.72 | convolution fusion | flops 101855232 | bytes 4588736 | tf_op jit(solution)/shard_map/dot_general | solution.py:22
  65.4 4.0 %multiply_convert_fusion.6 = bf16[256,4096]{1,0:T(8,128)(2,1)} fusion(f32[256,4096]{1,0:T(8,128)S(1)} %fusion.26, bf16[128,4096]{1,0:T(8,128)(2,1)} %collective-permute-done, bf16[4,256,129]{2,1,0:T(8,128)(2,1)S(1)} %copy_bitcast_fusion), kind=kOutput, calls=%fused_computation.18 | convolution fusion | flops 274726912 | bytes 7405568 | tf_op jit(solution)/shard_map/srf,sfh->srh/dot_general | solution.py:26
  69.5 6.5 %fusion.11 = f32[256,128]{1,0:T(8,128)S(1)} fusion(bf16[1024,128]{1,0:T(8,128)(2,1)S(1)} %copy-done.6, bf16[256,4096]{1,0:T(8,128)(2,1)} %multiply_convert_fusion.6, bf16[4096,1024]{1,0:T(8,128)(2,1)} %param.15), kind=kOutput, calls=%fused_computation.47 | convolution fusion | flops 2215903232 | bytes 10878976 | tf_op jit(solution)/shard_map/dot_general | solution.py:35
  76.9 5.2 %multiply_convert_fusion.5 = bf16[256,4096]{1,0:T(8,128)(2,1)} fusion(f32[256,4096]{1,0:T(8,128)} %fusion.24, bf16[128,4096]{1,0:T(8,128)(2,1)} %collective-permute-done.2, bf16[4,256,129]{2,1,0:T(8,128)(2,1)S(1)} %copy_bitcast_fusion), kind=kOutput, calls=%fused_computation.17 | convolution fusion | flops 274726912 | bytes 7405568 | tf_op jit(solution)/shard_map/srf,sfh->srh/dot_general | solution.py:26
  82.2 6.5 %fusion.12 = f32[256,128]{1,0:T(8,128)S(1)} fusion(bf16[1024,128]{1,0:T(8,128)(2,1)S(1)} %copy-done.6, bf16[256,4096]{1,0:T(8,128)(2,1)} %multiply_convert_fusion.5, bf16[4096,1024]{1,0:T(8,128)(2,1)} %param.15), kind=kOutput, calls=%fused_computation.48 | convolution fusion | flops 2215903232 | bytes 10878976 | tf_op jit(solution)/shard_map/dot_general | solution.py:35
  88.7 1.3 collective-permute-start.3
  91.0 4.9 %multiply_convert_fusion.4 = bf16[256,4096]{1,0:T(8,128)(2,1)} fusion(f32[256,4096]{1,0:T(8,128)} %fusion.22, bf16[128,4096]{1,0:T(8,128)(2,1)S(1)} %collective-permute-done.4, bf16[4,256,129]{2,1,0:T(8,128)(2,1)S(1)} %copy_bitcast_fusion), kind=kOutput, calls=%fused_computation.16 | convolution fusion | flops 274726912 | bytes 7405568 | tf_op jit(solution)/shard_map/srf,sfh->srh/dot_general | solution.py:26
  95.9 6.8 %fusion.13 = f32[256,128]{1,0:T(8,128)S(1)} fusion(bf16[1024,128]{1,0:T(8,128)(2,1)S(1)} %copy-done.6, bf16[256,4096]{1,0:T(8,128)(2,1)} %multiply_convert_fusion.4, bf16[4096,1024]{1,0:T(8,128)(2,1)} %param.15), kind=kOutput, calls=%fused_computation.49 | convolution fusion | flops 2215903232 | bytes 10878976 | tf_op jit(solution)/shard_map/dot_general | solution.py:35
  102.7 1.5 collective-permute-start.5
  104.2 4.9 %multiply_convert_fusion.7 = bf16[256,4096]{1,0:T(8,128)(2,1)} fusion(f32[256,4096]{1,0:T(8,128)} %fusion.28, bf16[128,4096]{1,0:T(8,128)(2,1)S(1)} %copy-done.4, bf16[4,256,129]{2,1,0:T(8,128)(2,1)S(1)} %copy_bitcast_fusion), kind=kOutput, calls=%fused_computation.19 | convolution fusion | flops 274726912 | bytes 7405568 | tf_op jit(solution)/shard_map/srf,sfh->srh/dot_general | solution.py:26
  109.2 6.6 %fusion.5 = bf16[256,128]{1,0:T(8,128)(2,1)S(1)} fusion(f32[256,128]{1,0:T(8,128)S(1)} %collective-permute-done.5, f32[256,128]{1,0:T(8,128)S(1)} %collective-permute-done.3, f32[256,128]{1,0:T(8,128)S(1)} %collective-permute-done.1, bf16[1024,128]{1,0:T(8,128)(2,1)S(1)} %copy-done.6, bf16[256,4096]{1,0:T(8,128)(2,1)} %multiply_convert_fusion.7, ...), kind=kOutput, calls=%fused_computation.32 | convolution fusion | flops 2216034304 | bytes 11206656 | tf_op jit(solution)/shard_map/dot_general | solution.py:35
  116.8 1.1 collective-permute-start.8
  117.9 1.4 collective-permute-start.10
  119.3 1.4 collective-permute-done.6
  120.7 5.4 %multiply_convert_fusion.2 = bf16[256,4096]{1,0:T(8,128)(2,1)} fusion(f32[256,4096]{1,0:T(8,128)} %copy-done.1, bf16[128,4096]{1,0:T(8,128)(2,1)} %collective-permute-done, bf16[256,128]{1,0:T(8,128)(2,1)S(1)} %collective-permute-done.6, bf16[128,128]{1,0:T(8,128)(2,1)S(1)} %copy-done.7, bf16[4,256,129]{2,1,0:T(8,128)(2,1)S(1)} %copy_bitcast_fusion), kind=kOutput, calls=%fused_computation.14 | convolution fusion | flops 283213824 | bytes 7503872 | tf_op jit(solution)/shard_map/srf,sfh->srh/dot_general | solution.py:26
  126.0 6.5 %fusion.14 = f32[256,128]{1,0:T(8,128)S(1)} fusion(bf16[1024,128]{1,0:T(8,128)(2,1)S(1)} %copy-done.6, bf16[256,4096]{1,0:T(8,128)(2,1)} %multiply_convert_fusion.2, bf16[4096,1024]{1,0:T(8,128)(2,1)} %param.15), kind=kOutput, calls=%fused_computation.50 | convolution fusion | flops 2215903232 | bytes 10878976 | tf_op jit(solution)/shard_map/dot_general | solution.py:35
  133.7 5.3 %multiply_convert_fusion.1 = bf16[256,4096]{1,0:T(8,128)(2,1)} fusion(f32[256,4096]{1,0:T(8,128)} %fusion.24, bf16[128,4096]{1,0:T(8,128)(2,1)} %collective-permute-done.2, bf16[256,128]{1,0:T(8,128)(2,1)S(1)} %collective-permute-done.8, bf16[128,128]{1,0:T(8,128)(2,1)S(1)} %copy-done.7, bf16[4,256,129]{2,1,0:T(8,128)(2,1)S(1)} %copy_bitcast_fusion), kind=kOutput, calls=%fused_computation.13 | convolution fusion | flops 283213824 | bytes 7503872 | tf_op jit(solution)/shard_map/srf,sfh->srh/dot_general | solution.py:26
  139.0 6.5 %fusion.15 = f32[256,128]{1,0:T(8,128)S(1)} fusion(bf16[1024,128]{1,0:T(8,128)(2,1)S(1)} %copy-done.6, bf16[256,4096]{1,0:T(8,128)(2,1)} %multiply_convert_fusion.1, bf16[4096,1024]{1,0:T(8,128)(2,1)} %param.15), kind=kOutput, calls=%fused_computation.51 | convolution fusion | flops 2215903232 | bytes 10878976 | tf_op jit(solution)/shard_map/dot_general | solution.py:35
  146.3 5.6 %multiply_convert_fusion = bf16[256,4096]{1,0:T(8,128)(2,1)} fusion(f32[256,4096]{1,0:T(8,128)} %fusion.22, bf16[128,4096]{1,0:T(8,128)(2,1)} %copy-done.5, bf16[256,128]{1,0:T(8,128)(2,1)S(1)} %collective-permute-done.10, bf16[128,128]{1,0:T(8,128)(2,1)S(1)} %copy-done.7, bf16[4,256,129]{2,1,0:T(8,128)(2,1)S(1)} %copy_bitcast_fusion), kind=kOutput, calls=%fused_computation.12 | convolution fusion | flops 283213824 | bytes 7503872 | tf_op jit(solution)/shard_map/srf,sfh->srh/dot_general | solution.py:26
  151.9 6.5 %fusion.16 = f32[256,128]{1,0:T(8,128)S(1)} fusion(bf16[1024,128]{1,0:T(8,128)(2,1)S(1)} %copy-done.6, bf16[256,4096]{1,0:T(8,128)(2,1)} %multiply_convert_fusion, bf16[4096,1024]{1,0:T(8,128)(2,1)} %param.15), kind=kOutput, calls=%fused_computation.52 | convolution fusion | flops 2215903232 | bytes 10878976 | tf_op jit(solution)/shard_map/dot_general | solution.py:35
  158.5 1.8 collective-permute-start.11
  160.3 5.0 %multiply_convert_fusion.3 = bf16[256,4096]{1,0:T(8,128)(2,1)} fusion(f32[256,4096]{1,0:T(8,128)} %fusion.28, bf16[128,4096]{1,0:T(8,128)(2,1)S(1)} %copy-done.4, bf16[256,128]{1,0:T(8,128)(2,1)S(1)} %fusion.5, bf16[128,128]{1,0:T(8,128)(2,1)S(1)} %copy-done.7, bf16[4,256,129]{2,1,0:T(8,128)(2,1)S(1)} %copy_bitcast_fusion), kind=kOutput, calls=%fused_computation.15 | convolution fusion | flops 283213824 | bytes 7503872 | tf_op jit(solution)/shard_map/srf,sfh->srh/dot_general | solution.py:26
  165.4 7.2 %fusion.10 = bf16[32,8,128]{2,1,0:T(8,128)(2,1)} fusion(f32[256,128]{1,0:T(8,128)S(1)} %collective-permute-done.11, f32[256,128]{1,0:T(8,128)S(1)} %collective-permute-done.9, f32[256,128]{1,0:T(8,128)S(1)} %collective-permute-done.7, bf16[1024,128]{1,0:T(8,128)(2,1)S(1)} %copy-done.6, bf16[256,4096]{1,0:T(8,128)(2,1)} %multiply_convert_fusion.3, ...), kind=kOutput, calls=%fused_computation.37 | convolution fusion | flops 2216034304 | bytes 11206656 | tf_op jit(solution)/shard_map/dot_general | solution.py:35
  172.6 4.6 %all-to-all-start.1 = ((bf16[32,8,128]{2,1,0:T(8,128)(2,1)}), bf16[32,8,128]{2,1,0:T(8,128)(2,1)S(1)}, u32[]{:S(2)}, u32[]{:S(2)}) async-start(bf16[32,8,128]{2,1,0:T(8,128)(2,1)} %fusion.10), calls=%async_computation.1 | async-start | bytes 131072 | tf_op jit(solution)/shard_map/all_to_all | solution.py:120
  177.2 7.3 %all-to-all-done.1 = bf16[32,8,128]{2,1,0:T(8,128)(2,1)S(1)} async-done(((bf16[32,8,128]{2,1,0:T(8,128)(2,1)}), bf16[32,8,128]{2,1,0:T(8,128)(2,1)S(1)}, u32[]{:S(2)}, u32[]{:S(2)}) %all-to-all-start.1) | async-done | bytes 65568 | tf_op jit(solution)/shard_map/all_to_all | solution.py:120
  (56 shorter events, 14.4 us)
Async XLA Ops:
  0.0 9.9 %copy-start = (bf16[2048,128]{1,0:T(8,128)(2,1)S(1)}, bf16[2048,128]{1,0:T(8,128)(2,1)}, u32[]{:S(2)}) copy-start(bf16[2048,128]{1,0:T(8,128)(2,1)} %param.10) | copy-start | bytes 1572868
  0.0 19.6 %copy-start.2 = (f32[16,4096]{1,0:T(8,128)S(1)}, f32[16,4096]{1,0:T(8,128)}, u32[]{:S(2)}) copy-start(f32[16,4096]{1,0:T(8,128)} %param.17) | copy-start | bytes 786436
  0.0 65.4 %collective-permute-start = (bf16[128,4096]{1,0:T(8,128)(2,1)}, bf16[128,4096]{1,0:T(8,128)(2,1)}, u32[]{:S(2)}, u32[]{:S(2)}) collective-permute-start(bf16[128,4096]{1,0:T(8,128)(2,1)} %param.14), channel_id=1, source_target_pairs={{0,8},{8,0},{16,24},{24,16},{1,9},{9,1},{17,25},{25,17},{2,10},{10... | collective-permute-start | bytes 3145736 | tf_op jit(solution)/shard_map/ppermute | solution.py:63
  3.0 74.0 %collective-permute-start.2 = (bf16[128,4096]{1,0:T(8,128)(2,1)}, bf16[128,4096]{1,0:T(8,128)(2,1)}, u32[]{:S(2)}, u32[]{:S(2)}) collective-permute-start(bf16[128,4096]{1,0:T(8,128)(2,1)} %param.14), channel_id=1, source_target_pairs={{0,16},{8,24},{16,0},{24,8},{1,17},{9,25},{17,1},{25,9},{2,18},{10... | collective-permute-start | bytes 3145736 | tf_op jit(solution)/shard_map/ppermute | solution.py:63
  4.5 85.5 %collective-permute-start.4 = (bf16[128,4096]{1,0:T(8,128)(2,1)}, bf16[128,4096]{1,0:T(8,128)(2,1)S(1)}, u32[]{:S(2)}, u32[]{:S(2)}) collective-permute-start(bf16[128,4096]{1,0:T(8,128)(2,1)} %param.14), channel_id=1, source_target_pairs={{0,24},{8,16},{16,8},{24,0},{1,25},{9,17},{17,9},{25,1},{2,26},{10... | collective-permute-start | bytes 3145736 | tf_op jit(solution)/shard_map/ppermute | solution.py:63
  13.3 42.6 %all-to-all-start = ((bf16[32,32,129]{2,1,0:T(8,128)(2,1)}), bf16[32,32,129]{2,1,0:T(8,128)(2,1)S(1)}, u32[]{:S(2)}, u32[]{:S(2)}) async-start(bf16[32,32,129]{2,1,0:T(8,128)(2,1)} %bitcast.8), calls=%async_computation | async-start | bytes 1048576 | tf_op jit(solution)/shard_map/all_to_all | solution.py:89
  56.9 8.5 %copy-start.1 = (f32[256,4096]{1,0:T(8,128)}, f32[256,4096]{1,0:T(8,128)S(1)}, u32[]{:S(2)}) copy-start(f32[256,4096]{1,0:T(8,128)S(1)} %fusion.26) | copy-start | bytes 12582916
  65.4 4.1 %copy-start.6 = (bf16[1024,128]{1,0:T(8,128)(2,1)S(1)}, bf16[1024,128]{1,0:T(8,128)(2,1)}, u32[]{:S(2)}) copy-start(bf16[1024,128]{1,0:T(8,128)(2,1)} %param.16) | copy-start | bytes 786436
  76.0 33.1 %collective-permute-start.1 = (f32[256,128]{1,0:T(8,128)S(1)}, f32[256,128]{1,0:T(8,128)S(1)}, u32[]{:S(2)}, u32[]{:S(2)}) collective-permute-start(f32[256,128]{1,0:T(8,128)S(1)} %fusion.11), channel_id=1, source_target_pairs={{0,8},{8,0},{16,24},{24,16},{1,9},{9,1},{17,25},{25,17},{2,10},{10... | collective-permute-start | bytes 393224 | tf_op jit(solution)/shard_map/ppermute | solution.py:105
  88.7 20.4 %collective-permute-start.3 = (f32[256,128]{1,0:T(8,128)S(1)}, f32[256,128]{1,0:T(8,128)S(1)}, u32[]{:S(2)}, u32[]{:S(2)}) collective-permute-start(f32[256,128]{1,0:T(8,128)S(1)} %fusion.12), channel_id=1, source_target_pairs={{0,16},{8,24},{16,0},{24,8},{1,17},{9,25},{17,1},{25,9},{2,18},{10... | collective-permute-start | bytes 393224 | tf_op jit(solution)/shard_map/ppermute | solution.py:105
  90.0 1.0 copy-start.5
  95.9 8.3 %copy-start.4 = (bf16[128,4096]{1,0:T(8,128)(2,1)S(1)}, bf16[128,4096]{1,0:T(8,128)(2,1)}, u32[]{:S(2)}) copy-start(bf16[128,4096]{1,0:T(8,128)(2,1)} %param.14) | copy-start | bytes 3145732
  102.7 6.4 %collective-permute-start.5 = (f32[256,128]{1,0:T(8,128)S(1)}, f32[256,128]{1,0:T(8,128)S(1)}, u32[]{:S(2)}, u32[]{:S(2)}) collective-permute-start(f32[256,128]{1,0:T(8,128)S(1)} %fusion.13), channel_id=1, source_target_pairs={{0,24},{8,16},{16,8},{24,0},{1,25},{9,17},{17,9},{25,1},{2,26},{10... | collective-permute-start | bytes 393224 | tf_op jit(solution)/shard_map/ppermute | solution.py:105
  109.2 11.5 %copy-start.7 = (bf16[128,128]{1,0:T(8,128)(2,1)S(1)}, bf16[128,128]{1,0:T(8,128)(2,1)}, u32[]{:S(2)}) copy-start(bf16[128,128]{1,0:T(8,128)(2,1)} %param.18) | copy-start | bytes 98308
  115.7 4.9 %collective-permute-start.6 = (bf16[256,128]{1,0:T(8,128)(2,1)S(1)}, bf16[256,128]{1,0:T(8,128)(2,1)S(1)}, u32[]{:S(2)}, u32[]{:S(2)}) collective-permute-start(bf16[256,128]{1,0:T(8,128)(2,1)S(1)} %fusion.5), channel_id=1, source_target_pairs={{0,8},{8,0},{16,24},{24,16},{1,9},{9,1},{17,25},{25,17},{2,10},{10... | collective-permute-start | bytes 196616 | tf_op jit(solution)/shard_map/ppermute | solution.py:109
  116.8 16.9 %collective-permute-start.8 = (bf16[256,128]{1,0:T(8,128)(2,1)S(1)}, bf16[256,128]{1,0:T(8,128)(2,1)S(1)}, u32[]{:S(2)}, u32[]{:S(2)}) collective-permute-start(bf16[256,128]{1,0:T(8,128)(2,1)S(1)} %fusion.5), channel_id=1, source_target_pairs={{0,16},{8,24},{16,0},{24,8},{1,17},{9,25},{17,1},{25,9},{2,18},{10... | collective-permute-start | bytes 196616 | tf_op jit(solution)/shard_map/ppermute | solution.py:109
  117.9 28.5 %collective-permute-start.10 = (bf16[256,128]{1,0:T(8,128)(2,1)S(1)}, bf16[256,128]{1,0:T(8,128)(2,1)S(1)}, u32[]{:S(2)}, u32[]{:S(2)}) collective-permute-start(bf16[256,128]{1,0:T(8,128)(2,1)S(1)} %fusion.5), channel_id=1, source_target_pairs={{0,24},{8,16},{16,8},{24,0},{1,25},{9,17},{17,9},{25,1},{2,26},{10... | collective-permute-start | bytes 196616 | tf_op jit(solution)/shard_map/ppermute | solution.py:109
  132.6 32.8 %collective-permute-start.7 = (f32[256,128]{1,0:T(8,128)S(1)}, f32[256,128]{1,0:T(8,128)S(1)}, u32[]{:S(2)}, u32[]{:S(2)}) collective-permute-start(f32[256,128]{1,0:T(8,128)S(1)} %fusion.14), channel_id=1, source_target_pairs={{0,8},{8,0},{16,24},{24,16},{1,9},{9,1},{17,25},{25,17},{2,10},{10... | collective-permute-start | bytes 393224 | tf_op jit(solution)/shard_map/ppermute | solution.py:105
  145.6 19.8 %collective-permute-start.9 = (f32[256,128]{1,0:T(8,128)S(1)}, f32[256,128]{1,0:T(8,128)S(1)}, u32[]{:S(2)}, u32[]{:S(2)}) collective-permute-start(f32[256,128]{1,0:T(8,128)S(1)} %fusion.15), channel_id=1, source_target_pairs={{0,16},{8,24},{16,0},{24,8},{1,17},{9,25},{17,1},{25,9},{2,18},{10... | collective-permute-start | bytes 393224 | tf_op jit(solution)/shard_map/ppermute | solution.py:105
  158.5 6.9 %collective-permute-start.11 = (f32[256,128]{1,0:T(8,128)S(1)}, f32[256,128]{1,0:T(8,128)S(1)}, u32[]{:S(2)}, u32[]{:S(2)}) collective-permute-start(f32[256,128]{1,0:T(8,128)S(1)} %fusion.16), channel_id=1, source_target_pairs={{0,24},{8,16},{16,8},{24,0},{1,25},{9,17},{17,9},{25,1},{2,26},{10... | collective-permute-start | bytes 393224 | tf_op jit(solution)/shard_map/ppermute | solution.py:105
  165.4 11.8 %copy-start.3 = (s32[128,1]{0,1:T(1,128)S(1)}, s32[128,1]{0,1:T(1,128)}, u32[]{:S(2)}) copy-start(s32[128,1]{0,1:T(1,128)} %param.13) | copy-start | bytes 1540
  172.6 11.9 %all-to-all-start.1 = ((bf16[32,8,128]{2,1,0:T(8,128)(2,1)}), bf16[32,8,128]{2,1,0:T(8,128)(2,1)S(1)}, u32[]{:S(2)}, u32[]{:S(2)}) async-start(bf16[32,8,128]{2,1,0:T(8,128)(2,1)} %fusion.10), calls=%async_computation.1 | async-start | bytes 131072 | tf_op jit(solution)/shard_map/all_to_all | solution.py:120

commit v4 on v2

--- a/solution.py
+++ b/solution.py
@@ -89,30 +89,29 @@
     got = lax.all_to_all(send, ("sec", "dev"), split_axis=0, concat_axis=0, tiled=True)
     got = got.reshape(count_all, n_sec, slot_count, feat_width + 1).transpose(1, 0, 2, 3)
     got = got.reshape(n_sec, count_all * slot_count, feat_width + 1)
-    rows = [got[k, :, :feat_width] for k in range(n_sec)]
-    got_band = [got[k, :, feat_width].astype(jnp.int32) for k in range(n_sec)]
+    rows = got[:, :, :feat_width]
+    got_band = got[:, :, feat_width].astype(jnp.int32).reshape(-1)
+    every_first = jnp.stack(block_first)
 
     result = None
     for segment_index in range(PASSES):
-        partial = []
-        for k in range(n_sec):
-            hidden = first_hidden(rows[k][None], block_first[k][None], got_band[k], parts)
-            partial.append(surrogate_tail(hidden, middle_weight, out_weight))
+        hidden = first_hidden(rows, every_first, got_band, parts)
+        partial = surrogate_tail(hidden, middle_weight, out_weight).reshape(
+            n_sec, rows.shape[1], -1
+        )
         own_sum = partial[0]
         for k in range(1, n_sec):
             own_sum = own_sum + lax.ppermute(partial[k], "sec", xor_pairs(n_sec, k))
         own_values = own_sum.astype(jnp.bfloat16)
         if segment_index + 1 < PASSES:
-            values = [own_values] + [
-                lax.ppermute(own_values, "sec", xor_pairs(n_sec, k)) for k in range(1, n_sec)
-            ]
-            rows = [
-                (
-                    rows[k].astype(jnp.float32)
-                    + jnp.dot(values[k], back_weight, preferred_element_type=jnp.float32)
-                ).astype(jnp.bfloat16)
-                for k in range(n_sec)
-            ]
+            values = jnp.stack(
+                [own_values]
+                + [lax.ppermute(own_values, "sec", xor_pairs(n_sec, k)) for k in range(1, n_sec)]
+            )
+            rows = (
+                rows.astype(jnp.float32)
+                + jnp.einsum("sro,of->srf", values, back_weight, preferred_element_type=jnp.float32)
+            ).astype(jnp.bfloat16)
         else:
             out_width = own_values.shape[1]
             back = lax.all_to_all(

time: 164 us -> 162 us (0.988)
  matrix products: 82.3 us -> 52 us
  other arithmetic: 5.47 us -> 22.1 us
  waiting for transfers between devices: 44.8 us -> 56.4 us
    dot_general x12 -> x2, matrix products: 68.2 us -> 12.5 us  [first_hidden(): jnp.einsum('srf,sfh->srh', rows, weights, preferred_element_type=jnp.floa...]
    dot_general x8 -> x2, matrix products: 3.11 us -> 29.2 us  [surrogate_tail(): return jnp.dot(middle, out_weight, preferred_element_type=jnp.float32)]
    convert_element_type x1 -> x3, other arithmetic: 0.22 us -> 15.1 us  [the longest x1 14.9 us: first_hidden(): return jax.nn.silu(mixed).astype(jnp.bfloat16)]
    ppermute x6, waiting for transfers between devices: 0.02 us -> 9.79 us  [per_device(): own_sum = own_sum + lax.ppermute(partial[k], 'sec', xor_pairs(n_sec, k))]
    ppermute x3, waiting for transfers between devices: 1.2 us -> 4.04 us  [per_device(): lax.ppermute(own_values, 'sec', xor_pairs(n_sec, k))]
    dot_general x4 -> x1, matrix products: 10.8 us -> 10.1 us  [band_rows(): return jnp.dot(picks, parts, preferred_element_type=jnp.float32)]
  transfers between devices with their start and end apart: 14 -> 14, of which waited for: 3 -> 11; matrix products, arithmetic and copies ran while one was open for 55% -> 6% of each run, Pallas kernels for 0% -> 0%
where the time goes in v4:
time: 162 us
  waiting for transfers between devices  56.4 us (35%)
  matrix products  52 us (32%)
  starting transfers between devices  26 us (16%)
  other arithmetic  22.1 us (14%)
  local copies, waits for them, and re-layouts  4.87 us (3%)
    all_to_all x1, waiting for transfers between devices, per_device(): lax.all_to_all(send, ('sec', 'dev'), split_axis=0, concat_axis=0, tiled=T...  35.2 us
    dot_general x2, matrix products, surrogate_tail(): return jnp.dot(middle, out_weight, preferred_element_type=jnp.float32)  29.2 us
    convert_element_type x1, other arithmetic, first_hidden(): return jax.nn.silu(mixed).astype(jnp.bfloat16)  14.9 us
    dot_general x2, matrix products, first_hidden(): jnp.einsum('srf,sfh->srh', rows, weights, preferred_element_type=jnp.floa...  12.5 us
    dot_general x1, matrix products, band_rows(): return jnp.dot(picks, parts, preferred_element_type=jnp.float32)  10.1 us
    ppermute x6, waiting for transfers between devices, per_device(): own_sum = own_sum + lax.ppermute(partial[k], 'sec', xor_pairs(n_sec, k))  9.79 us
    all_to_all x1, waiting for transfers between devices, per_device(): lax.all_to_all(own_values.reshape(count_all, slot_count, out_width), ('se...  7.35 us
    ppermute x6, starting transfers between devices, per_device(): own_sum = own_sum + lax.ppermute(partial[k], 'sec', xor_pairs(n_sec, k))  7.11 us
  transfers between devices with their start and end apart: 14, of which 11 were waited for; matrix products, arithmetic and copies ran while one was open for 6% of the time, Pallas kernels for 0%

profile of v4, /device:TPU:0, one launch (start us, length us, event | category | flops | bytes accessed | tf_op | source)
XLA Modules:
  0.0 161.6 jit_solution(9070494213283435634)
XLA Ops:
  0.0 3.0 %collective-permute-start = (bf16[128,4096]{1,0:T(8,128)(2,1)}, bf16[128,4096]{1,0:T(8,128)(2,1)S(1)}, u32[]{:S(2)}, u32[]{:S(2)}) collective-permute-start(bf16[128,4096]{1,0:T(8,128)(2,1)} %param.14), channel_id=1, source_target_pairs={{0,8},{8,0},{16,24},{24,16},{1,9},{9,1},{17,25},{25,17},{2,10},{10... | collective-permute-start | bytes 3145736 | tf_op jit(solution)/shard_map/ppermute | solution.py:63
  3.0 1.5 collective-permute-start.1
  7.6 1.6 %gather_fusion.1 = s32[128]{0:T(128)S(1)} fusion(s32[2048]{0:T(1024)} %param.11, s32[1024]{0:T(1024)S(1)} %pad_clamp_fusion.2), kind=kCustom, calls=%fused_computation.1 | custom fusion | bytes 1536 | tf_op jit(solution)/shard_map/jit(_take)/gather | solution.py:68
  12.4 0.9 copy.14
  13.3 6.3 %all-to-all-start = ((bf16[32,32,129]{2,1,0:T(8,128)(2,1)}), bf16[32,32,129]{2,1,0:T(8,128)(2,1)S(1)}, u32[]{:S(2)}, u32[]{:S(2)}) async-start(bf16[32,32,129]{2,1,0:T(8,128)(2,1)} %bitcast.8), calls=%async_computation | async-start | bytes 1048576 | tf_op jit(solution)/shard_map/all_to_all | solution.py:89
  19.6 1.1 fusion.58
  20.7 35.2 %all-to-all-done = bf16[32,32,129]{2,1,0:T(8,128)(2,1)S(1)} async-done(((bf16[32,32,129]{2,1,0:T(8,128)(2,1)}), bf16[32,32,129]{2,1,0:T(8,128)(2,1)S(1)}, u32[]{:S(2)}, u32[]{:S(2)}) %all-to-all-start) | async-done | bytes 264224 | tf_op jit(solution)/shard_map/all_to_all | solution.py:89
  56.2 4.1 %fusion.4 = f32[4,256,4096]{2,1,0:T(8,128)S(1)} fusion(bf16[1,128,4096]{2,1,0:T(8,128)(2,1)} %bitcast.15, bf16[1,128,4096]{2,1,0:T(8,128)(2,1)S(1)} %bitcast.61, bf16[1,128,4096]{2,1,0:T(8,128)(2,1)S(1)} %bitcast.59, bf16[1,128,4096]{2,1,0:T(8,128)(2,1)} %bitcast.57, bf16[4,256,129]{2,1,0:T(8,128)(2,1)S(1)} %copy_bitcast_fusion), kind=kOutput, calls=%fused_computation.17 | convolution fusion | flops 1080033280 | bytes 21233664 | tf_op jit(solution)/shard_map/srf,sfh->srh/dot_general | solution.py:26
  60.3 10.1 %multiply_convert_fusion.1 = (bf16[1024,4096]{1,0:T(8,128)(2,1)}, f32[1024,4096]{1,0:T(8,128)}) fusion(f32[4,256,4096]{2,1,0:T(8,128)S(1)} %fusion.4, bf16[16,4096]{1,0:T(8,128)(2,1)S(1)} %get-tuple-element.16, bf16[16,4096]{1,0:T(8,128)(2,1)S(1)} %get-tuple-element.17, bf16[16,4096]{1,0:T(8,128)(2,1)S(1)} %get-tuple-element.15, s32[48]{0:T(128)S(1)} %and_select_fusion, ...), kind=kOutput, calls=%fused_computation.7 | convolution fusion | flops 429047808 | bytes 42340544 | tf_op jit(solution)/shard_map/dot_general | solution.py:22
  70.4 14.6 %fusion = f32[1024,128]{1,0:T(8,128)S(1)} fusion(bf16[1024,128]{1,0:T(8,128)(2,1)} %param.16, bf16[1024,4096]{1,0:T(8,128)(2,1)} %get-tuple-element.18, bf16[4096,1024]{1,0:T(8,128)(2,1)} %param.15), kind=kOutput, calls=%fused_computation.11 | convolution fusion | flops 8863612928 | bytes 17563648 | tf_op jit(solution)/shard_map/dot_general | solution.py:35
  85.0 0.9 collective-permute-start.3
  85.9 1.2 collective-permute-start.4
  87.1 1.4 collective-permute-start.5
  88.6 2.6 %collective-permute-done.3 = f32[256,128]{1,0:T(8,128)S(1)} collective-permute-done((f32[256,128]{1,0:T(8,128)S(1)}, f32[256,128]{1,0:T(8,128)S(1)}, u32[]{:S(2)}, u32[]{:S(2)}) %collective-permute-start.3) | collective-permute-done | bytes 131104 | tf_op jit(solution)/shard_map/ppermute | solution.py:104
  91.2 1.4 collective-permute-done.4
  92.6 1.5 collective-permute-done.5
  94.1 1.0 collective-permute-start.6
  95.0 1.4 collective-permute-start.7
  96.5 1.1 collective-permute-start.8
  97.6 1.1 collective-permute-done.6
  98.7 1.1 collective-permute-done.7
  99.8 1.9 %collective-permute-done.8 = bf16[256,128]{1,0:T(8,128)(2,1)S(1)} collective-permute-done((bf16[256,128]{1,0:T(8,128)(2,1)S(1)}, bf16[256,128]{1,0:T(8,128)(2,1)S(1)}, u32[]{:S(2)}, u32[]{:S(2)}) %collective-permute-start.8) | collective-permute-done | bytes 65568 | tf_op jit(solution)/shard_map/ppermute | solution.py:109
  101.7 8.4 %fusion.3 = f32[4,256,4096]{2,1,0:T(8,128)} fusion(bf16[1,128,4096]{2,1,0:T(8,128)(2,1)} %bitcast.15, bf16[1,128,4096]{2,1,0:T(8,128)(2,1)} %bitcast.62, bf16[1,128,4096]{2,1,0:T(8,128)(2,1)S(1)} %bitcast.60, bf16[1,128,4096]{2,1,0:T(8,128)(2,1)S(1)} %bitcast.58, bf16[1,256,128]{2,1,0:T(8,128)(2,1)S(1)} %bitcast.69, bf16[1,256,128]{2,1,0:T(8,128)(2,1)S(1)} %bitcast.68, ...), kind=kOutput, calls=%fused_computation.15 | convolution fusion | flops 1114374144 | bytes 21528576 | tf_op jit(solution)/shard_map/srf,sfh->srh/dot_general | solution.py:26
  110.0 14.9 %multiply_convert_fusion = bf16[1024,4096]{1,0:T(8,128)(2,1)} fusion(f32[1024,4096]{1,0:T(8,128)} %get-tuple-element.19, f32[4,256,4096]{2,1,0:T(8,128)} %fusion.3), kind=kLoop, calls=%fused_computation.6 | loop fusion | flops 25165824 | bytes 41943040 | tf_op jit(solution)/shard_map/convert_element_type | solution.py:28
  124.9 14.7 %fusion.1 = f32[1024,128]{1,0:T(8,128)S(1)} fusion(bf16[1024,128]{1,0:T(8,128)(2,1)S(1)} %copy-done.6, bf16[1024,4096]{1,0:T(8,128)(2,1)} %multiply_convert_fusion, bf16[4096,1024]{1,0:T(8,128)(2,1)} %param.15), kind=kOutput, calls=%fused_computation.12 | convolution fusion | flops 8863612928 | bytes 17563648 | tf_op jit(solution)/shard_map/dot_general | solution.py:35
  140.3 1.5 collective-permute-start.11
  141.9 1.4 collective-permute-start.9
  143.2 1.5 collective-permute-done.10
  144.7 1.5 collective-permute-done.11
  146.2 1.4 collective-permute-done.9
  148.2 4.5 %all-to-all-start.1 = ((bf16[32,8,128]{2,1,0:T(8,128)(2,1)}), bf16[32,8,128]{2,1,0:T(8,128)(2,1)S(1)}, u32[]{:S(2)}, u32[]{:S(2)}) async-start(bf16[32,8,128]{2,1,0:T(8,128)(2,1)} %fusion.38), calls=%async_computation.1 | async-start | bytes 131072 | tf_op jit(solution)/shard_map/all_to_all | solution.py:117
  152.8 7.3 %all-to-all-done.1 = bf16[32,8,128]{2,1,0:T(8,128)(2,1)S(1)} async-done(((bf16[32,8,128]{2,1,0:T(8,128)(2,1)}), bf16[32,8,128]{2,1,0:T(8,128)(2,1)S(1)}, u32[]{:S(2)}, u32[]{:S(2)}) %all-to-all-start.1) | async-done | bytes 65568 | tf_op jit(solution)/shard_map/all_to_all | solution.py:117
  (45 shorter events, 9.4 us)
Async XLA Ops:
  0.0 9.9 %copy-start = (bf16[2048,128]{1,0:T(8,128)(2,1)S(1)}, bf16[2048,128]{1,0:T(8,128)(2,1)}, u32[]{:S(2)}) copy-start(bf16[2048,128]{1,0:T(8,128)(2,1)} %param.10) | copy-start | bytes 1572868
  0.0 56.2 %collective-permute-start = (bf16[128,4096]{1,0:T(8,128)(2,1)}, bf16[128,4096]{1,0:T(8,128)(2,1)S(1)}, u32[]{:S(2)}, u32[]{:S(2)}) collective-permute-start(bf16[128,4096]{1,0:T(8,128)(2,1)} %param.14), channel_id=1, source_target_pairs={{0,8},{8,0},{16,24},{24,16},{1,9},{9,1},{17,25},{25,17},{2,10},{10... | collective-permute-start | bytes 3145736 | tf_op jit(solution)/shard_map/ppermute | solution.py:63
  3.0 53.2 %collective-permute-start.1 = (bf16[128,4096]{1,0:T(8,128)(2,1)}, bf16[128,4096]{1,0:T(8,128)(2,1)S(1)}, u32[]{:S(2)}, u32[]{:S(2)}) collective-permute-start(bf16[128,4096]{1,0:T(8,128)(2,1)} %param.14), channel_id=1, source_target_pairs={{0,16},{8,24},{16,0},{24,8},{1,17},{9,25},{17,1},{25,9},{2,18},{10... | collective-permute-start | bytes 3145736 | tf_op jit(solution)/shard_map/ppermute | solution.py:63
  4.5 51.7 %collective-permute-start.2 = (bf16[128,4096]{1,0:T(8,128)(2,1)}, bf16[128,4096]{1,0:T(8,128)(2,1)}, u32[]{:S(2)}, u32[]{:S(2)}) collective-permute-start(bf16[128,4096]{1,0:T(8,128)(2,1)} %param.14), channel_id=1, source_target_pairs={{0,24},{8,16},{16,8},{24,0},{1,25},{9,17},{17,9},{25,1},{2,26},{10... | collective-permute-start | bytes 3145736 | tf_op jit(solution)/shard_map/ppermute | solution.py:63
  13.3 42.6 %all-to-all-start = ((bf16[32,32,129]{2,1,0:T(8,128)(2,1)}), bf16[32,32,129]{2,1,0:T(8,128)(2,1)S(1)}, u32[]{:S(2)}, u32[]{:S(2)}) async-start(bf16[32,32,129]{2,1,0:T(8,128)(2,1)} %bitcast.8), calls=%async_computation | async-start | bytes 1048576 | tf_op jit(solution)/shard_map/all_to_all | solution.py:89
  56.2 4.2 %copy-start.3 = (bf16[128,4096]{1,0:T(8,128)(2,1)}, bf16[128,4096]{1,0:T(8,128)(2,1)S(1)}, u32[]{:S(2)}) copy-start(bf16[128,4096]{1,0:T(8,128)(2,1)S(1)} %collective-permute-done.1) | copy-start | bytes 3145732
  70.4 31.3 %copy-start.2 = (bf16[128,4096]{1,0:T(8,128)(2,1)S(1)}, bf16[128,4096]{1,0:T(8,128)(2,1)}, u32[]{:S(2)}) copy-start(bf16[128,4096]{1,0:T(8,128)(2,1)} %param.14) | copy-start | bytes 3145732
  70.4 31.3 %copy-start.4 = (bf16[128,128]{1,0:T(8,128)(2,1)S(1)}, bf16[128,128]{1,0:T(8,128)(2,1)}, u32[]{:S(2)}) copy-start(bf16[128,128]{1,0:T(8,128)(2,1)} %param.18) | copy-start | bytes 98308
  85.0 6.2 %collective-permute-start.3 = (f32[256,128]{1,0:T(8,128)S(1)}, f32[256,128]{1,0:T(8,128)S(1)}, u32[]{:S(2)}, u32[]{:S(2)}) collective-permute-start(f32[256,128]{1,0:T(8,128)S(1)} %get-tuple-element.12), channel_id=1, source_target_pairs={{0,8},{8,0},{16,24},{24,16},{1,9},{9,1},{17,25},{25,17},{2,10},{10... | collective-permute-start | bytes 393224 | tf_op jit(solution)/shard_map/ppermute | solution.py:104
  85.9 6.7 %collective-permute-start.4 = (f32[256,128]{1,0:T(8,128)S(1)}, f32[256,128]{1,0:T(8,128)S(1)}, u32[]{:S(2)}, u32[]{:S(2)}) collective-permute-start(f32[256,128]{1,0:T(8,128)S(1)} %get-tuple-element.14), channel_id=1, source_target_pairs={{0,16},{8,24},{16,0},{24,8},{1,17},{9,25},{17,1},{25,9},{2,18},{10... | collective-permute-start | bytes 393224 | tf_op jit(solution)/shard_map/ppermute | solution.py:104
  87.1 6.9 %collective-permute-start.5 = (f32[256,128]{1,0:T(8,128)S(1)}, f32[256,128]{1,0:T(8,128)S(1)}, u32[]{:S(2)}, u32[]{:S(2)}) collective-permute-start(f32[256,128]{1,0:T(8,128)S(1)} %get-tuple-element.13), channel_id=1, source_target_pairs={{0,24},{8,16},{16,8},{24,0},{1,25},{9,17},{17,9},{25,1},{2,26},{10... | collective-permute-start | bytes 393224 | tf_op jit(solution)/shard_map/ppermute | solution.py:104
  94.1 4.7 %collective-permute-start.6 = (bf16[256,128]{1,0:T(8,128)(2,1)S(1)}, bf16[256,128]{1,0:T(8,128)(2,1)S(1)}, u32[]{:S(2)}, u32[]{:S(2)}) collective-permute-start(bf16[256,128]{1,0:T(8,128)(2,1)S(1)} %fusion.37), channel_id=1, source_target_pairs={{0,8},{8,0},{16,24},{24,16},{1,9},{9,1},{17,25},{25,17},{2,10},{10... | collective-permute-start | bytes 196616 | tf_op jit(solution)/shard_map/ppermute | solution.py:109
  95.0 4.7 %collective-permute-start.7 = (bf16[256,128]{1,0:T(8,128)(2,1)S(1)}, bf16[256,128]{1,0:T(8,128)(2,1)S(1)}, u32[]{:S(2)}, u32[]{:S(2)}) collective-permute-start(bf16[256,128]{1,0:T(8,128)(2,1)S(1)} %fusion.37), channel_id=1, source_target_pairs={{0,16},{8,24},{16,0},{24,8},{1,17},{9,25},{17,1},{25,9},{2,18},{10... | collective-permute-start | bytes 196616 | tf_op jit(solution)/shard_map/ppermute | solution.py:109
  96.5 5.2 %collective-permute-start.8 = (bf16[256,128]{1,0:T(8,128)(2,1)S(1)}, bf16[256,128]{1,0:T(8,128)(2,1)S(1)}, u32[]{:S(2)}, u32[]{:S(2)}) collective-permute-start(bf16[256,128]{1,0:T(8,128)(2,1)S(1)} %fusion.37), channel_id=1, source_target_pairs={{0,24},{8,16},{16,8},{24,0},{1,25},{9,17},{17,9},{25,1},{2,26},{10... | collective-permute-start | bytes 196616 | tf_op jit(solution)/shard_map/ppermute | solution.py:109
  110.0 14.9 %copy-start.6 = (bf16[1024,128]{1,0:T(8,128)(2,1)S(1)}, bf16[1024,128]{1,0:T(8,128)(2,1)}, u32[]{:S(2)}) copy-start(bf16[1024,128]{1,0:T(8,128)(2,1)} %param.16) | copy-start | bytes 786436
  124.9 27.8 %copy-start.5 = (s32[128,1]{0,1:T(1,128)S(1)}, s32[128,1]{0,1:T(1,128)}, u32[]{:S(2)}) copy-start(s32[128,1]{0,1:T(1,128)} %param.13) | copy-start | bytes 1540
  124.9 36.6 %copy-start.1 = (bf16[2048,128]{1,0:T(8,128)(2,1)S(1)}, bf16[2048,128]{1,0:T(8,128)(2,1)}, u32[]{:S(2)}) copy-start(bf16[2048,128]{1,0:T(8,128)(2,1)} %param.10) | copy-start | bytes 1572868
  139.7 5.0 %collective-permute-start.10 = (f32[256,128]{1,0:T(8,128)S(1)}, f32[256,128]{1,0:T(8,128)S(1)}, u32[]{:S(2)}, u32[]{:S(2)}) collective-permute-start(f32[256,128]{1,0:T(8,128)S(1)} %get-tuple-element.11), channel_id=1, source_target_pairs={{0,16},{8,24},{16,0},{24,8},{1,17},{9,25},{17,1},{25,9},{2,18},{10... | collective-permute-start | bytes 393224 | tf_op jit(solution)/shard_map/ppermute | solution.py:104
  140.3 5.9 %collective-permute-start.11 = (f32[256,128]{1,0:T(8,128)S(1)}, f32[256,128]{1,0:T(8,128)S(1)}, u32[]{:S(2)}, u32[]{:S(2)}) collective-permute-start(f32[256,128]{1,0:T(8,128)S(1)} %get-tuple-element.10), channel_id=1, source_target_pairs={{0,24},{8,16},{16,8},{24,0},{1,25},{9,17},{17,9},{25,1},{2,26},{10... | collective-permute-start | bytes 393224 | tf_op jit(solution)/shard_map/ppermute | solution.py:104
  141.9 5.7 %collective-permute-start.9 = (f32[256,128]{1,0:T(8,128)S(1)}, f32[256,128]{1,0:T(8,128)S(1)}, u32[]{:S(2)}, u32[]{:S(2)}) collective-permute-start(f32[256,128]{1,0:T(8,128)S(1)} %get-tuple-element.9), channel_id=1, source_target_pairs={{0,8},{8,0},{16,24},{24,16},{1,9},{9,1},{17,25},{25,17},{2,10},{10... | collective-permute-start | bytes 393224 | tf_op jit(solution)/shard_map/ppermute | solution.py:104
  148.2 11.9 %all-to-all-start.1 = ((bf16[32,8,128]{2,1,0:T(8,128)(2,1)}), bf16[32,8,128]{2,1,0:T(8,128)(2,1)S(1)}, u32[]{:S(2)}, u32[]{:S(2)}) async-start(bf16[32,8,128]{2,1,0:T(8,128)(2,1)} %fusion.38), calls=%async_computation.1 | async-start | bytes 131072 | tf_op jit(solution)/shard_map/all_to_all | solution.py:117

commit v5 on v4

--- a/solution.py
+++ b/solution.py
@@ -2,6 +2,7 @@
 import jax.numpy as jnp
 import numpy as np
 from jax import lax
+from jax.experimental import pallas as pl
 from jax.sharding import PartitionSpec as P
 
 PASSES = 2
@@ -15,17 +16,44 @@
     return jnp.concatenate([hi, mid, lo], axis=0)
 
 
-def band_rows(band_values, parts):
+def band_picks(band_values, parts):
     levels = parts.shape[0] // 3
     level_ids = jnp.arange(3 * levels, dtype=jnp.int32) % levels
-    picks = (band_values[:, None] == level_ids[None, :]).astype(jnp.bfloat16)
-    return jnp.dot(picks, parts, preferred_element_type=jnp.float32)
+    return (band_values[..., None] == level_ids).astype(jnp.bfloat16)
 
 
-def first_hidden(rows, weights, band_values, parts):
-    mixed = jnp.einsum("srf,sfh->srh", rows, weights, preferred_element_type=jnp.float32)
-    mixed = mixed.reshape(-1, weights.shape[2]) * band_rows(band_values, parts)
-    return jax.nn.silu(mixed).astype(jnp.bfloat16)
+def first_kernel(x_ref, w_ref, p_ref, s_ref, o_ref):
+    mixed = jnp.dot(x_ref[...], w_ref[...], preferred_element_type=jnp.float32)
+    scale = jnp.dot(p_ref[...], s_ref[...], preferred_element_type=jnp.float32)
+    v = mixed * scale
+    o_ref[...] = (v / (1.0 + jnp.exp(-v))).astype(o_ref.dtype)
+
+
+def first_hidden(rows, weights, picks, parts, interpret=False):
+    n_blocks, n_rows, feat = rows.shape
+    hid = weights.shape[2]
+    n_pick = picks.shape[2]
+    row_tile = min(n_rows, 256)
+    col_tile = min(hid, 512)
+    row_steps = n_rows // row_tile
+    return pl.pallas_call(
+        first_kernel,
+        grid=(n_blocks, row_steps, hid // col_tile),
+        in_specs=[
+            pl.BlockSpec((None, row_tile, feat), lambda s, i, j: (s, i, 0)),
+            pl.BlockSpec((None, feat, col_tile), lambda s, i, j: (s, 0, j)),
+            pl.BlockSpec((None, row_tile, n_pick), lambda s, i, j: (s, i, 0)),
+            pl.BlockSpec((n_pick, col_tile), lambda s, i, j: (0, j)),
+        ],
+        out_specs=pl.BlockSpec((row_tile, col_tile), lambda s, i, j: (s * row_steps + i, j)),
+        out_shape=jax.ShapeDtypeStruct((n_blocks * n_rows, hid), jnp.bfloat16),
+        cost_estimate=pl.CostEstimate(
+            flops=2 * n_blocks * n_rows * hid * (feat + n_pick),
+            transcendentals=n_blocks * n_rows * hid,
+            bytes_accessed=2 * (n_blocks * n_rows * hid + n_blocks * feat * hid * row_steps),
+        ),
+        interpret=interpret,
+    )(rows, weights, picks, parts)
 
 
 def surrogate_tail(hidden_block, middle_weight, out_weight):
@@ -90,12 +118,12 @@
     got = got.reshape(count_all, n_sec, slot_count, feat_width + 1).transpose(1, 0, 2, 3)
     got = got.reshape(n_sec, count_all * slot_count, feat_width + 1)
     rows = got[:, :, :feat_width]
-    got_band = got[:, :, feat_width].astype(jnp.int32).reshape(-1)
+    picks = band_picks(got[:, :, feat_width].astype(jnp.int32), parts)
     every_first = jnp.stack(block_first)
 
     result = None
     for segment_index in range(PASSES):
-        hidden = first_hidden(rows, every_first, got_band, parts)
+        hidden = first_hidden(rows, every_first, picks, parts)
         partial = surrogate_tail(hidden, middle_weight, out_weight).reshape(
             n_sec, rows.shape[1], -1
         )

time: 162 us -> 179 us (1.10)
  Pallas kernels: 0 us -> 47.6 us
  matrix products: 52 us -> 30.1 us
  other arithmetic: 22.1 us -> 11.5 us
    pallas_call x0 -> x2, Pallas kernels: none -> 47.6 us  [first_hidden(): pl.pallas_call(first_kernel, grid=(n_blocks, row_steps, hid // col_tile),...]
    dot_general x3 -> x1, matrix products: 22.6 us -> 0.91 us  [per_device(): jnp.einsum('sro,of->srf', values, back_weight, preferred_element_type=jnp...]
    convert_element_type x2 -> x1, other arithmetic: 15.1 us -> 0.93 us  [band_picks(): return (band_values[..., None] == level_ids).astype(jnp.bfloat16)]
    another operation x0 -> x1, other arithmetic: none -> 3.6 us  [per_device(): every_first = jnp.stack(block_first)]
where the time goes in v5:
time: 179 us; the launch traced here: 178 us
  waiting for transfers between devices  56.6 us (32%)
  Pallas kernels  47.6 us (27%)
  matrix products  30.1 us (17%)
  starting transfers between devices  26.2 us (15%)
  other arithmetic  11.5 us (6%)
  local copies, waits for them, and re-layouts  5.61 us (3%)
    pallas_call x2, Pallas kernels, first_hidden(): pl.pallas_call(first_kernel, grid=(n_blocks, row_steps, hid // col_tile),...  47.6 us
    all_to_all x1, waiting for transfers between devices, per_device(): lax.all_to_all(send, ('sec', 'dev'), split_axis=0, concat_axis=0, tiled=T...  35.4 us
    dot_general x2, matrix products, surrogate_tail(): return jnp.dot(middle, out_weight, preferred_element_type=jnp.float32)  29 us
    ppermute x6, waiting for transfers between devices, per_device(): own_sum = own_sum + lax.ppermute(partial[k], 'sec', xor_pairs(n_sec, k))  9.89 us
    all_to_all x1, waiting for transfers between devices, per_device(): lax.all_to_all(own_values.reshape(count_all, slot_count, out_width), ('se...  7.35 us
    ppermute x6, starting transfers between devices, per_device(): own_sum = own_sum + lax.ppermute(partial[k], 'sec', xor_pairs(n_sec, k))  7.11 us
    all_to_all x1, starting transfers between devices, per_device(): lax.all_to_all(send, ('sec', 'dev'), split_axis=0, concat_axis=0, tiled=T...  6.31 us
    all_to_all x1, starting transfers between devices, per_device(): lax.all_to_all(own_values.reshape(count_all, slot_count, out_width), ('se...  4.62 us
  transfers between devices with their start and end apart: 14, of which 11 were waited for; matrix products, arithmetic and copies ran while one was open for 6% of the time, Pallas kernels for 0%

profile of v5, /device:TPU:0, one launch (start us, length us, event | category | flops | bytes accessed | tf_op | source)
XLA Modules:
  0.0 177.9 jit_solution(14457253198150525301)
XLA Ops:
  0.0 3.0 %collective-permute-start = (bf16[128,4096]{1,0:T(8,128)(2,1)}, bf16[128,4096]{1,0:T(8,128)(2,1)}, u32[]{:S(2)}, u32[]{:S(2)}) collective-permute-start(bf16[128,4096]{1,0:T(8,128)(2,1)} %param.14), channel_id=1, source_target_pairs={{0,8},{8,0},{16,24},{24,16},{1,9},{9,1},{17,25},{25,17},{2,10},{10... | collective-permute-start | bytes 3145736 | tf_op jit(solution)/shard_map/ppermute | solution.py:91
  3.0 1.5 collective-permute-start.1
  7.7 1.6 gather_fusion.1
  12.5 0.9 copy.14
  13.4 6.3 %all-to-all-start = ((bf16[32,32,129]{2,1,0:T(8,128)(2,1)}), bf16[32,32,129]{2,1,0:T(8,128)(2,1)S(1)}, u32[]{:S(2)}, u32[]{:S(2)}) async-start(bf16[32,32,129]{2,1,0:T(8,128)(2,1)} %bitcast.8), calls=%async_computation | async-start | bytes 1048576 | tf_op jit(solution)/shard_map/all_to_all | solution.py:117
  20.6 35.4 %all-to-all-done = bf16[32,32,129]{2,1,0:T(8,128)(2,1)S(1)} async-done(((bf16[32,32,129]{2,1,0:T(8,128)(2,1)}), bf16[32,32,129]{2,1,0:T(8,128)(2,1)S(1)}, u32[]{:S(2)}, u32[]{:S(2)}) %all-to-all-start) | async-done | bytes 264224 | tf_op jit(solution)/shard_map/all_to_all | solution.py:117
  57.0 0.9 compare_convert_fusion.p_ref
  57.9 3.6 %pad_maximum_fusion.w_ref = bf16[4,128,4096]{2,1,0:T(8,128)(2,1)} fusion(bf16[1,128,4096]{2,1,0:T(8,128)(2,1)} %bitcast.15, bf16[1,128,4096]{2,1,0:T(8,128)(2,1)} %bitcast.14, bf16[1,128,4096]{2,1,0:T(8,128)(2,1)} %bitcast.13, bf16[1,128,4096]{2,1,0:T(8,128)(2,1)S(1)} %bitcast.49), kind=kLoop, calls=%fused_computation.4 | loop fusion | flops 6291456 | bytes 8388608 | tf_op jit(solution)/shard_map/stack | solution.py:122
  61.5 23.8 %shard_map.100 = bf16[1024,4096]{1,0:T(8,128)(2,1)} custom-call(bf16[4,256,128]{2,1,0:T(8,128)(2,1)} %slice.56.x_ref, bf16[4,128,4096]{2,1,0:T(8,128)(2,1)} %pad_maximum_fusion.w_ref, bf16[4,256,48]{2,1,0:T(8,128)(2,1)} %compare_convert_fusion.p_ref, bf16[48,4096]{1,0:T(8,128)(2,1)} %pad_maximum_fusion.1.s_ref), custom_call_target="tpu_custom_call" | custom-call | flops 1476395008 | bytes 12582912 | tf_op jit(solution)/shard_map/pallas_call | solution.py:39
  85.4 14.5 %fusion = f32[1024,128]{1,0:T(8,128)S(1)} fusion(bf16[1024,128]{1,0:T(8,128)(2,1)S(1)} %copy-done.4, bf16[1024,4096]{1,0:T(8,128)(2,1)} %shard_map.100, bf16[4096,1024]{1,0:T(8,128)(2,1)} %param.15), kind=kOutput, calls=%fused_computation.7 | convolution fusion | flops 8863612928 | bytes 17563648 | tf_op jit(solution)/shard_map/dot_general | solution.py:63
  99.9 0.9 collective-permute-start.3
  100.8 1.2 collective-permute-start.4
  102.0 1.4 collective-permute-start.5
  103.5 2.6 %collective-permute-done.3 = f32[256,128]{1,0:T(8,128)S(1)} collective-permute-done((f32[256,128]{1,0:T(8,128)S(1)}, f32[256,128]{1,0:T(8,128)S(1)}, u32[]{:S(2)}, u32[]{:S(2)}) %collective-permute-start.3) | collective-permute-done | bytes 131104 | tf_op jit(solution)/shard_map/ppermute | solution.py:132
  106.1 1.4 collective-permute-done.4
  107.5 1.6 collective-permute-done.5
  109.1 0.9 collective-permute-start.6
  110.0 1.5 collective-permute-start.7
  111.4 1.2 collective-permute-start.8
  112.6 1.0 collective-permute-done.6
  113.6 1.1 collective-permute-done.7
  114.7 1.9 %collective-permute-done.8 = bf16[256,128]{1,0:T(8,128)(2,1)S(1)} collective-permute-done((bf16[256,128]{1,0:T(8,128)(2,1)S(1)}, bf16[256,128]{1,0:T(8,128)(2,1)S(1)}, u32[]{:S(2)}, u32[]{:S(2)}) %collective-permute-start.8) | collective-permute-done | bytes 65568 | tf_op jit(solution)/shard_map/ppermute | solution.py:137
  116.6 0.9 fusion.2.x_ref
  117.5 23.8 %shard_map.101 = bf16[1024,4096]{1,0:T(8,128)(2,1)} custom-call(bf16[4,256,128]{2,1,0:T(8,128)(2,1)} %fusion.2.x_ref, bf16[4,128,4096]{2,1,0:T(8,128)(2,1)} %pad_maximum_fusion.w_ref, bf16[4,256,48]{2,1,0:T(8,128)(2,1)} %compare_convert_fusion.p_ref, bf16[48,4096]{1,0:T(8,128)(2,1)} %pad_maximum_fusion.1.s_ref), custom_call_target="tpu_custom_call" | custom-call | flops 1476395008 | bytes 12582912 | tf_op jit(solution)/shard_map/pallas_call | solution.py:39
  141.3 14.5 %fusion.1 = f32[1024,128]{1,0:T(8,128)S(1)} fusion(bf16[1024,128]{1,0:T(8,128)(2,1)S(1)} %copy-done.4, bf16[1024,4096]{1,0:T(8,128)(2,1)} %shard_map.101, bf16[4096,1024]{1,0:T(8,128)(2,1)} %param.15), kind=kOutput, calls=%fused_computation.8 | convolution fusion | flops 8863612928 | bytes 17563648 | tf_op jit(solution)/shard_map/dot_general | solution.py:63
  156.5 1.5 collective-permute-start.11
  158.0 1.4 collective-permute-start.9
  159.4 1.5 collective-permute-done.10
  160.9 1.5 collective-permute-done.11
  162.4 1.4 collective-permute-done.9
  164.4 4.6 %all-to-all-start.1 = ((bf16[32,8,128]{2,1,0:T(8,128)(2,1)}), bf16[32,8,128]{2,1,0:T(8,128)(2,1)S(1)}, u32[]{:S(2)}, u32[]{:S(2)}) async-start(bf16[32,8,128]{2,1,0:T(8,128)(2,1)} %fusion.17), calls=%async_computation.1 | async-start | bytes 131072 | tf_op jit(solution)/shard_map/all_to_all | solution.py:145
  169.1 7.3 %all-to-all-done.1 = bf16[32,8,128]{2,1,0:T(8,128)(2,1)S(1)} async-done(((bf16[32,8,128]{2,1,0:T(8,128)(2,1)}), bf16[32,8,128]{2,1,0:T(8,128)(2,1)S(1)}, u32[]{:S(2)}, u32[]{:S(2)}) %all-to-all-start.1) | async-done | bytes 65568 | tf_op jit(solution)/shard_map/all_to_all | solution.py:145
  (45 shorter events, 10.9 us)
Async XLA Ops:
  0.0 10.0 %copy-start = (bf16[2048,128]{1,0:T(8,128)(2,1)S(1)}, bf16[2048,128]{1,0:T(8,128)(2,1)}, u32[]{:S(2)}) copy-start(bf16[2048,128]{1,0:T(8,128)(2,1)} %param.10) | copy-start | bytes 1572868
  0.0 57.9 %copy-start.1 = (bf16[128,4096]{1,0:T(8,128)(2,1)S(1)}, bf16[128,4096]{1,0:T(8,128)(2,1)}, u32[]{:S(2)}) copy-start(bf16[128,4096]{1,0:T(8,128)(2,1)} %param.14) | copy-start | bytes 3145732
  0.0 19.7 %copy-start.2 = (f32[16,4096]{1,0:T(8,128)S(1)}, f32[16,4096]{1,0:T(8,128)}, u32[]{:S(2)}) copy-start(f32[16,4096]{1,0:T(8,128)} %param.17) | copy-start | bytes 786436
  0.0 57.9 %collective-permute-start = (bf16[128,4096]{1,0:T(8,128)(2,1)}, bf16[128,4096]{1,0:T(8,128)(2,1)}, u32[]{:S(2)}, u32[]{:S(2)}) collective-permute-start(bf16[128,4096]{1,0:T(8,128)(2,1)} %param.14), channel_id=1, source_target_pairs={{0,8},{8,0},{16,24},{24,16},{1,9},{9,1},{17,25},{25,17},{2,10},{10... | collective-permute-start | bytes 3145736 | tf_op jit(solution)/shard_map/ppermute | solution.py:91
  3.0 54.9 %collective-permute-start.1 = (bf16[128,4096]{1,0:T(8,128)(2,1)}, bf16[128,4096]{1,0:T(8,128)(2,1)}, u32[]{:S(2)}, u32[]{:S(2)}) collective-permute-start(bf16[128,4096]{1,0:T(8,128)(2,1)} %param.14), channel_id=1, source_target_pairs={{0,16},{8,24},{16,0},{24,8},{1,17},{9,25},{17,1},{25,9},{2,18},{10... | collective-permute-start | bytes 3145736 | tf_op jit(solution)/shard_map/ppermute | solution.py:91
  4.6 53.3 %collective-permute-start.2 = (bf16[128,4096]{1,0:T(8,128)(2,1)}, bf16[128,4096]{1,0:T(8,128)(2,1)}, u32[]{:S(2)}, u32[]{:S(2)}) collective-permute-start(bf16[128,4096]{1,0:T(8,128)(2,1)} %param.14), channel_id=1, source_target_pairs={{0,24},{8,16},{16,8},{24,0},{1,25},{9,17},{17,9},{25,1},{2,26},{10... | collective-permute-start | bytes 3145736 | tf_op jit(solution)/shard_map/ppermute | solution.py:91
  13.4 42.6 %all-to-all-start = ((bf16[32,32,129]{2,1,0:T(8,128)(2,1)}), bf16[32,32,129]{2,1,0:T(8,128)(2,1)S(1)}, u32[]{:S(2)}, u32[]{:S(2)}) async-start(bf16[32,32,129]{2,1,0:T(8,128)(2,1)} %bitcast.8), calls=%async_computation | async-start | bytes 1048576 | tf_op jit(solution)/shard_map/all_to_all | solution.py:117
  61.5 23.8 %copy-start.4 = (bf16[1024,128]{1,0:T(8,128)(2,1)S(1)}, bf16[1024,128]{1,0:T(8,128)(2,1)}, u32[]{:S(2)}) copy-start(bf16[1024,128]{1,0:T(8,128)(2,1)} %param.16) | copy-start | bytes 786436
  85.4 31.2 %copy-start.5 = (bf16[128,128]{1,0:T(8,128)(2,1)S(1)}, bf16[128,128]{1,0:T(8,128)(2,1)}, u32[]{:S(2)}) copy-start(bf16[128,128]{1,0:T(8,128)(2,1)} %param.18) | copy-start | bytes 98308
  99.9 6.2 %collective-permute-start.3 = (f32[256,128]{1,0:T(8,128)S(1)}, f32[256,128]{1,0:T(8,128)S(1)}, u32[]{:S(2)}, u32[]{:S(2)}) collective-permute-start(f32[256,128]{1,0:T(8,128)S(1)} %get-tuple-element.12), channel_id=1, source_target_pairs={{0,8},{8,0},{16,24},{24,16},{1,9},{9,1},{17,25},{25,17},{2,10},{10... | collective-permute-start | bytes 393224 | tf_op jit(solution)/shard_map/ppermute | solution.py:132
  100.8 6.6 %collective-permute-start.4 = (f32[256,128]{1,0:T(8,128)S(1)}, f32[256,128]{1,0:T(8,128)S(1)}, u32[]{:S(2)}, u32[]{:S(2)}) collective-permute-start(f32[256,128]{1,0:T(8,128)S(1)} %get-tuple-element.14), channel_id=1, source_target_pairs={{0,16},{8,24},{16,0},{24,8},{1,17},{9,25},{17,1},{25,9},{2,18},{10... | collective-permute-start | bytes 393224 | tf_op jit(solution)/shard_map/ppermute | solution.py:132
  102.0 7.0 %collective-permute-start.5 = (f32[256,128]{1,0:T(8,128)S(1)}, f32[256,128]{1,0:T(8,128)S(1)}, u32[]{:S(2)}, u32[]{:S(2)}) collective-permute-start(f32[256,128]{1,0:T(8,128)S(1)} %get-tuple-element.13), channel_id=1, source_target_pairs={{0,24},{8,16},{16,8},{24,0},{1,25},{9,17},{17,9},{25,1},{2,26},{10... | collective-permute-start | bytes 393224 | tf_op jit(solution)/shard_map/ppermute | solution.py:132
  109.1 4.6 %collective-permute-start.6 = (bf16[256,128]{1,0:T(8,128)(2,1)S(1)}, bf16[256,128]{1,0:T(8,128)(2,1)S(1)}, u32[]{:S(2)}, u32[]{:S(2)}) collective-permute-start(bf16[256,128]{1,0:T(8,128)(2,1)S(1)} %fusion.16), channel_id=1, source_target_pairs={{0,8},{8,0},{16,24},{24,16},{1,9},{9,1},{17,25},{25,17},{2,10},{10... | collective-permute-start | bytes 196616 | tf_op jit(solution)/shard_map/ppermute | solution.py:137
  110.0 4.7 %collective-permute-start.7 = (bf16[256,128]{1,0:T(8,128)(2,1)S(1)}, bf16[256,128]{1,0:T(8,128)(2,1)S(1)}, u32[]{:S(2)}, u32[]{:S(2)}) collective-permute-start(bf16[256,128]{1,0:T(8,128)(2,1)S(1)} %fusion.16), channel_id=1, source_target_pairs={{0,16},{8,24},{16,0},{24,8},{1,17},{9,25},{17,1},{25,9},{2,18},{10... | collective-permute-start | bytes 196616 | tf_op jit(solution)/shard_map/ppermute | solution.py:137
  111.4 5.2 %collective-permute-start.8 = (bf16[256,128]{1,0:T(8,128)(2,1)S(1)}, bf16[256,128]{1,0:T(8,128)(2,1)S(1)}, u32[]{:S(2)}, u32[]{:S(2)}) collective-permute-start(bf16[256,128]{1,0:T(8,128)(2,1)S(1)} %fusion.16), channel_id=1, source_target_pairs={{0,24},{8,16},{16,8},{24,0},{1,25},{9,17},{17,9},{25,1},{2,26},{10... | collective-permute-start | bytes 196616 | tf_op jit(solution)/shard_map/ppermute | solution.py:137
  141.3 27.7 %copy-start.3 = (s32[128,1]{0,1:T(1,128)S(1)}, s32[128,1]{0,1:T(1,128)}, u32[]{:S(2)}) copy-start(s32[128,1]{0,1:T(1,128)} %param.13) | copy-start | bytes 1540
  155.9 5.0 %collective-permute-start.10 = (f32[256,128]{1,0:T(8,128)S(1)}, f32[256,128]{1,0:T(8,128)S(1)}, u32[]{:S(2)}, u32[]{:S(2)}) collective-permute-start(f32[256,128]{1,0:T(8,128)S(1)} %get-tuple-element.11), channel_id=1, source_target_pairs={{0,16},{8,24},{16,0},{24,8},{1,17},{9,25},{17,1},{25,9},{2,18},{10... | collective-permute-start | bytes 393224 | tf_op jit(solution)/shard_map/ppermute | solution.py:132
  156.5 5.9 %collective-permute-start.11 = (f32[256,128]{1,0:T(8,128)S(1)}, f32[256,128]{1,0:T(8,128)S(1)}, u32[]{:S(2)}, u32[]{:S(2)}) collective-permute-start(f32[256,128]{1,0:T(8,128)S(1)} %get-tuple-element.10), channel_id=1, source_target_pairs={{0,24},{8,16},{16,8},{24,0},{1,25},{9,17},{17,9},{25,1},{2,26},{10... | collective-permute-start | bytes 393224 | tf_op jit(solution)/shard_map/ppermute | solution.py:132
  158.0 5.8 %collective-permute-start.9 = (f32[256,128]{1,0:T(8,128)S(1)}, f32[256,128]{1,0:T(8,128)S(1)}, u32[]{:S(2)}, u32[]{:S(2)}) collective-permute-start(f32[256,128]{1,0:T(8,128)S(1)} %get-tuple-element.9), channel_id=1, source_target_pairs={{0,8},{8,0},{16,24},{24,16},{1,9},{9,1},{17,25},{25,17},{2,10},{10... | collective-permute-start | bytes 393224 | tf_op jit(solution)/shard_map/ppermute | solution.py:132
  164.4 12.0 %all-to-all-start.1 = ((bf16[32,8,128]{2,1,0:T(8,128)(2,1)}), bf16[32,8,128]{2,1,0:T(8,128)(2,1)S(1)}, u32[]{:S(2)}, u32[]{:S(2)}) async-start(bf16[32,8,128]{2,1,0:T(8,128)(2,1)} %fusion.17), calls=%async_computation.1 | async-start | bytes 131072 | tf_op jit(solution)/shard_map/all_to_all | solution.py:145

commit v6 on v5

--- a/solution.py
+++ b/solution.py
@@ -22,26 +22,40 @@
     return (band_values[..., None] == level_ids).astype(jnp.bfloat16)
 
 
-def first_kernel(x_ref, w_ref, p_ref, s_ref, o_ref):
-    mixed = jnp.dot(x_ref[...], w_ref[...], preferred_element_type=jnp.float32)
-    scale = jnp.dot(p_ref[...], s_ref[...], preferred_element_type=jnp.float32)
-    v = mixed * scale
-    o_ref[...] = (v / (1.0 + jnp.exp(-v))).astype(o_ref.dtype)
+def first_kernel(x_ref, *refs):
+    w_refs, (p_ref, s_ref, o_ref) = refs[:-3], refs[-3:]
+    block = pl.program_id(0)
+    for k, w_ref in enumerate(w_refs):
+
+        @pl.when(block == k)
+        def _():
+            mixed = jnp.dot(x_ref[...], w_ref[...], preferred_element_type=jnp.float32)
+            scale = jnp.dot(p_ref[...], s_ref[...], preferred_element_type=jnp.float32)
+            v = mixed * scale
+            o_ref[...] = (v * jax.nn.sigmoid(v)).astype(o_ref.dtype)
+
+
+def weight_spec(k, feat, col_tile, col_steps):
+    def index(s, i, j):
+        return (0, jnp.where(s == k, j, jnp.where(s < k, 0, col_steps - 1)))
+
+    return pl.BlockSpec((feat, col_tile), index)
 
 
 def first_hidden(rows, weights, picks, parts, interpret=False):
     n_blocks, n_rows, feat = rows.shape
-    hid = weights.shape[2]
+    hid = weights[0].shape[1]
     n_pick = picks.shape[2]
     row_tile = min(n_rows, 256)
-    col_tile = min(hid, 512)
+    col_tile = min(hid, 4096)
     row_steps = n_rows // row_tile
+    col_steps = hid // col_tile
     return pl.pallas_call(
         first_kernel,
-        grid=(n_blocks, row_steps, hid // col_tile),
-        in_specs=[
-            pl.BlockSpec((None, row_tile, feat), lambda s, i, j: (s, i, 0)),
-            pl.BlockSpec((None, feat, col_tile), lambda s, i, j: (s, 0, j)),
+        grid=(n_blocks, row_steps, col_steps),
+        in_specs=[pl.BlockSpec((None, row_tile, feat), lambda s, i, j: (s, i, 0))]
+        + [weight_spec(k, feat, col_tile, col_steps) for k in range(n_blocks)]
+        + [
             pl.BlockSpec((None, row_tile, n_pick), lambda s, i, j: (s, i, 0)),
             pl.BlockSpec((n_pick, col_tile), lambda s, i, j: (0, j)),
         ],
@@ -53,7 +67,7 @@
             bytes_accessed=2 * (n_blocks * n_rows * hid + n_blocks * feat * hid * row_steps),
         ),
         interpret=interpret,
-    )(rows, weights, picks, parts)
+    )(rows, *weights, picks, parts)
 
 
 def surrogate_tail(hidden_block, middle_weight, out_weight):
@@ -119,11 +133,10 @@
     got = got.reshape(n_sec, count_all * slot_count, feat_width + 1)
     rows = got[:, :, :feat_width]
     picks = band_picks(got[:, :, feat_width].astype(jnp.int32), parts)
-    every_first = jnp.stack(block_first)
 
     result = None
     for segment_index in range(PASSES):
-        hidden = first_hidden(rows, every_first, picks, parts)
+        hidden = first_hidden(rows, block_first, picks, parts)
         partial = surrogate_tail(hidden, middle_weight, out_weight).reshape(
             n_sec, rows.shape[1], -1
         )

time: 179 us -> 148 us (0.83)
  Pallas kernels: 47.6 us -> 19 us
  other arithmetic: 11.5 us -> 8.91 us
  local copies, waits for them, and re-layouts: 5.61 us -> 7.97 us
    pallas_call x2, Pallas kernels: 47.6 us -> 19 us  [first_hidden(): pl.pallas_call(first_kernel, grid=(n_blocks, row_steps, col_steps), in_sp...]
    another operation x1 -> x0, other arithmetic: 3.6 us -> none  [per_device(): every_first = jnp.stack(block_first)]
  transfers between devices with their start and end apart: 14 -> 14, of which waited for: 11 -> 11; matrix products, arithmetic and copies ran while one was open for 6% -> 9% of each run, Pallas kernels for 0% -> 0%
where the time goes in v6:
time: 148 us
  waiting for transfers between devices  55.5 us (38%)
  matrix products  30.2 us (20%)
  starting transfers between devices  26 us (18%)
  Pallas kernels  19 us (13%)
  other arithmetic  8.91 us (6%)
  local copies, waits for them, and re-layouts  7.97 us (5%)
    all_to_all x1, waiting for transfers between devices, per_device(): lax.all_to_all(send, ('sec', 'dev'), split_axis=0, concat_axis=0, tiled=T...  34.3 us
    dot_general x2, matrix products, surrogate_tail(): return jnp.dot(middle, out_weight, preferred_element_type=jnp.float32)  29 us
    pallas_call x2, Pallas kernels, first_hidden(): pl.pallas_call(first_kernel, grid=(n_blocks, row_steps, col_steps), in_sp...  19 us
    ppermute x6, waiting for transfers between devices, per_device(): own_sum = own_sum + lax.ppermute(partial[k], 'sec', xor_pairs(n_sec, k))  9.78 us
    all_to_all x1, waiting for transfers between devices, per_device(): lax.all_to_all(own_values.reshape(count_all, slot_count, out_width), ('se...  7.35 us
    ppermute x6, starting transfers between devices, per_device(): own_sum = own_sum + lax.ppermute(partial[k], 'sec', xor_pairs(n_sec, k))  7.11 us
    all_to_all x1, starting transfers between devices, per_device(): lax.all_to_all(send, ('sec', 'dev'), split_axis=0, concat_axis=0, tiled=T...  6.44 us
    ppermute x3, starting transfers between devices, per_device(): lax.ppermute(first_layers, 'sec', xor_pairs(n_sec, k))  4.5 us
  transfers between devices with their start and end apart: 14, of which 11 were waited for; matrix products, arithmetic and copies ran while one was open for 9% of the time, Pallas kernels for 0%

profile of v6, /device:TPU:0, one launch (start us, length us, event | category | flops | bytes accessed | tf_op | source)
XLA Modules:
  0.0 147.7 jit_solution(10067551792711637690)
XLA Ops:
  0.0 3.0 %collective-permute-start = (bf16[128,4096]{1,0:T(8,128)(2,1)}, bf16[128,4096]{1,0:T(8,128)(2,1)S(1)}, u32[]{:S(2)}, u32[]{:S(2)}) collective-permute-start(bf16[128,4096]{1,0:T(8,128)(2,1)} %refs_0_.3), channel_id=1, source_target_pairs={{0,8},{8,0},{16,24},{24,16},{1,9},{9,1},{17,25},{25,17},{2,10},{10... | collective-permute-start | bytes 3145736 | tf_op jit(solution)/shard_map/ppermute | solution.py:105
  3.0 1.5 %collective-permute-start.1 = (bf16[128,4096]{1,0:T(8,128)(2,1)}, bf16[128,4096]{1,0:T(8,128)(2,1)S(1)}, u32[]{:S(2)}, u32[]{:S(2)}) collective-permute-start(bf16[128,4096]{1,0:T(8,128)(2,1)} %refs_0_.3), channel_id=1, source_target_pairs={{0,16},{8,24},{16,0},{24,8},{1,17},{9,25},{17,1},{25,9},{2,18},{10... | collective-permute-start | bytes 3145736 | tf_op jit(solution)/shard_map/ppermute | solution.py:105
  7.6 1.6 %gather_fusion.1 = s32[128]{0:T(128)S(1)} fusion(s32[2048]{0:T(1024)} %param.11, s32[1024]{0:T(1024)S(1)} %pad_clamp_fusion.2), kind=kCustom, calls=%fused_computation.1 | custom fusion | bytes 1536 | tf_op jit(solution)/shard_map/jit(_take)/gather | solution.py:110
  13.3 6.4 %all-to-all-start = ((bf16[32,32,129]{2,1,0:T(8,128)(2,1)}), bf16[32,32,129]{2,1,0:T(8,128)(2,1)}, u32[]{:S(2)}, u32[]{:S(2)}) async-start(bf16[32,32,129]{2,1,0:T(8,128)(2,1)} %bitcast.8), calls=%async_computation | async-start | bytes 1048576 | tf_op jit(solution)/shard_map/all_to_all | solution.py:131
  19.8 1.1 fusion.33
  21.7 34.3 %all-to-all-done = bf16[32,32,129]{2,1,0:T(8,128)(2,1)} async-done(((bf16[32,32,129]{2,1,0:T(8,128)(2,1)}), bf16[32,32,129]{2,1,0:T(8,128)(2,1)}, u32[]{:S(2)}, u32[]{:S(2)}) %all-to-all-start) | async-done | bytes 264224 | tf_op jit(solution)/shard_map/all_to_all | solution.py:131
  56.0 1.1 copy_bitcast_fusion
  58.0 0.9 compare_convert_fusion.refs_4_
  59.0 1.0 copy-done.1
  60.3 9.5 %shard_map.100 = bf16[1024,4096]{1,0:T(8,128)(2,1)} custom-call(bf16[4,256,128]{2,1,0:T(8,128)(2,1)} %slice.56.x_ref, bf16[128,4096]{1,0:T(8,128)(2,1)} %refs_0_.3, bf16[128,4096]{1,0:T(8,128)(2,1)} %copy-done.1, bf16[128,4096]{1,0:T(8,128)(2,1)} %copy-done.2, bf16[128,4096]{1,0:T(8,128)(2,1)} %collective-permute-done.2.refs_3_, ...), custom_call_target="tpu_custom_call" | custom-call | flops 1476395008 | bytes 12582912 | tf_op jit(solution)/shard_map/pallas_call | solution.py:53
  69.8 14.5 %fusion = f32[1024,128]{1,0:T(8,128)S(1)} fusion(bf16[1024,128]{1,0:T(8,128)(2,1)S(1)} %copy-done.4, bf16[1024,4096]{1,0:T(8,128)(2,1)} %shard_map.100, bf16[4096,1024]{1,0:T(8,128)(2,1)} %param.15), kind=kOutput, calls=%fused_computation.6 | convolution fusion | flops 8863612928 | bytes 17563648 | tf_op jit(solution)/shard_map/dot_general | solution.py:77
  85.2 1.2 collective-permute-start.4
  86.5 1.4 collective-permute-start.5
  87.9 2.6 %collective-permute-done.3 = f32[256,128]{1,0:T(8,128)S(1)} collective-permute-done((f32[256,128]{1,0:T(8,128)S(1)}, f32[256,128]{1,0:T(8,128)S(1)}, u32[]{:S(2)}, u32[]{:S(2)}) %collective-permute-start.3) | collective-permute-done | bytes 131104 | tf_op jit(solution)/shard_map/ppermute | solution.py:145
  90.5 1.4 collective-permute-done.4
  91.9 1.4 collective-permute-done.5
  93.4 1.0 collective-permute-start.6
  94.4 1.4 collective-permute-start.7
  95.8 1.1 collective-permute-start.8
  96.9 1.1 collective-permute-done.6
  98.0 1.1 collective-permute-done.7
  99.1 1.9 %collective-permute-done.8 = bf16[256,128]{1,0:T(8,128)(2,1)S(1)} collective-permute-done((bf16[256,128]{1,0:T(8,128)(2,1)S(1)}, bf16[256,128]{1,0:T(8,128)(2,1)S(1)}, u32[]{:S(2)}, u32[]{:S(2)}) %collective-permute-start.8) | collective-permute-done | bytes 65568 | tf_op jit(solution)/shard_map/ppermute | solution.py:150
  101.0 0.9 fusion.2.x_ref
  101.9 9.5 %shard_map.101 = bf16[1024,4096]{1,0:T(8,128)(2,1)} custom-call(bf16[4,256,128]{2,1,0:T(8,128)(2,1)} %fusion.2.x_ref, bf16[128,4096]{1,0:T(8,128)(2,1)} %refs_0_.3, bf16[128,4096]{1,0:T(8,128)(2,1)} %copy-done.1, bf16[128,4096]{1,0:T(8,128)(2,1)} %copy-done.2, bf16[128,4096]{1,0:T(8,128)(2,1)} %collective-permute-done.2.refs_3_, ...), custom_call_target="tpu_custom_call" | custom-call | flops 1476395008 | bytes 12582912 | tf_op jit(solution)/shard_map/pallas_call | solution.py:53
  111.4 14.5 %fusion.1 = f32[1024,128]{1,0:T(8,128)S(1)} fusion(bf16[1024,128]{1,0:T(8,128)(2,1)S(1)} %copy-done.4, bf16[1024,4096]{1,0:T(8,128)(2,1)} %shard_map.101, bf16[4096,1024]{1,0:T(8,128)(2,1)} %param.15), kind=kOutput, calls=%fused_computation.7 | convolution fusion | flops 8863612928 | bytes 17563648 | tf_op jit(solution)/shard_map/dot_general | solution.py:77
  126.6 1.5 %collective-permute-start.11 = (f32[256,128]{1,0:T(8,128)S(1)}, f32[256,128]{1,0:T(8,128)S(1)}, u32[]{:S(2)}, u32[]{:S(2)}) collective-permute-start(f32[256,128]{1,0:T(8,128)S(1)} %get-tuple-element.10), channel_id=1, source_target_pairs={{0,24},{8,16},{16,8},{24,0},{1,25},{9,17},{17,9},{25,1},{2,26},{10... | collective-permute-start | bytes 393224 | tf_op jit(solution)/shard_map/ppermute | solution.py:145
  128.2 1.4 collective-permute-start.9
  129.5 1.5 %collective-permute-done.10 = f32[256,128]{1,0:T(8,128)S(1)} collective-permute-done((f32[256,128]{1,0:T(8,128)S(1)}, f32[256,128]{1,0:T(8,128)S(1)}, u32[]{:S(2)}, u32[]{:S(2)}) %collective-permute-start.10) | collective-permute-done | bytes 131104 | tf_op jit(solution)/shard_map/ppermute | solution.py:145
  131.0 1.5 collective-permute-done.11
  132.5 1.4 collective-permute-done.9
  134.5 4.4 %all-to-all-start.1 = ((bf16[32,8,128]{2,1,0:T(8,128)(2,1)}), bf16[32,8,128]{2,1,0:T(8,128)(2,1)S(1)}, u32[]{:S(2)}, u32[]{:S(2)}) async-start(bf16[32,8,128]{2,1,0:T(8,128)(2,1)} %fusion.17), calls=%async_computation.1 | async-start | bytes 131072 | tf_op jit(solution)/shard_map/all_to_all | solution.py:158
  139.0 7.3 %all-to-all-done.1 = bf16[32,8,128]{2,1,0:T(8,128)(2,1)S(1)} async-done(((bf16[32,8,128]{2,1,0:T(8,128)(2,1)}), bf16[32,8,128]{2,1,0:T(8,128)(2,1)S(1)}, u32[]{:S(2)}, u32[]{:S(2)}) %all-to-all-start.1) | async-done | bytes 65568 | tf_op jit(solution)/shard_map/all_to_all | solution.py:158
  (44 shorter events, 13.0 us)
Async XLA Ops:
  0.0 9.9 %copy-start = (bf16[2048,128]{1,0:T(8,128)(2,1)S(1)}, bf16[2048,128]{1,0:T(8,128)(2,1)}, u32[]{:S(2)}) copy-start(bf16[2048,128]{1,0:T(8,128)(2,1)} %param.10) | copy-start | bytes 1572868
  0.0 59.0 %collective-permute-start = (bf16[128,4096]{1,0:T(8,128)(2,1)}, bf16[128,4096]{1,0:T(8,128)(2,1)S(1)}, u32[]{:S(2)}, u32[]{:S(2)}) collective-permute-start(bf16[128,4096]{1,0:T(8,128)(2,1)} %refs_0_.3), channel_id=1, source_target_pairs={{0,8},{8,0},{16,24},{24,16},{1,9},{9,1},{17,25},{25,17},{2,10},{10... | collective-permute-start | bytes 3145736 | tf_op jit(solution)/shard_map/ppermute | solution.py:105
  3.0 56.0 %collective-permute-start.1 = (bf16[128,4096]{1,0:T(8,128)(2,1)}, bf16[128,4096]{1,0:T(8,128)(2,1)S(1)}, u32[]{:S(2)}, u32[]{:S(2)}) collective-permute-start(bf16[128,4096]{1,0:T(8,128)(2,1)} %refs_0_.3), channel_id=1, source_target_pairs={{0,16},{8,24},{16,0},{24,8},{1,17},{9,25},{17,1},{25,9},{2,18},{10... | collective-permute-start | bytes 3145736 | tf_op jit(solution)/shard_map/ppermute | solution.py:105
  4.5 54.5 %collective-permute-start.2 = (bf16[128,4096]{1,0:T(8,128)(2,1)}, bf16[128,4096]{1,0:T(8,128)(2,1)}, u32[]{:S(2)}, u32[]{:S(2)}) collective-permute-start(bf16[128,4096]{1,0:T(8,128)(2,1)} %refs_0_.3), channel_id=1, source_target_pairs={{0,24},{8,16},{16,8},{24,0},{1,25},{9,17},{17,9},{25,1},{2,26},{10... | collective-permute-start | bytes 3145736 | tf_op jit(solution)/shard_map/ppermute | solution.py:105
  13.3 42.7 %all-to-all-start = ((bf16[32,32,129]{2,1,0:T(8,128)(2,1)}), bf16[32,32,129]{2,1,0:T(8,128)(2,1)}, u32[]{:S(2)}, u32[]{:S(2)}) async-start(bf16[32,32,129]{2,1,0:T(8,128)(2,1)} %bitcast.8), calls=%async_computation | async-start | bytes 1048576 | tf_op jit(solution)/shard_map/all_to_all | solution.py:131
  19.8 50.0 %copy-start.4 = (bf16[1024,128]{1,0:T(8,128)(2,1)S(1)}, bf16[1024,128]{1,0:T(8,128)(2,1)}, u32[]{:S(2)}) copy-start(bf16[1024,128]{1,0:T(8,128)(2,1)} %param.16) | copy-start | bytes 786436
  59.0 1.0 copy-start.1
  59.0 1.3 copy-start.2
  69.8 31.2 %copy-start.5 = (bf16[128,128]{1,0:T(8,128)(2,1)S(1)}, bf16[128,128]{1,0:T(8,128)(2,1)}, u32[]{:S(2)}) copy-start(bf16[128,128]{1,0:T(8,128)(2,1)} %param.18) | copy-start | bytes 98308
  84.4 6.2 %collective-permute-start.3 = (f32[256,128]{1,0:T(8,128)S(1)}, f32[256,128]{1,0:T(8,128)S(1)}, u32[]{:S(2)}, u32[]{:S(2)}) collective-permute-start(f32[256,128]{1,0:T(8,128)S(1)} %get-tuple-element.12), channel_id=1, source_target_pairs={{0,8},{8,0},{16,24},{24,16},{1,9},{9,1},{17,25},{25,17},{2,10},{10... | collective-permute-start | bytes 393224 | tf_op jit(solution)/shard_map/ppermute | solution.py:145
  85.2 6.6 %collective-permute-start.4 = (f32[256,128]{1,0:T(8,128)S(1)}, f32[256,128]{1,0:T(8,128)S(1)}, u32[]{:S(2)}, u32[]{:S(2)}) collective-permute-start(f32[256,128]{1,0:T(8,128)S(1)} %get-tuple-element.14), channel_id=1, source_target_pairs={{0,16},{8,24},{16,0},{24,8},{1,17},{9,25},{17,1},{25,9},{2,18},{10... | collective-permute-start | bytes 393224 | tf_op jit(solution)/shard_map/ppermute | solution.py:145
  86.5 6.9 %collective-permute-start.5 = (f32[256,128]{1,0:T(8,128)S(1)}, f32[256,128]{1,0:T(8,128)S(1)}, u32[]{:S(2)}, u32[]{:S(2)}) collective-permute-start(f32[256,128]{1,0:T(8,128)S(1)} %get-tuple-element.13), channel_id=1, source_target_pairs={{0,24},{8,16},{16,8},{24,0},{1,25},{9,17},{17,9},{25,1},{2,26},{10... | collective-permute-start | bytes 393224 | tf_op jit(solution)/shard_map/ppermute | solution.py:145
  93.4 4.6 %collective-permute-start.6 = (bf16[256,128]{1,0:T(8,128)(2,1)S(1)}, bf16[256,128]{1,0:T(8,128)(2,1)S(1)}, u32[]{:S(2)}, u32[]{:S(2)}) collective-permute-start(bf16[256,128]{1,0:T(8,128)(2,1)S(1)} %fusion.16), channel_id=1, source_target_pairs={{0,8},{8,0},{16,24},{24,16},{1,9},{9,1},{17,25},{25,17},{2,10},{10... | collective-permute-start | bytes 196616 | tf_op jit(solution)/shard_map/ppermute | solution.py:150
  94.4 4.7 %collective-permute-start.7 = (bf16[256,128]{1,0:T(8,128)(2,1)S(1)}, bf16[256,128]{1,0:T(8,128)(2,1)S(1)}, u32[]{:S(2)}, u32[]{:S(2)}) collective-permute-start(bf16[256,128]{1,0:T(8,128)(2,1)S(1)} %fusion.16), channel_id=1, source_target_pairs={{0,16},{8,24},{16,0},{24,8},{1,17},{9,25},{17,1},{25,9},{2,18},{10... | collective-permute-start | bytes 196616 | tf_op jit(solution)/shard_map/ppermute | solution.py:150
  95.8 5.2 %collective-permute-start.8 = (bf16[256,128]{1,0:T(8,128)(2,1)S(1)}, bf16[256,128]{1,0:T(8,128)(2,1)S(1)}, u32[]{:S(2)}, u32[]{:S(2)}) collective-permute-start(bf16[256,128]{1,0:T(8,128)(2,1)S(1)} %fusion.16), channel_id=1, source_target_pairs={{0,24},{8,16},{16,8},{24,0},{1,25},{9,17},{17,9},{25,1},{2,26},{10... | collective-permute-start | bytes 196616 | tf_op jit(solution)/shard_map/ppermute | solution.py:150
  111.4 27.5 %copy-start.3 = (s32[128,1]{0,1:T(1,128)S(1)}, s32[128,1]{0,1:T(1,128)}, u32[]{:S(2)}) copy-start(s32[128,1]{0,1:T(1,128)} %param.13) | copy-start | bytes 1540
  126.0 5.0 %collective-permute-start.10 = (f32[256,128]{1,0:T(8,128)S(1)}, f32[256,128]{1,0:T(8,128)S(1)}, u32[]{:S(2)}, u32[]{:S(2)}) collective-permute-start(f32[256,128]{1,0:T(8,128)S(1)} %get-tuple-element.11), channel_id=1, source_target_pairs={{0,16},{8,24},{16,0},{24,8},{1,17},{9,25},{17,1},{25,9},{2,18},{10... | collective-permute-start | bytes 393224 | tf_op jit(solution)/shard_map/ppermute | solution.py:145
  126.6 5.9 %collective-permute-start.11 = (f32[256,128]{1,0:T(8,128)S(1)}, f32[256,128]{1,0:T(8,128)S(1)}, u32[]{:S(2)}, u32[]{:S(2)}) collective-permute-start(f32[256,128]{1,0:T(8,128)S(1)} %get-tuple-element.10), channel_id=1, source_target_pairs={{0,24},{8,16},{16,8},{24,0},{1,25},{9,17},{17,9},{25,1},{2,26},{10... | collective-permute-start | bytes 393224 | tf_op jit(solution)/shard_map/ppermute | solution.py:145
  128.2 5.7 %collective-permute-start.9 = (f32[256,128]{1,0:T(8,128)S(1)}, f32[256,128]{1,0:T(8,128)S(1)}, u32[]{:S(2)}, u32[]{:S(2)}) collective-permute-start(f32[256,128]{1,0:T(8,128)S(1)} %get-tuple-element.9), channel_id=1, source_target_pairs={{0,8},{8,0},{16,24},{24,16},{1,9},{9,1},{17,25},{25,17},{2,10},{10... | collective-permute-start | bytes 393224 | tf_op jit(solution)/shard_map/ppermute | solution.py:145
  134.5 11.8 %all-to-all-start.1 = ((bf16[32,8,128]{2,1,0:T(8,128)(2,1)}), bf16[32,8,128]{2,1,0:T(8,128)(2,1)S(1)}, u32[]{:S(2)}, u32[]{:S(2)}) async-start(bf16[32,8,128]{2,1,0:T(8,128)(2,1)} %fusion.17), calls=%async_computation.1 | async-start | bytes 131072 | tf_op jit(solution)/shard_map/all_to_all | solution.py:158

commit v7 on v6

--- a/solution.py
+++ b/solution.py
@@ -81,6 +81,11 @@
     return [(i, i ^ k) for i in range(n)]
 
 
+def realign(block, k, n_sec):
+    order = np.bitwise_xor(np.arange(n_sec), k)
+    return block.reshape(n_sec, -1, block.shape[-1])[order].reshape(block.shape)
+
+
 def per_device(
     strain_rows,
     bands,
@@ -123,14 +128,16 @@
         [features, band_local.astype(jnp.bfloat16)[:, None]], axis=1
     )
     grp = jnp.dot(dispatch, packed, preferred_element_type=jnp.float32).astype(jnp.bfloat16)
-    grp = grp.reshape(n_dev, n_sec, slot_count, feat_width + 1)
-    xor_table = np.bitwise_xor.outer(np.arange(n_sec), np.arange(n_sec)).reshape(-1)
-    send = jnp.take(grp, jnp.asarray(xor_table, jnp.int32), axis=1)
-    send = send.reshape(n_dev, n_sec, n_sec, slot_count, feat_width + 1).transpose(1, 0, 2, 3, 4)
-    send = send.reshape(count_all, group_slots, feat_width + 1)
-    got = lax.all_to_all(send, ("sec", "dev"), split_axis=0, concat_axis=0, tiled=True)
-    got = got.reshape(count_all, n_sec, slot_count, feat_width + 1).transpose(1, 0, 2, 3)
-    got = got.reshape(n_sec, count_all * slot_count, feat_width + 1)
+    my_sec = lax.axis_index("sec")
+    sec_turn = jnp.bitwise_xor(jnp.arange(n_sec, dtype=jnp.int32), my_sec)
+    grp = grp.reshape(n_dev, group_slots, feat_width + 1)
+    got_dev = lax.all_to_all(grp, "dev", split_axis=0, concat_axis=0, tiled=True)
+    pieces = [got_dev] + [
+        lax.ppermute(got_dev, "sec", xor_pairs(n_sec, j)) for j in range(1, n_sec)
+    ]
+    got = jnp.stack(pieces).reshape(n_sec, n_dev, n_sec, slot_count, feat_width + 1)
+    got = jnp.take(got, sec_turn, axis=2).transpose(2, 0, 1, 3, 4)
+    got = got.reshape(n_sec, n_sec * n_dev * slot_count, feat_width + 1)
     rows = got[:, :, :feat_width]
     picks = band_picks(got[:, :, feat_width].astype(jnp.int32), parts)
 
@@ -142,12 +149,17 @@
         )
         own_sum = partial[0]
         for k in range(1, n_sec):
-            own_sum = own_sum + lax.ppermute(partial[k], "sec", xor_pairs(n_sec, k))
+            own_sum = own_sum + realign(
+                lax.ppermute(partial[k], "sec", xor_pairs(n_sec, k)), k, n_sec
+            )
         own_values = own_sum.astype(jnp.bfloat16)
         if segment_index + 1 < PASSES:
             values = jnp.stack(
                 [own_values]
-                + [lax.ppermute(own_values, "sec", xor_pairs(n_sec, k)) for k in range(1, n_sec)]
+                + [
+                    realign(lax.ppermute(own_values, "sec", xor_pairs(n_sec, k)), k, n_sec)
+                    for k in range(1, n_sec)
+                ]
             )
             rows = (
                 rows.astype(jnp.float32)
@@ -155,8 +167,9 @@
             ).astype(jnp.bfloat16)
         else:
             out_width = own_values.shape[1]
+            back = jnp.take(own_values.reshape(n_sec, -1, out_width), sec_turn, axis=0)
             back = lax.all_to_all(
-                own_values.reshape(count_all, slot_count, out_width),
+                back.reshape(count_all, slot_count, out_width),
                 ("sec", "dev"),
                 split_axis=0,
                 concat_axis=0,

time: 148 us -> 154 us (1.041)
  waiting for transfers between devices: 55.5 us -> 49.6 us
  local copies, waits for them, and re-layouts: 7.97 us -> 13.2 us
  starting transfers between devices: 26 us -> 31 us
    all_to_all x2, waiting for transfers between devices: 41.7 us -> 11.5 us  [the longest x1 7.35 us: per_device(): lax.all_to_all(back.reshape(count_all, slot_count, out_width), ('sec', 'd...]
    ppermute x6 -> x9, waiting for transfers between devices: 9.78 us -> 35.9 us  [the longest x3 27.9 us: per_device(): lax.ppermute(got_dev, 'sec', xor_pairs(n_sec, j))]
    ppermute x6 -> x9, starting transfers between devices: 7.11 us -> 12.8 us  [the longest x6 7.11 us: per_device(): lax.ppermute(partial[k], 'sec', xor_pairs(n_sec, k))]
    gather x2 -> x11, local copies, waits for them, and re-layouts: 1.48 us -> 6.96 us  [the longest x9 5.02 us: realign(): return block.reshape(n_sec, -1, block.shape[-1])[order].reshape(block.shape)]
    ppermute x3, waiting for transfers between devices: 4.05 us -> 2.15 us  [per_device(): lax.ppermute(own_values, 'sec', xor_pairs(n_sec, k))]
    select_n x0 -> x3, other arithmetic: none -> 1.89 us  [the longest x1 1.16 us: per_device(): got = jnp.take(got, sec_turn, axis=2).transpose(2, 0, 1, 3, 4)]
  transfers between devices with their start and end apart: 14 -> 17, of which waited for: 11 -> 12; matrix products, arithmetic and copies ran while one was open for 9% -> 12% of each run, Pallas kernels for 0% -> 0%
where the time goes in v7:
time: 154 us
  waiting for transfers between devices  49.6 us (32%)
  starting transfers between devices  31 us (20%)
  matrix products  30.2 us (20%)
  Pallas kernels  19 us (12%)
  local copies, waits for them, and re-layouts  13.2 us (9%)
  other arithmetic  10.3 us (7%)
    dot_general x2, matrix products, surrogate_tail(): return jnp.dot(middle, out_weight, preferred_element_type=jnp.float32)  29 us
    ppermute x3, waiting for transfers between devices, per_device(): lax.ppermute(got_dev, 'sec', xor_pairs(n_sec, j))  27.9 us
    pallas_call x2, Pallas kernels, first_hidden(): pl.pallas_call(first_kernel, grid=(n_blocks, row_steps, col_steps), in_sp...  19 us
    ppermute x6, waiting for transfers between devices, per_device(): lax.ppermute(partial[k], 'sec', xor_pairs(n_sec, k))  8.03 us
    all_to_all x1, waiting for transfers between devices, per_device(): lax.all_to_all(back.reshape(count_all, slot_count, out_width), ('sec', 'd...  7.35 us
    ppermute x6, starting transfers between devices, per_device(): lax.ppermute(partial[k], 'sec', xor_pairs(n_sec, k))  7.11 us
    ppermute x3, starting transfers between devices, per_device(): lax.ppermute(got_dev, 'sec', xor_pairs(n_sec, j))  5.71 us
    all_to_all x1, starting transfers between devices, per_device(): lax.all_to_all(grp, 'dev', split_axis=0, concat_axis=0, tiled=True)  5.34 us
  transfers between devices with their start and end apart: 17, of which 12 were waited for; matrix products, arithmetic and copies ran while one was open for 12% of the time, Pallas kernels for 0%

profile of v7, /device:TPU:0, one launch (start us, length us, event | category | flops | bytes accessed | tf_op | source)
XLA Modules:
  0.0 153.7 jit_solution(5153312504687711782)
XLA Ops:
  0.0 3.0 %collective-permute-start.3 = (bf16[128,4096]{1,0:T(8,128)(2,1)}, bf16[128,4096]{1,0:T(8,128)(2,1)S(1)}, u32[]{:S(2)}, u32[]{:S(2)}) collective-permute-start(bf16[128,4096]{1,0:T(8,128)(2,1)} %refs_0_.3), channel_id=1, source_target_pairs={{0,8},{8,0},{16,24},{24,16},{1,9},{9,1},{17,25},{25,17},{2,10},{10... | collective-permute-start | bytes 3145736 | tf_op jit(solution)/shard_map/ppermute | solution.py:110
  3.0 1.5 collective-permute-start.4
  7.6 1.6 %gather_fusion.1 = s32[128]{0:T(128)S(1)} fusion(s32[2048]{0:T(1024)} %param.28, s32[1024]{0:T(1024)S(1)} %pad_clamp_fusion.5), kind=kCustom, calls=%fused_computation.1 | custom fusion | bytes 1536 | tf_op jit(solution)/shard_map/jit(_take)/gather | solution.py:115
  11.8 5.3 %all-to-all-start = ((bf16[8,32,129]{2,1,0:T(8,128)(2,1)}), bf16[8,32,129]{2,1,0:T(8,128)(2,1)S(1)}, u32[]{:S(2)}, u32[]{:S(2)}) async-start(bf16[8,32,129]{2,1,0:T(8,128)(2,1)} %bitcast.4), calls=%async_computation | async-start | bytes 262144 | tf_op jit(solution)/shard_map/all_to_all | solution.py:134
  17.2 1.1 fusion.30
  19.7 4.2 %all-to-all-done = bf16[8,32,129]{2,1,0:T(8,128)(2,1)S(1)} async-done(((bf16[8,32,129]{2,1,0:T(8,128)(2,1)}), bf16[8,32,129]{2,1,0:T(8,128)(2,1)S(1)}, u32[]{:S(2)}, u32[]{:S(2)}) %all-to-all-start) | async-done | bytes 66080 | tf_op jit(solution)/shard_map/all_to_all | solution.py:134
  23.9 1.5 collective-permute-start
  25.4 1.5 collective-permute-start.1
  26.9 24.7 %collective-permute-done = bf16[8,32,129]{2,1,0:T(8,128)(2,1)S(1)} collective-permute-done((bf16[8,32,129]{2,1,0:T(8,128)(2,1)S(1)}, bf16[8,32,129]{2,1,0:T(8,128)(2,1)S(1)}, u32[]{:S(2)}, u32[]{:S(2)}) %collective-permute-start) | collective-permute-done | bytes 66080 | tf_op jit(solution)/shard_map/ppermute | solution.py:136
  51.7 2.7 %collective-permute-start.2 = (bf16[8,32,129]{2,1,0:T(8,128)(2,1)S(1)}, bf16[8,32,129]{2,1,0:T(8,128)(2,1)S(1)}, u32[]{:S(2)}, u32[]{:S(2)}) collective-permute-start(bf16[8,32,129]{2,1,0:T(8,128)(2,1)S(1)} %all-to-all-done), channel_id=1, source_target_pairs={{0,24},{8,16},{16,8},{24,0},{1,25},{9,17},{17,9},{25,1},{2,26},{10... | collective-permute-start | bytes 198152 | tf_op jit(solution)/shard_map/ppermute | solution.py:136
  54.4 3.2 %collective-permute-done.2 = bf16[8,32,129]{2,1,0:T(8,128)(2,1)S(1)} collective-permute-done((bf16[8,32,129]{2,1,0:T(8,128)(2,1)S(1)}, bf16[8,32,129]{2,1,0:T(8,128)(2,1)S(1)}, u32[]{:S(2)}, u32[]{:S(2)}) %collective-permute-start.2) | collective-permute-done | bytes 66080 | tf_op jit(solution)/shard_map/ppermute | solution.py:136
  57.7 1.4 gather_fusion.2
  59.1 1.2 broadcast_select_fusion
  62.2 1.0 copy-done.1
  63.5 9.5 %shard_map.253 = bf16[1024,4096]{1,0:T(8,128)(2,1)} custom-call(bf16[4,256,128]{2,1,0:T(8,128)(2,1)} %slice.76.x_ref, bf16[128,4096]{1,0:T(8,128)(2,1)} %refs_0_.3, bf16[128,4096]{1,0:T(8,128)(2,1)} %copy-done.1, bf16[128,4096]{1,0:T(8,128)(2,1)} %copy-done.2, bf16[128,4096]{1,0:T(8,128)(2,1)} %collective-permute-done.5.refs_3_, ...), custom_call_target="tpu_custom_call" | custom-call | flops 1476395008 | bytes 12582912 | tf_op jit(solution)/shard_map/pallas_call | solution.py:53
  73.0 14.5 %fusion = f32[1024,128]{1,0:T(8,128)S(1)} fusion(bf16[1024,128]{1,0:T(8,128)(2,1)S(1)} %copy-done.6, bf16[1024,4096]{1,0:T(8,128)(2,1)} %shard_map.253, bf16[4096,1024]{1,0:T(8,128)(2,1)} %param.32), kind=kOutput, calls=%fused_computation.16 | convolution fusion | flops 8863612928 | bytes 17563648 | tf_op jit(solution)/shard_map/dot_general | solution.py:77
  87.6 1.8 %collective-permute-start.6 = (f32[256,128]{1,0:T(8,128)S(1)}, f32[256,128]{1,0:T(8,128)S(1)}, u32[]{:S(2)}, u32[]{:S(2)}) collective-permute-start(f32[256,128]{1,0:T(8,128)S(1)} %get-tuple-element.13), channel_id=1, source_target_pairs={{0,8},{8,0},{16,24},{24,16},{1,9},{9,1},{17,25},{25,17},{2,10},{10... | collective-permute-start | bytes 393224 | tf_op jit(solution)/shard_map/ppermute | solution.py:153
  89.4 1.5 collective-permute-start.7
  91.2 2.5 %collective-permute-done.6 = f32[256,128]{1,0:T(8,128)S(1)} collective-permute-done((f32[256,128]{1,0:T(8,128)S(1)}, f32[256,128]{1,0:T(8,128)S(1)}, u32[]{:S(2)}, u32[]{:S(2)}) %collective-permute-start.6) | collective-permute-done | bytes 131104 | tf_op jit(solution)/shard_map/ppermute | solution.py:153
  95.3 1.5 collective-permute-done.8
  98.0 1.1 collective-permute-start.10
  99.1 1.9 %collective-permute-start.11 = (bf16[256,128]{1,0:T(8,128)(2,1)S(1)}, bf16[256,128]{1,0:T(8,128)(2,1)S(1)}, u32[]{:S(2)}, u32[]{:S(2)}) collective-permute-start(bf16[256,128]{1,0:T(8,128)(2,1)S(1)} %fusion.13), channel_id=1, source_target_pairs={{0,24},{8,16},{16,8},{24,0},{1,25},{9,17},{17,9},{25,1},{2,26},{10... | collective-permute-start | bytes 196616 | tf_op jit(solution)/shard_map/ppermute | solution.py:160
  102.9 1.4 collective-permute-done.11
  105.7 9.5 %shard_map.254 = bf16[1024,4096]{1,0:T(8,128)(2,1)} custom-call(bf16[4,256,128]{2,1,0:T(8,128)(2,1)} %fusion.2.x_ref, bf16[128,4096]{1,0:T(8,128)(2,1)} %refs_0_.3, bf16[128,4096]{1,0:T(8,128)(2,1)} %copy-done.1, bf16[128,4096]{1,0:T(8,128)(2,1)} %copy-done.2, bf16[128,4096]{1,0:T(8,128)(2,1)} %collective-permute-done.5.refs_3_, ...), custom_call_target="tpu_custom_call" | custom-call | flops 1476395008 | bytes 12582912 | tf_op jit(solution)/shard_map/pallas_call | solution.py:53
  115.2 14.5 %fusion.1 = f32[1024,128]{1,0:T(8,128)S(1)} fusion(bf16[1024,128]{1,0:T(8,128)(2,1)S(1)} %copy-done.6, bf16[1024,4096]{1,0:T(8,128)(2,1)} %shard_map.254, bf16[4096,1024]{1,0:T(8,128)(2,1)} %param.32), kind=kOutput, calls=%fused_computation.17 | convolution fusion | flops 8863612928 | bytes 17563648 | tf_op jit(solution)/shard_map/dot_general | solution.py:77
  129.8 1.0 collective-permute-start.13
  130.8 1.5 collective-permute-start.12
  132.3 1.0 collective-permute-start.14
  133.5 1.3 collective-permute-done.13
  136.4 1.8 %collective-permute-done.14 = f32[256,128]{1,0:T(8,128)S(1)} collective-permute-done((f32[256,128]{1,0:T(8,128)S(1)}, f32[256,128]{1,0:T(8,128)S(1)}, u32[]{:S(2)}, u32[]{:S(2)}) %collective-permute-start.14) | collective-permute-done | bytes 131104 | tf_op jit(solution)/shard_map/ppermute | solution.py:153
  140.1 4.8 %all-to-all-start.1 = ((bf16[32,8,128]{2,1,0:T(8,128)(2,1)}), bf16[32,8,128]{2,1,0:T(8,128)(2,1)S(1)}, u32[]{:S(2)}, u32[]{:S(2)}) async-start(bf16[32,8,128]{2,1,0:T(8,128)(2,1)} %broadcast_select_fusion.1), calls=%async_computation.1 | async-start | bytes 131072 | tf_op jit(solution)/shard_map/all_to_all | solution.py:171
  144.9 7.3 %all-to-all-done.1 = bf16[32,8,128]{2,1,0:T(8,128)(2,1)S(1)} async-done(((bf16[32,8,128]{2,1,0:T(8,128)(2,1)}), bf16[32,8,128]{2,1,0:T(8,128)(2,1)S(1)}, u32[]{:S(2)}, u32[]{:S(2)}) %all-to-all-start.1) | async-done | bytes 65568 | tf_op jit(solution)/shard_map/all_to_all | solution.py:171
  (73 shorter events, 21.0 us)
Async XLA Ops:
  0.0 9.9 %copy-start = (bf16[2048,128]{1,0:T(8,128)(2,1)S(1)}, bf16[2048,128]{1,0:T(8,128)(2,1)}, u32[]{:S(2)}) copy-start(bf16[2048,128]{1,0:T(8,128)(2,1)} %param.27) | copy-start | bytes 1572868
  0.0 62.2 %collective-permute-start.3 = (bf16[128,4096]{1,0:T(8,128)(2,1)}, bf16[128,4096]{1,0:T(8,128)(2,1)S(1)}, u32[]{:S(2)}, u32[]{:S(2)}) collective-permute-start(bf16[128,4096]{1,0:T(8,128)(2,1)} %refs_0_.3), channel_id=1, source_target_pairs={{0,8},{8,0},{16,24},{24,16},{1,9},{9,1},{17,25},{25,17},{2,10},{10... | collective-permute-start | bytes 3145736 | tf_op jit(solution)/shard_map/ppermute | solution.py:110
  3.0 59.2 %collective-permute-start.4 = (bf16[128,4096]{1,0:T(8,128)(2,1)}, bf16[128,4096]{1,0:T(8,128)(2,1)S(1)}, u32[]{:S(2)}, u32[]{:S(2)}) collective-permute-start(bf16[128,4096]{1,0:T(8,128)(2,1)} %refs_0_.3), channel_id=1, source_target_pairs={{0,16},{8,24},{16,0},{24,8},{1,17},{9,25},{17,1},{25,9},{2,18},{10... | collective-permute-start | bytes 3145736 | tf_op jit(solution)/shard_map/ppermute | solution.py:110
  4.5 57.7 %collective-permute-start.5 = (bf16[128,4096]{1,0:T(8,128)(2,1)}, bf16[128,4096]{1,0:T(8,128)(2,1)}, u32[]{:S(2)}, u32[]{:S(2)}) collective-permute-start(bf16[128,4096]{1,0:T(8,128)(2,1)} %refs_0_.3), channel_id=1, source_target_pairs={{0,24},{8,16},{16,8},{24,0},{1,25},{9,17},{17,9},{25,1},{2,26},{10... | collective-permute-start | bytes 3145736 | tf_op jit(solution)/shard_map/ppermute | solution.py:110
  11.8 12.1 %all-to-all-start = ((bf16[8,32,129]{2,1,0:T(8,128)(2,1)}), bf16[8,32,129]{2,1,0:T(8,128)(2,1)S(1)}, u32[]{:S(2)}, u32[]{:S(2)}) async-start(bf16[8,32,129]{2,1,0:T(8,128)(2,1)} %bitcast.4), calls=%async_computation | async-start | bytes 262144 | tf_op jit(solution)/shard_map/all_to_all | solution.py:134
  23.9 27.8 %collective-permute-start = (bf16[8,32,129]{2,1,0:T(8,128)(2,1)S(1)}, bf16[8,32,129]{2,1,0:T(8,128)(2,1)S(1)}, u32[]{:S(2)}, u32[]{:S(2)}) collective-permute-start(bf16[8,32,129]{2,1,0:T(8,128)(2,1)S(1)} %all-to-all-done), channel_id=1, source_target_pairs={{0,8},{8,0},{16,24},{24,16},{1,9},{9,1},{17,25},{25,17},{2,10},{10... | collective-permute-start | bytes 198152 | tf_op jit(solution)/shard_map/ppermute | solution.py:136
  25.4 29.0 %collective-permute-start.1 = (bf16[8,32,129]{2,1,0:T(8,128)(2,1)S(1)}, bf16[8,32,129]{2,1,0:T(8,128)(2,1)S(1)}, u32[]{:S(2)}, u32[]{:S(2)}) collective-permute-start(bf16[8,32,129]{2,1,0:T(8,128)(2,1)S(1)} %all-to-all-done), channel_id=1, source_target_pairs={{0,16},{8,24},{16,0},{24,8},{1,17},{9,25},{17,1},{25,9},{2,18},{10... | collective-permute-start | bytes 198152 | tf_op jit(solution)/shard_map/ppermute | solution.py:136
  51.7 5.9 %collective-permute-start.2 = (bf16[8,32,129]{2,1,0:T(8,128)(2,1)S(1)}, bf16[8,32,129]{2,1,0:T(8,128)(2,1)S(1)}, u32[]{:S(2)}, u32[]{:S(2)}) collective-permute-start(bf16[8,32,129]{2,1,0:T(8,128)(2,1)S(1)} %all-to-all-done), channel_id=1, source_target_pairs={{0,24},{8,16},{16,8},{24,0},{1,25},{9,17},{17,9},{25,1},{2,26},{10... | collective-permute-start | bytes 198152 | tf_op jit(solution)/shard_map/ppermute | solution.py:136
  57.7 15.3 %copy-start.6 = (bf16[1024,128]{1,0:T(8,128)(2,1)S(1)}, bf16[1024,128]{1,0:T(8,128)(2,1)}, u32[]{:S(2)}) copy-start(bf16[1024,128]{1,0:T(8,128)(2,1)} %param.33) | copy-start | bytes 786436
  62.2 1.0 copy-start.1
  62.2 1.3 copy-start.2
  73.0 18.1 %copy-start.5 = (s32[4]{0:T(128)S(1)}, s32[4]{0:T(128)}, u32[]{:S(2)}) copy-start(s32[4]{0:T(128)} %constant.146) | copy-start | bytes 52
  73.0 18.2 %copy-start.4 = (s32[4]{0:T(128)S(1)}, s32[4]{0:T(128)}, u32[]{:S(2)}) copy-start(s32[4]{0:T(128)} %constant.147) | copy-start | bytes 52
  73.0 31.8 %copy-start.7 = (bf16[128,128]{1,0:T(8,128)(2,1)S(1)}, bf16[128,128]{1,0:T(8,128)(2,1)}, u32[]{:S(2)}) copy-start(bf16[128,128]{1,0:T(8,128)(2,1)} %param.35) | copy-start | bytes 98308
  87.6 6.1 %collective-permute-start.6 = (f32[256,128]{1,0:T(8,128)S(1)}, f32[256,128]{1,0:T(8,128)S(1)}, u32[]{:S(2)}, u32[]{:S(2)}) collective-permute-start(f32[256,128]{1,0:T(8,128)S(1)} %get-tuple-element.13), channel_id=1, source_target_pairs={{0,8},{8,0},{16,24},{24,16},{1,9},{9,1},{17,25},{25,17},{2,10},{10... | collective-permute-start | bytes 393224 | tf_op jit(solution)/shard_map/ppermute | solution.py:153
  89.4 5.4 %collective-permute-start.7 = (f32[256,128]{1,0:T(8,128)S(1)}, f32[256,128]{1,0:T(8,128)S(1)}, u32[]{:S(2)}, u32[]{:S(2)}) collective-permute-start(f32[256,128]{1,0:T(8,128)S(1)} %get-tuple-element.15), channel_id=1, source_target_pairs={{0,16},{8,24},{16,0},{24,8},{1,17},{9,25},{17,1},{25,9},{2,18},{10... | collective-permute-start | bytes 393224 | tf_op jit(solution)/shard_map/ppermute | solution.py:153
  90.9 5.9 %collective-permute-start.8 = (f32[256,128]{1,0:T(8,128)S(1)}, f32[256,128]{1,0:T(8,128)S(1)}, u32[]{:S(2)}, u32[]{:S(2)}) collective-permute-start(f32[256,128]{1,0:T(8,128)S(1)} %get-tuple-element.14), channel_id=1, source_target_pairs={{0,24},{8,16},{16,8},{24,0},{1,25},{9,17},{17,9},{25,1},{2,26},{10... | collective-permute-start | bytes 393224 | tf_op jit(solution)/shard_map/ppermute | solution.py:153
  97.4 4.3 %collective-permute-start.9 = (bf16[256,128]{1,0:T(8,128)(2,1)S(1)}, bf16[256,128]{1,0:T(8,128)(2,1)S(1)}, u32[]{:S(2)}, u32[]{:S(2)}) collective-permute-start(bf16[256,128]{1,0:T(8,128)(2,1)S(1)} %fusion.13), channel_id=1, source_target_pairs={{0,8},{8,0},{16,24},{24,16},{1,9},{9,1},{17,25},{25,17},{2,10},{10... | collective-permute-start | bytes 196616 | tf_op jit(solution)/shard_map/ppermute | solution.py:160
  98.0 4.3 %collective-permute-start.10 = (bf16[256,128]{1,0:T(8,128)(2,1)S(1)}, bf16[256,128]{1,0:T(8,128)(2,1)S(1)}, u32[]{:S(2)}, u32[]{:S(2)}) collective-permute-start(bf16[256,128]{1,0:T(8,128)(2,1)S(1)} %fusion.13), channel_id=1, source_target_pairs={{0,16},{8,24},{16,0},{24,8},{1,17},{9,25},{17,1},{25,9},{2,18},{10... | collective-permute-start | bytes 196616 | tf_op jit(solution)/shard_map/ppermute | solution.py:160
  99.1 5.2 %collective-permute-start.11 = (bf16[256,128]{1,0:T(8,128)(2,1)S(1)}, bf16[256,128]{1,0:T(8,128)(2,1)S(1)}, u32[]{:S(2)}, u32[]{:S(2)}) collective-permute-start(bf16[256,128]{1,0:T(8,128)(2,1)S(1)} %fusion.13), channel_id=1, source_target_pairs={{0,24},{8,16},{16,8},{24,0},{1,25},{9,17},{17,9},{25,1},{2,26},{10... | collective-permute-start | bytes 196616 | tf_op jit(solution)/shard_map/ppermute | solution.py:160
  115.2 29.6 %copy-start.3 = (s32[128,1]{0,1:T(1,128)S(1)}, s32[128,1]{0,1:T(1,128)}, u32[]{:S(2)}) copy-start(s32[128,1]{0,1:T(1,128)} %param.30) | copy-start | bytes 1540
  129.8 5.0 %collective-permute-start.13 = (f32[256,128]{1,0:T(8,128)S(1)}, f32[256,128]{1,0:T(8,128)S(1)}, u32[]{:S(2)}, u32[]{:S(2)}) collective-permute-start(f32[256,128]{1,0:T(8,128)S(1)} %get-tuple-element.11), channel_id=1, source_target_pairs={{0,16},{8,24},{16,0},{24,8},{1,17},{9,25},{17,1},{25,9},{2,18},{10... | collective-permute-start | bytes 393224 | tf_op jit(solution)/shard_map/ppermute | solution.py:153
  130.8 5.0 %collective-permute-start.12 = (f32[256,128]{1,0:T(8,128)S(1)}, f32[256,128]{1,0:T(8,128)S(1)}, u32[]{:S(2)}, u32[]{:S(2)}) collective-permute-start(f32[256,128]{1,0:T(8,128)S(1)} %get-tuple-element.9), channel_id=1, source_target_pairs={{0,8},{8,0},{16,24},{24,16},{1,9},{9,1},{17,25},{25,17},{2,10},{10... | collective-permute-start | bytes 393224 | tf_op jit(solution)/shard_map/ppermute | solution.py:153
  132.3 5.9 %collective-permute-start.14 = (f32[256,128]{1,0:T(8,128)S(1)}, f32[256,128]{1,0:T(8,128)S(1)}, u32[]{:S(2)}, u32[]{:S(2)}) collective-permute-start(f32[256,128]{1,0:T(8,128)S(1)} %get-tuple-element.10), channel_id=1, source_target_pairs={{0,24},{8,16},{16,8},{24,0},{1,25},{9,17},{17,9},{25,1},{2,26},{10... | collective-permute-start | bytes 393224 | tf_op jit(solution)/shard_map/ppermute | solution.py:153
  140.1 12.2 %all-to-all-start.1 = ((bf16[32,8,128]{2,1,0:T(8,128)(2,1)}), bf16[32,8,128]{2,1,0:T(8,128)(2,1)S(1)}, u32[]{:S(2)}, u32[]{:S(2)}) async-start(bf16[32,8,128]{2,1,0:T(8,128)(2,1)} %broadcast_select_fusion.1), calls=%async_computation.1 | async-start | bytes 131072 | tf_op jit(solution)/shard_map/all_to_all | solution.py:171

commit v8 on v6

--- a/solution.py
+++ b/solution.py
@@ -1,8 +1,11 @@
+import functools
+
 import jax
 import jax.numpy as jnp
 import numpy as np
 from jax import lax
 from jax.experimental import pallas as pl
+from jax.experimental.pallas import tpu as pltpu
 from jax.sharding import PartitionSpec as P
 
 PASSES = 2
@@ -22,12 +25,13 @@
     return (band_values[..., None] == level_ids).astype(jnp.bfloat16)
 
 
-def first_kernel(x_ref, *refs):
+def first_kernel(live_tiles, x_ref, *refs):
     w_refs, (p_ref, s_ref, o_ref) = refs[:-3], refs[-3:]
     block = pl.program_id(0)
+    step = pl.program_id(1)
     for k, w_ref in enumerate(w_refs):
 
-        @pl.when(block == k)
+        @pl.when((block == k) & (step < live_tiles[k]))
         def _():
             mixed = jnp.dot(x_ref[...], w_ref[...], preferred_element_type=jnp.float32)
             scale = jnp.dot(p_ref[...], s_ref[...], preferred_element_type=jnp.float32)
@@ -35,46 +39,89 @@
             o_ref[...] = (v * jax.nn.sigmoid(v)).astype(o_ref.dtype)
 
 
-def weight_spec(k, feat, col_tile, col_steps):
-    def index(s, i, j):
-        return (0, jnp.where(s == k, j, jnp.where(s < k, 0, col_steps - 1)))
-
-    return pl.BlockSpec((feat, col_tile), index)
-
-
-def first_hidden(rows, weights, picks, parts, interpret=False):
+def last_live(step, live):
+    return jnp.minimum(step, jnp.maximum(live - 1, 0))
+
+
+ROW_TILE = 128
+
+
+def first_hidden(rows, weights, picks, parts, live_tiles):
     n_blocks, n_rows, feat = rows.shape
     hid = weights[0].shape[1]
     n_pick = picks.shape[2]
-    row_tile = min(n_rows, 256)
-    col_tile = min(hid, 4096)
+    row_tile = min(n_rows, ROW_TILE)
     row_steps = n_rows // row_tile
-    col_steps = hid // col_tile
+
+    def weight_spec(k):
+        return pl.BlockSpec((feat, hid), lambda s, i, j, live: (0, 0))
+
+    def row_spec(width):
+        return pl.BlockSpec(
+            (None, row_tile, width), lambda s, i, j, live: (s, last_live(i, live[s]), 0)
+        )
+
     return pl.pallas_call(
         first_kernel,
-        grid=(n_blocks, row_steps, col_steps),
-        in_specs=[pl.BlockSpec((None, row_tile, feat), lambda s, i, j: (s, i, 0))]
-        + [weight_spec(k, feat, col_tile, col_steps) for k in range(n_blocks)]
-        + [
-            pl.BlockSpec((None, row_tile, n_pick), lambda s, i, j: (s, i, 0)),
-            pl.BlockSpec((n_pick, col_tile), lambda s, i, j: (0, j)),
-        ],
-        out_specs=pl.BlockSpec((row_tile, col_tile), lambda s, i, j: (s * row_steps + i, j)),
+        grid_spec=pltpu.PrefetchScalarGridSpec(
+            num_scalar_prefetch=1,
+            grid=(n_blocks, row_steps, 1),
+            in_specs=[row_spec(feat)]
+            + [weight_spec(k) for k in range(n_blocks)]
+            + [row_spec(n_pick), pl.BlockSpec((n_pick, hid), lambda s, i, j, live: (0, 0))],
+            out_specs=pl.BlockSpec(
+                (row_tile, hid), lambda s, i, j, live: (s * row_steps + last_live(i, live[s]), 0)
+            ),
+        ),
         out_shape=jax.ShapeDtypeStruct((n_blocks * n_rows, hid), jnp.bfloat16),
         cost_estimate=pl.CostEstimate(
             flops=2 * n_blocks * n_rows * hid * (feat + n_pick),
             transcendentals=n_blocks * n_rows * hid,
-            bytes_accessed=2 * (n_blocks * n_rows * hid + n_blocks * feat * hid * row_steps),
-        ),
-        interpret=interpret,
-    )(rows, *weights, picks, parts)
-
-
-def surrogate_tail(hidden_block, middle_weight, out_weight):
-    middle = jax.nn.silu(
-        jnp.dot(hidden_block, middle_weight, preferred_element_type=jnp.float32)
-    ).astype(jnp.bfloat16)
-    return jnp.dot(middle, out_weight, preferred_element_type=jnp.float32)
+            bytes_accessed=2 * (n_blocks * n_rows * hid + n_blocks * feat * hid),
+        ),
+    )(live_tiles, rows, *weights, picks, parts)
+
+
+def tail_kernel(live_tiles, h_ref, m_ref, w_ref, o_ref, *, row_steps):
+    tile = pl.program_id(0)
+
+    @pl.when(tile % row_steps < live_tiles[tile // row_steps])
+    def _():
+        middle = jnp.dot(h_ref[...], m_ref[...], preferred_element_type=jnp.float32)
+        middle = (middle * jax.nn.sigmoid(middle)).astype(jnp.bfloat16)
+        o_ref[...] = jnp.dot(middle, w_ref[...], preferred_element_type=jnp.float32)
+
+
+def surrogate_tail(hidden, middle_weight, out_weight, live_tiles, n_blocks):
+    n_all, hid = hidden.shape
+    mid = middle_weight.shape[1]
+    out_width = out_weight.shape[1]
+    row_tile = min(n_all // n_blocks, ROW_TILE)
+    row_steps = n_all // n_blocks // row_tile
+
+    def tile_index(t, live):
+        return (t // row_steps) * row_steps + last_live(t % row_steps, live[t // row_steps])
+
+    return pl.pallas_call(
+        functools.partial(tail_kernel, row_steps=row_steps),
+        grid_spec=pltpu.PrefetchScalarGridSpec(
+            num_scalar_prefetch=1,
+            grid=(n_blocks * row_steps,),
+            in_specs=[
+                pl.BlockSpec((row_tile, hid), lambda t, live: (tile_index(t, live), 0)),
+                pl.BlockSpec((hid, mid), lambda t, live: (0, 0)),
+                pl.BlockSpec((mid, out_width), lambda t, live: (0, 0)),
+            ],
+            out_specs=pl.BlockSpec((row_tile, out_width), lambda t, live: (tile_index(t, live), 0)),
+        ),
+        out_shape=jax.ShapeDtypeStruct((n_all, out_width), jnp.float32),
+        compiler_params=pltpu.CompilerParams(vmem_limit_bytes=48 * 1024 * 1024),
+        cost_estimate=pl.CostEstimate(
+            flops=2 * n_all * mid * (hid + out_width),
+            transcendentals=n_all * mid,
+            bytes_accessed=2 * (n_all * hid + hid * mid + mid * out_width) + 4 * n_all * out_width,
+        ),
+    )(live_tiles, hidden, middle_weight, out_weight)
 
 
 def xor_pairs(n, k):
@@ -120,7 +167,7 @@
         jnp.arange(n_dev * group_slots, dtype=jnp.int32)[:, None] == target[None, :]
     ).astype(jnp.bfloat16)
     packed = jnp.concatenate(
-        [features, band_local.astype(jnp.bfloat16)[:, None]], axis=1
+        [features, (band_local + 1).astype(jnp.bfloat16)[:, None]], axis=1
     )
     grp = jnp.dot(dispatch, packed, preferred_element_type=jnp.float32).astype(jnp.bfloat16)
     grp = grp.reshape(n_dev, n_sec, slot_count, feat_width + 1)
@@ -131,13 +178,30 @@
     got = lax.all_to_all(send, ("sec", "dev"), split_axis=0, concat_axis=0, tiled=True)
     got = got.reshape(count_all, n_sec, slot_count, feat_width + 1).transpose(1, 0, 2, 3)
     got = got.reshape(n_sec, count_all * slot_count, feat_width + 1)
+    flag = got[:, :, feat_width].astype(jnp.int32)
+    live = flag > 0
+    n_rows = got.shape[1]
+    live_count = jnp.sum(live.astype(jnp.int32), axis=1)
+    place = jnp.where(
+        live,
+        jnp.cumsum(live.astype(jnp.int32), axis=1) - 1,
+        live_count[:, None] + jnp.cumsum((~live).astype(jnp.int32), axis=1) - 1,
+    )
+    moves = (place[:, None, :] == jnp.arange(n_rows, dtype=jnp.int32)[None, :, None]).astype(
+        jnp.bfloat16
+    )
+    got = jnp.einsum("kpr,krf->kpf", moves, got, preferred_element_type=jnp.float32).astype(
+        jnp.bfloat16
+    )
+    row_tile = min(n_rows, ROW_TILE)
+    live_tiles = (live_count + row_tile - 1) // row_tile
     rows = got[:, :, :feat_width]
-    picks = band_picks(got[:, :, feat_width].astype(jnp.int32), parts)
+    picks = band_picks(got[:, :, feat_width].astype(jnp.int32) - 1, parts)
 
     result = None
     for segment_index in range(PASSES):
-        hidden = first_hidden(rows, block_first, picks, parts)
-        partial = surrogate_tail(hidden, middle_weight, out_weight).reshape(
+        hidden = first_hidden(rows, block_first, picks, parts, live_tiles)
+        partial = surrogate_tail(hidden, middle_weight, out_weight, live_tiles, n_sec).reshape(
             n_sec, rows.shape[1], -1
         )
         own_sum = partial[0]
@@ -155,6 +219,7 @@
             ).astype(jnp.bfloat16)
         else:
             out_width = own_values.shape[1]
+            own_values = jnp.take(own_values, place[0], axis=0)
             back = lax.all_to_all(
                 own_values.reshape(count_all, slot_count, out_width),
                 ("sec", "dev"),

time: 148 us -> 159 us (1.074)
  Pallas kernels: 19 us -> 47.9 us
  matrix products: 30.2 us -> 1.47 us
  other arithmetic: 8.91 us -> 12.4 us
  starting transfers between devices: 26 us -> 29.3 us
  local copies, waits for them, and re-layouts: 7.97 us -> 10.3 us
    pallas_call x2 -> x4, Pallas kernels: 19 us -> 47.9 us  [the longest x2 28.1 us: surrogate_tail(): pl.pallas_call(functools.partial(tail_kernel, row_steps=row_steps), grid_...]
    dot_general x2 -> x1, matrix products: 29 us -> 0.32 us  [per_device(): jnp.einsum('kpr,krf->kpf', moves, got, preferred_element_type=jnp.float32)]
    another operation x0 -> x4, other arithmetic: none -> 2.51 us
    all_to_all x1, starting transfers between devices: 4.41 us -> 6.66 us  [per_device(): lax.all_to_all(own_values.reshape(count_all, slot_count, out_width), ('se...]
  transfers between devices with their start and end apart: 14 -> 14, of which waited for: 11 -> 11; matrix products, arithmetic and copies ran while one was open for 9% -> 12% of each run, Pallas kernels for 0% -> 0%
where the time goes in v8:
time: 159 us; the launch traced here: 158 us
  waiting for transfers between devices  55.9 us (35%)
  Pallas kernels  47.9 us (30%)
  starting transfers between devices  29.3 us (18%)
  other arithmetic  12.4 us (8%)
  local copies, waits for them, and re-layouts  10.3 us (6%)
    all_to_all x1, waiting for transfers between devices, per_device(): lax.all_to_all(send, ('sec', 'dev'), split_axis=0, concat_axis=0, tiled=T...  34.4 us
    pallas_call x2, Pallas kernels, surrogate_tail(): pl.pallas_call(functools.partial(tail_kernel, row_steps=row_steps), grid_...  28.1 us
    pallas_call x2, Pallas kernels, first_hidden(): pl.pallas_call(first_kernel, grid_spec=pltpu.PrefetchScalarGridSpec(num_s...  19.9 us
    ppermute x6, waiting for transfers between devices, per_device(): own_sum = own_sum + lax.ppermute(partial[k], 'sec', xor_pairs(n_sec, k))  10.2 us
    ppermute x6, starting transfers between devices, per_device(): own_sum = own_sum + lax.ppermute(partial[k], 'sec', xor_pairs(n_sec, k))  8.3 us
    all_to_all x1, waiting for transfers between devices, per_device(): lax.all_to_all(own_values.reshape(count_all, slot_count, out_width), ('se...  7.35 us
    all_to_all x1, starting transfers between devices, per_device(): lax.all_to_all(own_values.reshape(count_all, slot_count, out_width), ('se...  6.66 us
    all_to_all x1, starting transfers between devices, per_device(): lax.all_to_all(send, ('sec', 'dev'), split_axis=0, concat_axis=0, tiled=T...  6.31 us
  transfers between devices with their start and end apart: 14, of which 11 were waited for; matrix products, arithmetic and copies ran while one was open for 12% of the time, Pallas kernels for 0%

profile of v8, /device:TPU:0, one launch (start us, length us, event | category | flops | bytes accessed | tf_op | source)
XLA Modules:
  0.0 157.6 jit_solution(11653336501488545484)
XLA Ops:
  0.0 3.0 %collective-permute-start = (bf16[128,4096]{1,0:T(8,128)(2,1)}, bf16[128,4096]{1,0:T(8,128)(2,1)S(1)}, u32[]{:S(2)}, u32[]{:S(2)}) collective-permute-start(bf16[128,4096]{1,0:T(8,128)(2,1)} %refs_0_.3), channel_id=1, source_target_pairs={{0,8},{8,0},{16,24},{24,16},{1,9},{9,1},{17,25},{25,17},{2,10},{10... | collective-permute-start | bytes 3145736 | tf_op jit(solution)/shard_map/ppermute | solution.py:152
  3.0 1.5 collective-permute-start.1
  7.6 1.6 %gather_fusion.1 = s32[128]{0:T(128)S(1)} fusion(s32[2048]{0:T(1024)} %param.11, s32[1024]{0:T(1024)S(1)} %pad_clamp_fusion.3), kind=kCustom, calls=%fused_computation.1 | custom fusion | bytes 1536 | tf_op jit(solution)/shard_map/jit(_take)/gather | solution.py:157
  13.3 6.3 %all-to-all-start = ((bf16[32,32,129]{2,1,0:T(8,128)(2,1)}), bf16[32,32,129]{2,1,0:T(8,128)(2,1)S(1)}, u32[]{:S(2)}, u32[]{:S(2)}) async-start(bf16[32,32,129]{2,1,0:T(8,128)(2,1)} %bitcast.65), calls=%async_computation | async-start | bytes 1048576 | tf_op jit(solution)/shard_map/all_to_all | solution.py:178
  19.6 1.1 fusion.31
  21.5 34.4 %all-to-all-done = bf16[32,32,129]{2,1,0:T(8,128)(2,1)S(1)} async-done(((bf16[32,32,129]{2,1,0:T(8,128)(2,1)}), bf16[32,32,129]{2,1,0:T(8,128)(2,1)S(1)}, u32[]{:S(2)}, u32[]{:S(2)}) %all-to-all-start) | async-done | bytes 264224 | tf_op jit(solution)/shard_map/all_to_all | solution.py:178
  56.7 1.1 copy.56
  57.9 1.2 reduce-window.16
  59.5 1.2 reduce-window.14
  63.1 0.9 compare_convert_fusion.refs_4_
  64.0 0.9 copy-done.4
  65.3 9.9 %shard_map.100.h_ref = bf16[1024,4096]{1,0:T(8,128)(2,1)} custom-call(s32[4]{0:T(128)} %and_select_fusion.1.live_tiles, bf16[4,256,128]{2,1,0:T(8,128)(2,1)} %slice.86.x_ref, bf16[128,4096]{1,0:T(8,128)(2,1)} %refs_0_.3, bf16[128,4096]{1,0:T(8,128)(2,1)} %copy-done.4, bf16[128,4096]{1,0:T(8,128)(2,1)} %copy-done.5, ...), custom_call_target="tpu_custom_call" | custom-call | flops 1476395008 | bytes 12582912 | tf_op jit(solution)/shard_map/pallas_call | solution.py:64
  75.3 14.0 %shard_map.101 = f32[1024,128]{1,0:T(8,128)S(1)} custom-call(s32[4]{0:T(128)S(1)} %copy-done.1, bf16[1024,4096]{1,0:T(8,128)(2,1)} %shard_map.100.h_ref, bf16[4096,1024]{1,0:T(8,128)(2,1)} %m_ref.3, bf16[1024,128]{1,0:T(8,128)(2,1)S(1)} %copy-done.3), custom_call_target="tpu_custom_call" | custom-call | flops 8858370048 | bytes 17563648 | tf_op jit(solution)/shard_map/pallas_call | solution.py:105
  89.4 0.9 collective-permute-start.3
  90.3 2.4 %collective-permute-start.4 = (f32[256,128]{1,0:T(8,128)S(1)}, f32[256,128]{1,0:T(8,128)S(1)}, u32[]{:S(2)}, u32[]{:S(2)}) collective-permute-start(f32[256,128]{1,0:T(8,128)S(1)} %get-tuple-element.16), channel_id=1, source_target_pairs={{0,16},{8,24},{16,0},{24,8},{1,17},{9,25},{17,1},{25,9},{2,18},{10... | collective-permute-start | bytes 393224 | tf_op jit(solution)/shard_map/ppermute | solution.py:209
  92.7 1.4 collective-permute-start.5
  94.7 3.5 %collective-permute-done.4 = f32[256,128]{1,0:T(8,128)S(1)} collective-permute-done((f32[256,128]{1,0:T(8,128)S(1)}, f32[256,128]{1,0:T(8,128)S(1)}, u32[]{:S(2)}, u32[]{:S(2)}) %collective-permute-start.4) | collective-permute-done | bytes 131104 | tf_op jit(solution)/shard_map/ppermute | solution.py:209
  98.2 1.8 %collective-permute-done.5 = f32[256,128]{1,0:T(8,128)S(1)} collective-permute-done((f32[256,128]{1,0:T(8,128)S(1)}, f32[256,128]{1,0:T(8,128)S(1)}, u32[]{:S(2)}, u32[]{:S(2)}) %collective-permute-start.5) | collective-permute-done | bytes 131104 | tf_op jit(solution)/shard_map/ppermute | solution.py:209
  100.7 1.7 %collective-permute-start.7 = (bf16[256,128]{1,0:T(8,128)(2,1)S(1)}, bf16[256,128]{1,0:T(8,128)(2,1)S(1)}, u32[]{:S(2)}, u32[]{:S(2)}) collective-permute-start(bf16[256,128]{1,0:T(8,128)(2,1)S(1)} %fusion.15), channel_id=1, source_target_pairs={{0,16},{8,24},{16,0},{24,8},{1,17},{9,25},{17,1},{25,9},{2,18},{10... | collective-permute-start | bytes 196616 | tf_op jit(solution)/shard_map/ppermute | solution.py:214
  102.4 1.2 collective-permute-start.8
  103.6 1.1 collective-permute-done.6
  104.7 1.0 collective-permute-done.7
  105.7 1.9 %collective-permute-done.8 = bf16[256,128]{1,0:T(8,128)(2,1)S(1)} collective-permute-done((bf16[256,128]{1,0:T(8,128)(2,1)S(1)}, bf16[256,128]{1,0:T(8,128)(2,1)S(1)}, u32[]{:S(2)}, u32[]{:S(2)}) %collective-permute-start.8) | collective-permute-done | bytes 65568 | tf_op jit(solution)/shard_map/ppermute | solution.py:214
  107.6 0.9 fusion.x_ref
  108.5 9.9 %shard_map.102.h_ref = bf16[1024,4096]{1,0:T(8,128)(2,1)} custom-call(s32[4]{0:T(128)} %and_select_fusion.1.live_tiles, bf16[4,256,128]{2,1,0:T(8,128)(2,1)} %fusion.x_ref, bf16[128,4096]{1,0:T(8,128)(2,1)} %refs_0_.3, bf16[128,4096]{1,0:T(8,128)(2,1)} %copy-done.4, bf16[128,4096]{1,0:T(8,128)(2,1)} %copy-done.5, ...), custom_call_target="tpu_custom_call" | custom-call | flops 1476395008 | bytes 12582912 | tf_op jit(solution)/shard_map/pallas_call | solution.py:64
  118.5 14.0 %shard_map.103 = f32[1024,128]{1,0:T(8,128)S(1)} custom-call(s32[4]{0:T(128)S(1)} %copy-done.2, bf16[1024,4096]{1,0:T(8,128)(2,1)} %shard_map.102.h_ref, bf16[4096,1024]{1,0:T(8,128)(2,1)} %m_ref.3, bf16[1024,128]{1,0:T(8,128)(2,1)S(1)} %copy-done.3), custom_call_target="tpu_custom_call" | custom-call | flops 8858370048 | bytes 17563648 | tf_op jit(solution)/shard_map/pallas_call | solution.py:105
  132.6 2.0 %collective-permute-start.10 = (f32[256,128]{1,0:T(8,128)S(1)}, f32[256,128]{1,0:T(8,128)S(1)}, u32[]{:S(2)}, u32[]{:S(2)}) collective-permute-start(f32[256,128]{1,0:T(8,128)S(1)} %get-tuple-element.13), channel_id=1, source_target_pairs={{0,16},{8,24},{16,0},{24,8},{1,17},{9,25},{17,1},{25,9},{2,18},{10... | collective-permute-start | bytes 393224 | tf_op jit(solution)/shard_map/ppermute | solution.py:209
  134.6 1.5 collective-permute-start.9
  136.2 2.4 %collective-permute-done.10 = f32[256,128]{1,0:T(8,128)S(1)} collective-permute-done((f32[256,128]{1,0:T(8,128)S(1)}, f32[256,128]{1,0:T(8,128)S(1)}, u32[]{:S(2)}, u32[]{:S(2)}) %collective-permute-start.10) | collective-permute-done | bytes 131104 | tf_op jit(solution)/shard_map/ppermute | solution.py:209
  138.5 1.9 %collective-permute-done.11 = f32[256,128]{1,0:T(8,128)S(1)} collective-permute-done((f32[256,128]{1,0:T(8,128)S(1)}, f32[256,128]{1,0:T(8,128)S(1)}, u32[]{:S(2)}, u32[]{:S(2)}) %collective-permute-start.11) | collective-permute-done | bytes 131104 | tf_op jit(solution)/shard_map/ppermute | solution.py:209
  142.2 6.7 %all-to-all-start.1 = ((bf16[32,8,128]{2,1,0:T(8,128)(2,1)}), bf16[32,8,128]{2,1,0:T(8,128)(2,1)S(1)}, u32[]{:S(2)}, u32[]{:S(2)}) async-start(bf16[32,8,128]{2,1,0:T(8,128)(2,1)} %bitcast_select_fusion), calls=%async_computation.1 | async-start | bytes 131072 | tf_op jit(solution)/shard_map/all_to_all | solution.py:223
  148.9 7.3 %all-to-all-done.1 = bf16[32,8,128]{2,1,0:T(8,128)(2,1)S(1)} async-done(((bf16[32,8,128]{2,1,0:T(8,128)(2,1)}), bf16[32,8,128]{2,1,0:T(8,128)(2,1)S(1)}, u32[]{:S(2)}, u32[]{:S(2)}) %all-to-all-start.1) | async-done | bytes 65568 | tf_op jit(solution)/shard_map/all_to_all | solution.py:223
  (82 shorter events, 16.4 us)
Async XLA Ops:
  0.0 9.9 %copy-start = (bf16[2048,128]{1,0:T(8,128)(2,1)S(1)}, bf16[2048,128]{1,0:T(8,128)(2,1)}, u32[]{:S(2)}) copy-start(bf16[2048,128]{1,0:T(8,128)(2,1)} %param.10) | copy-start | bytes 1572868
  0.0 64.0 %collective-permute-start = (bf16[128,4096]{1,0:T(8,128)(2,1)}, bf16[128,4096]{1,0:T(8,128)(2,1)S(1)}, u32[]{:S(2)}, u32[]{:S(2)}) collective-permute-start(bf16[128,4096]{1,0:T(8,128)(2,1)} %refs_0_.3), channel_id=1, source_target_pairs={{0,8},{8,0},{16,24},{24,16},{1,9},{9,1},{17,25},{25,17},{2,10},{10... | collective-permute-start | bytes 3145736 | tf_op jit(solution)/shard_map/ppermute | solution.py:152
  3.0 61.0 %collective-permute-start.1 = (bf16[128,4096]{1,0:T(8,128)(2,1)}, bf16[128,4096]{1,0:T(8,128)(2,1)S(1)}, u32[]{:S(2)}, u32[]{:S(2)}) collective-permute-start(bf16[128,4096]{1,0:T(8,128)(2,1)} %refs_0_.3), channel_id=1, source_target_pairs={{0,16},{8,24},{16,0},{24,8},{1,17},{9,25},{17,1},{25,9},{2,18},{10... | collective-permute-start | bytes 3145736 | tf_op jit(solution)/shard_map/ppermute | solution.py:152
  4.5 59.5 %collective-permute-start.2 = (bf16[128,4096]{1,0:T(8,128)(2,1)}, bf16[128,4096]{1,0:T(8,128)(2,1)}, u32[]{:S(2)}, u32[]{:S(2)}) collective-permute-start(bf16[128,4096]{1,0:T(8,128)(2,1)} %refs_0_.3), channel_id=1, source_target_pairs={{0,24},{8,16},{16,8},{24,0},{1,25},{9,17},{17,9},{25,1},{2,26},{10... | collective-permute-start | bytes 3145736 | tf_op jit(solution)/shard_map/ppermute | solution.py:152
  13.3 42.6 %all-to-all-start = ((bf16[32,32,129]{2,1,0:T(8,128)(2,1)}), bf16[32,32,129]{2,1,0:T(8,128)(2,1)S(1)}, u32[]{:S(2)}, u32[]{:S(2)}) async-start(bf16[32,32,129]{2,1,0:T(8,128)(2,1)} %bitcast.65), calls=%async_computation | async-start | bytes 1048576 | tf_op jit(solution)/shard_map/all_to_all | solution.py:178
  55.9 19.3 %copy-start.3 = (bf16[1024,128]{1,0:T(8,128)(2,1)S(1)}, bf16[1024,128]{1,0:T(8,128)(2,1)}, u32[]{:S(2)}) copy-start(bf16[1024,128]{1,0:T(8,128)(2,1)} %w_ref.3) | copy-start | bytes 786436
  61.5 2.5 %copy-start.6 = (bf16[4,256,129]{2,1,0:T(8,128)(2,1)}, bf16[4,256,129]{2,1,0:T(8,128)(2,1)S(1)}, u32[]{:S(2)}) copy-start(bf16[4,256,129]{2,1,0:T(8,128)(2,1)S(1)} %convolution_convert_fusion) | copy-start | bytes 792580
  63.1 12.2 %copy-start.1 = (s32[4]{0:T(128)S(1)}, s32[4]{0:T(128)}, u32[]{:S(2)}) copy-start(s32[4]{0:T(128)} %and_select_fusion.1.live_tiles) | copy-start | bytes 52
  64.0 1.0 copy-start.4
  64.0 1.3 copy-start.5
  75.2 32.4 %copy-start.7 = (bf16[4,256,129]{2,1,0:T(8,128)(2,1)S(1)}, bf16[4,256,129]{2,1,0:T(8,128)(2,1)}, u32[]{:S(2)}) copy-start(bf16[4,256,129]{2,1,0:T(8,128)(2,1)} %copy-done.6) | copy-start | bytes 792580
  75.3 32.4 %copy-start.9 = (bf16[128,128]{1,0:T(8,128)(2,1)S(1)}, bf16[128,128]{1,0:T(8,128)(2,1)}, u32[]{:S(2)}) copy-start(bf16[128,128]{1,0:T(8,128)(2,1)} %param.18) | copy-start | bytes 98308
  89.3 29.2 %copy-start.2 = (s32[4]{0:T(128)S(1)}, s32[4]{0:T(128)}, u32[]{:S(2)}) copy-start(s32[4]{0:T(128)} %and_select_fusion.1.live_tiles) | copy-start | bytes 52
  89.4 5.3 %collective-permute-start.3 = (f32[256,128]{1,0:T(8,128)S(1)}, f32[256,128]{1,0:T(8,128)S(1)}, u32[]{:S(2)}, u32[]{:S(2)}) collective-permute-start(f32[256,128]{1,0:T(8,128)S(1)} %get-tuple-element.14), channel_id=1, source_target_pairs={{0,8},{8,0},{16,24},{24,16},{1,9},{9,1},{17,25},{25,17},{2,10},{10... | collective-permute-start | bytes 393224 | tf_op jit(solution)/shard_map/ppermute | solution.py:209
  90.3 7.9 %collective-permute-start.4 = (f32[256,128]{1,0:T(8,128)S(1)}, f32[256,128]{1,0:T(8,128)S(1)}, u32[]{:S(2)}, u32[]{:S(2)}) collective-permute-start(f32[256,128]{1,0:T(8,128)S(1)} %get-tuple-element.16), channel_id=1, source_target_pairs={{0,16},{8,24},{16,0},{24,8},{1,17},{9,25},{17,1},{25,9},{2,18},{10... | collective-permute-start | bytes 393224 | tf_op jit(solution)/shard_map/ppermute | solution.py:209
  92.7 7.3 %collective-permute-start.5 = (f32[256,128]{1,0:T(8,128)S(1)}, f32[256,128]{1,0:T(8,128)S(1)}, u32[]{:S(2)}, u32[]{:S(2)}) collective-permute-start(f32[256,128]{1,0:T(8,128)S(1)} %get-tuple-element.15), channel_id=1, source_target_pairs={{0,24},{8,16},{16,8},{24,0},{1,25},{9,17},{17,9},{25,1},{2,26},{10... | collective-permute-start | bytes 393224 | tf_op jit(solution)/shard_map/ppermute | solution.py:209
  100.1 4.6 %collective-permute-start.6 = (bf16[256,128]{1,0:T(8,128)(2,1)S(1)}, bf16[256,128]{1,0:T(8,128)(2,1)S(1)}, u32[]{:S(2)}, u32[]{:S(2)}) collective-permute-start(bf16[256,128]{1,0:T(8,128)(2,1)S(1)} %fusion.15), channel_id=1, source_target_pairs={{0,8},{8,0},{16,24},{24,16},{1,9},{9,1},{17,25},{25,17},{2,10},{10... | collective-permute-start | bytes 196616 | tf_op jit(solution)/shard_map/ppermute | solution.py:214
  100.7 5.0 %collective-permute-start.7 = (bf16[256,128]{1,0:T(8,128)(2,1)S(1)}, bf16[256,128]{1,0:T(8,128)(2,1)S(1)}, u32[]{:S(2)}, u32[]{:S(2)}) collective-permute-start(bf16[256,128]{1,0:T(8,128)(2,1)S(1)} %fusion.15), channel_id=1, source_target_pairs={{0,16},{8,24},{16,0},{24,8},{1,17},{9,25},{17,1},{25,9},{2,18},{10... | collective-permute-start | bytes 196616 | tf_op jit(solution)/shard_map/ppermute | solution.py:214
  102.4 5.2 %collective-permute-start.8 = (bf16[256,128]{1,0:T(8,128)(2,1)S(1)}, bf16[256,128]{1,0:T(8,128)(2,1)S(1)}, u32[]{:S(2)}, u32[]{:S(2)}) collective-permute-start(bf16[256,128]{1,0:T(8,128)(2,1)S(1)} %fusion.15), channel_id=1, source_target_pairs={{0,24},{8,16},{16,8},{24,0},{1,25},{9,17},{17,9},{25,1},{2,26},{10... | collective-permute-start | bytes 196616 | tf_op jit(solution)/shard_map/ppermute | solution.py:214
  118.5 30.3 %copy-start.8 = (s32[128,1]{0,1:T(1,128)S(1)}, s32[128,1]{0,1:T(1,128)}, u32[]{:S(2)}) copy-start(s32[128,1]{0,1:T(1,128)} %param.13) | copy-start | bytes 1540
  132.6 6.0 %collective-permute-start.10 = (f32[256,128]{1,0:T(8,128)S(1)}, f32[256,128]{1,0:T(8,128)S(1)}, u32[]{:S(2)}, u32[]{:S(2)}) collective-permute-start(f32[256,128]{1,0:T(8,128)S(1)} %get-tuple-element.13), channel_id=1, source_target_pairs={{0,16},{8,24},{16,0},{24,8},{1,17},{9,25},{17,1},{25,9},{2,18},{10... | collective-permute-start | bytes 393224 | tf_op jit(solution)/shard_map/ppermute | solution.py:209
  134.6 5.9 %collective-permute-start.11 = (f32[256,128]{1,0:T(8,128)S(1)}, f32[256,128]{1,0:T(8,128)S(1)}, u32[]{:S(2)}, u32[]{:S(2)}) collective-permute-start(f32[256,128]{1,0:T(8,128)S(1)} %get-tuple-element.12), channel_id=1, source_target_pairs={{0,24},{8,16},{16,8},{24,0},{1,25},{9,17},{17,9},{25,1},{2,26},{10... | collective-permute-start | bytes 393224 | tf_op jit(solution)/shard_map/ppermute | solution.py:209
  134.6 5.9 %collective-permute-start.9 = (f32[256,128]{1,0:T(8,128)S(1)}, f32[256,128]{1,0:T(8,128)S(1)}, u32[]{:S(2)}, u32[]{:S(2)}) collective-permute-start(f32[256,128]{1,0:T(8,128)S(1)} %get-tuple-element.11), channel_id=1, source_target_pairs={{0,8},{8,0},{16,24},{24,16},{1,9},{9,1},{17,25},{25,17},{2,10},{10... | collective-permute-start | bytes 393224 | tf_op jit(solution)/shard_map/ppermute | solution.py:209
  142.2 14.1 %all-to-all-start.1 = ((bf16[32,8,128]{2,1,0:T(8,128)(2,1)}), bf16[32,8,128]{2,1,0:T(8,128)(2,1)S(1)}, u32[]{:S(2)}, u32[]{:S(2)}) async-start(bf16[32,8,128]{2,1,0:T(8,128)(2,1)} %bitcast_select_fusion), calls=%async_computation.1 | async-start | bytes 131072 | tf_op jit(solution)/shard_map/all_to_all | solution.py:223

commit v9 on v4

--- a/solution.py
+++ b/solution.py
@@ -2,6 +2,8 @@
 import jax.numpy as jnp
 import numpy as np
 from jax import lax
+from jax.experimental import pallas as pl
+from jax.experimental.pallas import tpu as pltpu
 from jax.sharding import PartitionSpec as P
 
 PASSES = 2
@@ -15,24 +17,65 @@
     return jnp.concatenate([hi, mid, lo], axis=0)
 
 
-def band_rows(band_values, parts):
+def band_picks(band_values, parts):
     levels = parts.shape[0] // 3
     level_ids = jnp.arange(3 * levels, dtype=jnp.int32) % levels
-    picks = (band_values[:, None] == level_ids[None, :]).astype(jnp.bfloat16)
-    return jnp.dot(picks, parts, preferred_element_type=jnp.float32)
+    return (band_values[..., None] == level_ids).astype(jnp.bfloat16)
 
 
-def first_hidden(rows, weights, band_values, parts):
-    mixed = jnp.einsum("srf,sfh->srh", rows, weights, preferred_element_type=jnp.float32)
-    mixed = mixed.reshape(-1, weights.shape[2]) * band_rows(band_values, parts)
-    return jax.nn.silu(mixed).astype(jnp.bfloat16)
+CHUNK = 512
 
 
-def surrogate_tail(hidden_block, middle_weight, out_weight):
-    middle = jax.nn.silu(
-        jnp.dot(hidden_block, middle_weight, preferred_element_type=jnp.float32)
-    ).astype(jnp.bfloat16)
-    return jnp.dot(middle, out_weight, preferred_element_type=jnp.float32)
+def pass_kernel(x_ref, *refs):
+    w_refs, (p_ref, s_ref, m_ref, u_ref, o_ref) = refs[:-5], refs[-5:]
+    block = pl.program_id(0)
+    hid = s_ref.shape[1]
+    for k, w_ref in enumerate(w_refs):
+
+        @pl.when(block == k)
+        def _():
+            x = x_ref[...]
+            p = p_ref[...]
+            acc = None
+            for c in range(hid // CHUNK):
+                cols = slice(c * CHUNK, (c + 1) * CHUNK)
+                mixed = jnp.dot(x, w_ref[:, cols], preferred_element_type=jnp.float32)
+                scale = jnp.dot(p, s_ref[:, cols], preferred_element_type=jnp.float32)
+                v = mixed * scale
+                h = (v * jax.nn.sigmoid(v)).astype(jnp.bfloat16)
+                part = jnp.dot(h, m_ref[cols, :], preferred_element_type=jnp.float32)
+                acc = part if acc is None else acc + part
+            middle = (acc * jax.nn.sigmoid(acc)).astype(jnp.bfloat16)
+            o_ref[...] = jnp.dot(middle, u_ref[...], preferred_element_type=jnp.float32)
+
+
+def pass_values(rows, weights, picks, parts, middle_weight, out_weight):
+    n_blocks, n_rows, feat = rows.shape
+    hid = weights[0].shape[1]
+    mid = middle_weight.shape[1]
+    out_width = out_weight.shape[1]
+    n_pick = picks.shape[2]
+    return pl.pallas_call(
+        pass_kernel,
+        grid=(n_blocks,),
+        in_specs=[pl.BlockSpec((None, n_rows, feat), lambda s: (s, 0, 0))]
+        + [pl.BlockSpec((feat, hid), lambda s: (0, 0)) for _ in range(n_blocks)]
+        + [
+            pl.BlockSpec((None, n_rows, n_pick), lambda s: (s, 0, 0)),
+            pl.BlockSpec((n_pick, hid), lambda s: (0, 0)),
+            pl.BlockSpec((hid, mid), lambda s: (0, 0)),
+            pl.BlockSpec((mid, out_width), lambda s: (0, 0)),
+        ],
+        out_specs=pl.BlockSpec((n_rows, out_width), lambda s: (s, 0)),
+        out_shape=jax.ShapeDtypeStruct((n_blocks * n_rows, out_width), jnp.float32),
+        compiler_params=pltpu.CompilerParams(vmem_limit_bytes=60 * 1024 * 1024),
+        cost_estimate=pl.CostEstimate(
+            flops=2 * n_blocks * n_rows * (hid * (feat + n_pick + mid) + mid * out_width),
+            transcendentals=n_blocks * n_rows * (hid + mid),
+            bytes_accessed=2 * (n_blocks * feat * hid + hid * mid + mid * out_width)
+            + 4 * n_blocks * n_rows * out_width,
+        ),
+    )(rows, *weights, picks, parts, middle_weight, out_weight)
 
 
 def xor_pairs(n, k):
@@ -90,13 +133,11 @@
     got = got.reshape(count_all, n_sec, slot_count, feat_width + 1).transpose(1, 0, 2, 3)
     got = got.reshape(n_sec, count_all * slot_count, feat_width + 1)
     rows = got[:, :, :feat_width]
-    got_band = got[:, :, feat_width].astype(jnp.int32).reshape(-1)
-    every_first = jnp.stack(block_first)
+    picks = band_picks(got[:, :, feat_width].astype(jnp.int32), parts)
 
     result = None
     for segment_index in range(PASSES):
-        hidden = first_hidden(rows, every_first, got_band, parts)
-        partial = surrogate_tail(hidden, middle_weight, out_weight).reshape(
+        partial = pass_values(rows, block_first, picks, parts, middle_weight, out_weight).reshape(
             n_sec, rows.shape[1], -1
         )
         own_sum = partial[0]

time: 162 us -> 148 us (0.914)
  matrix products: 52 us -> 1.15 us
  Pallas kernels: 0 us -> 44.9 us
  other arithmetic: 22.1 us -> 10.7 us
  local copies, waits for them, and re-layouts: 4.87 us -> 8.98 us
    dot_general x5 -> x1, matrix products: 51.8 us -> 0.94 us  [per_device(): jnp.einsum('sro,of->srf', values, back_weight, preferred_element_type=jnp...]
    pallas_call x0 -> x2, Pallas kernels: none -> 44.9 us  [pass_values(): pl.pallas_call(pass_kernel, grid=(n_blocks,), in_specs=[pl.BlockSpec((Non...]
    convert_element_type x2 -> x1, other arithmetic: 15.1 us -> 0.9 us  [band_picks(): return (band_values[..., None] == level_ids).astype(jnp.bfloat16)]
    slice x2, local copies, waits for them, and re-layouts: 0.06 us -> 2.11 us  [per_device(): own_sum = own_sum + lax.ppermute(partial[k], 'sec', xor_pairs(n_sec, k))]
  transfers between devices with their start and end apart: 14 -> 14, of which waited for: 11 -> 11; matrix products, arithmetic and copies ran while one was open for 6% -> 9% of each run, Pallas kernels for 0% -> 0%
where the time goes in v9:
time: 148 us; the launch traced here: 147 us
  waiting for transfers between devices  55.5 us (38%)
  Pallas kernels  44.9 us (30%)
  starting transfers between devices  26 us (18%)
  other arithmetic  10.7 us (7%)
  local copies, waits for them, and re-layouts  8.98 us (6%)
    pallas_call x2, Pallas kernels, pass_values(): pl.pallas_call(pass_kernel, grid=(n_blocks,), in_specs=[pl.BlockSpec((Non...  44.9 us
    all_to_all x1, waiting for transfers between devices, per_device(): lax.all_to_all(send, ('sec', 'dev'), split_axis=0, concat_axis=0, tiled=T...  34.3 us
    ppermute x6, waiting for transfers between devices, per_device(): own_sum = own_sum + lax.ppermute(partial[k], 'sec', xor_pairs(n_sec, k))  9.8 us
    all_to_all x1, waiting for transfers between devices, per_device(): lax.all_to_all(own_values.reshape(count_all, slot_count, out_width), ('se...  7.35 us
    ppermute x6, starting transfers between devices, per_device(): own_sum = own_sum + lax.ppermute(partial[k], 'sec', xor_pairs(n_sec, k))  7.11 us
    all_to_all x1, starting transfers between devices, per_device(): lax.all_to_all(send, ('sec', 'dev'), split_axis=0, concat_axis=0, tiled=T...  6.32 us
    all_to_all x1, starting transfers between devices, per_device(): lax.all_to_all(own_values.reshape(count_all, slot_count, out_width), ('se...  4.52 us
    ppermute x3, starting transfers between devices, per_device(): lax.ppermute(first_layers, 'sec', xor_pairs(n_sec, k))  4.5 us
  transfers between devices with their start and end apart: 14, of which 11 were waited for; matrix products, arithmetic and copies ran while one was open for 9% of the time, Pallas kernels for 0%

profile of v9, /device:TPU:0, one launch (start us, length us, event | category | flops | bytes accessed | tf_op | source)
XLA Modules:
  0.0 147.4 jit_solution(5169408918468454837)
XLA Ops:
  0.0 3.0 %collective-permute-start = (bf16[128,4096]{1,0:T(8,128)(2,1)}, bf16[128,4096]{1,0:T(8,128)(2,1)S(1)}, u32[]{:S(2)}, u32[]{:S(2)}) collective-permute-start(bf16[128,4096]{1,0:T(8,128)(2,1)} %refs_0_.3), channel_id=1, source_target_pairs={{0,8},{8,0},{16,24},{24,16},{1,9},{9,1},{17,25},{25,17},{2,10},{10... | collective-permute-start | bytes 3145736 | tf_op jit(solution)/shard_map/ppermute | solution.py:106
  3.0 1.5 %collective-permute-start.1 = (bf16[128,4096]{1,0:T(8,128)(2,1)}, bf16[128,4096]{1,0:T(8,128)(2,1)S(1)}, u32[]{:S(2)}, u32[]{:S(2)}) collective-permute-start(bf16[128,4096]{1,0:T(8,128)(2,1)} %refs_0_.3), channel_id=1, source_target_pairs={{0,16},{8,24},{16,0},{24,8},{1,17},{9,25},{17,1},{25,9},{2,18},{10... | collective-permute-start | bytes 3145736 | tf_op jit(solution)/shard_map/ppermute | solution.py:106
  7.6 1.6 %gather_fusion.1 = s32[128]{0:T(128)S(1)} fusion(s32[2048]{0:T(1024)} %param.11, s32[1024]{0:T(1024)S(1)} %pad_clamp_fusion.2), kind=kCustom, calls=%fused_computation.1 | custom fusion | bytes 1536 | tf_op jit(solution)/shard_map/jit(_take)/gather | solution.py:111
  13.3 6.3 %all-to-all-start = ((bf16[32,32,129]{2,1,0:T(8,128)(2,1)}), bf16[32,32,129]{2,1,0:T(8,128)(2,1)S(1)}, u32[]{:S(2)}, u32[]{:S(2)}) async-start(bf16[32,32,129]{2,1,0:T(8,128)(2,1)} %bitcast.8), calls=%async_computation | async-start | bytes 1048576 | tf_op jit(solution)/shard_map/all_to_all | solution.py:132
  19.6 1.1 fusion.29
  21.5 34.3 %all-to-all-done = bf16[32,32,129]{2,1,0:T(8,128)(2,1)S(1)} async-done(((bf16[32,32,129]{2,1,0:T(8,128)(2,1)}), bf16[32,32,129]{2,1,0:T(8,128)(2,1)S(1)}, u32[]{:S(2)}, u32[]{:S(2)}) %all-to-all-start) | async-done | bytes 264224 | tf_op jit(solution)/shard_map/all_to_all | solution.py:132
  57.8 1.0 copy-done.2
  59.1 22.4 %shard_map.100 = f32[1024,128]{1,0:T(8,128)} custom-call(bf16[4,256,128]{2,1,0:T(8,128)(2,1)} %slice.56.x_ref, bf16[128,4096]{1,0:T(8,128)(2,1)} %refs_0_.3, bf16[128,4096]{1,0:T(8,128)(2,1)} %copy-done.2, bf16[128,4096]{1,0:T(8,128)(2,1)} %copy-done.3, bf16[128,4096]{1,0:T(8,128)(2,1)} %collective-permute-done.2.refs_3_, ...), custom_call_target="tpu_custom_call" | custom-call | flops 10334765056 | bytes 13369344 | tf_op jit(solution)/shard_map/pallas_call | solution.py:58
  81.6 1.1 fusion.28
  83.5 1.2 collective-permute-start.4
  84.8 1.4 collective-permute-start.5
  86.2 2.6 %collective-permute-done.3 = f32[256,128]{1,0:T(8,128)S(1)} collective-permute-done((f32[256,128]{1,0:T(8,128)S(1)}, f32[256,128]{1,0:T(8,128)S(1)}, u32[]{:S(2)}, u32[]{:S(2)}) %collective-permute-start.3) | collective-permute-done | bytes 131104 | tf_op jit(solution)/shard_map/ppermute | solution.py:145
  88.8 1.4 collective-permute-done.4
  90.2 1.5 collective-permute-done.5
  91.6 0.9 fusion.14
  92.6 1.0 collective-permute-start.6
  93.6 1.4 collective-permute-start.7
  95.0 1.1 collective-permute-start.8
  96.1 1.1 collective-permute-done.6
  97.2 1.1 collective-permute-done.7
  98.3 1.9 %collective-permute-done.8 = bf16[256,128]{1,0:T(8,128)(2,1)S(1)} collective-permute-done((bf16[256,128]{1,0:T(8,128)(2,1)S(1)}, bf16[256,128]{1,0:T(8,128)(2,1)S(1)}, u32[]{:S(2)}, u32[]{:S(2)}) %collective-permute-start.8) | collective-permute-done | bytes 65568 | tf_op jit(solution)/shard_map/ppermute | solution.py:150
  100.2 0.9 fusion.x_ref
  101.1 22.5 %shard_map.101 = f32[1024,128]{1,0:T(8,128)} custom-call(bf16[4,256,128]{2,1,0:T(8,128)(2,1)} %fusion.x_ref, bf16[128,4096]{1,0:T(8,128)(2,1)} %refs_0_.3, bf16[128,4096]{1,0:T(8,128)(2,1)} %copy-done.2, bf16[128,4096]{1,0:T(8,128)(2,1)} %copy-done.3, bf16[128,4096]{1,0:T(8,128)(2,1)} %collective-permute-done.2.refs_3_, ...), custom_call_target="tpu_custom_call" | custom-call | flops 10334765056 | bytes 13369344 | tf_op jit(solution)/shard_map/pallas_call | solution.py:58
  123.6 1.1 fusion.27
  125.3 1.5 %collective-permute-start.11 = (f32[256,128]{1,0:T(8,128)S(1)}, f32[256,128]{1,0:T(8,128)S(1)}, u32[]{:S(2)}, u32[]{:S(2)}) collective-permute-start(f32[256,128]{1,0:T(8,128)S(1)} %get-tuple-element.10), channel_id=1, source_target_pairs={{0,24},{8,16},{16,8},{24,0},{1,25},{9,17},{17,9},{25,1},{2,26},{10... | collective-permute-start | bytes 393224 | tf_op jit(solution)/shard_map/ppermute | solution.py:145
  126.8 1.4 collective-permute-start.9
  128.2 1.5 %collective-permute-done.10 = f32[256,128]{1,0:T(8,128)S(1)} collective-permute-done((f32[256,128]{1,0:T(8,128)S(1)}, f32[256,128]{1,0:T(8,128)S(1)}, u32[]{:S(2)}, u32[]{:S(2)}) %collective-permute-start.10) | collective-permute-done | bytes 131104 | tf_op jit(solution)/shard_map/ppermute | solution.py:145
  129.7 1.5 %collective-permute-done.11 = f32[256,128]{1,0:T(8,128)S(1)} collective-permute-done((f32[256,128]{1,0:T(8,128)S(1)}, f32[256,128]{1,0:T(8,128)S(1)}, u32[]{:S(2)}, u32[]{:S(2)}) %collective-permute-start.11) | collective-permute-done | bytes 131104 | tf_op jit(solution)/shard_map/ppermute | solution.py:145
  131.2 1.4 collective-permute-done.9
  132.5 1.6 %fusion.15 = bf16[32,8,128]{2,1,0:T(8,128)(2,1)} fusion(f32[256,128]{1,0:T(8,128)S(1)} %collective-permute-done.11, f32[256,128]{1,0:T(8,128)S(1)} %collective-permute-done.10, f32[256,128]{1,0:T(8,128)S(1)} %collective-permute-done.9, f32[1024,128]{1,0:T(8,128)} %shard_map.101), kind=kLoop, calls=%fused_computation.30 | loop fusion | flops 131072 | bytes 589824 | tf_op jit(solution)/shard_map/reshape | solution.py:159
  134.1 4.5 %all-to-all-start.1 = ((bf16[32,8,128]{2,1,0:T(8,128)(2,1)}), bf16[32,8,128]{2,1,0:T(8,128)(2,1)S(1)}, u32[]{:S(2)}, u32[]{:S(2)}) async-start(bf16[32,8,128]{2,1,0:T(8,128)(2,1)} %fusion.15), calls=%async_computation.1 | async-start | bytes 131072 | tf_op jit(solution)/shard_map/all_to_all | solution.py:158
  138.7 7.3 %all-to-all-done.1 = bf16[32,8,128]{2,1,0:T(8,128)(2,1)S(1)} async-done(((bf16[32,8,128]{2,1,0:T(8,128)(2,1)}), bf16[32,8,128]{2,1,0:T(8,128)(2,1)S(1)}, u32[]{:S(2)}, u32[]{:S(2)}) %all-to-all-start.1) | async-done | bytes 65568 | tf_op jit(solution)/shard_map/all_to_all | solution.py:158
  (40 shorter events, 13.2 us)
Async XLA Ops:
  0.0 9.9 %copy-start = (bf16[2048,128]{1,0:T(8,128)(2,1)S(1)}, bf16[2048,128]{1,0:T(8,128)(2,1)}, u32[]{:S(2)}) copy-start(bf16[2048,128]{1,0:T(8,128)(2,1)} %param.10) | copy-start | bytes 1572868
  0.0 57.8 %collective-permute-start = (bf16[128,4096]{1,0:T(8,128)(2,1)}, bf16[128,4096]{1,0:T(8,128)(2,1)S(1)}, u32[]{:S(2)}, u32[]{:S(2)}) collective-permute-start(bf16[128,4096]{1,0:T(8,128)(2,1)} %refs_0_.3), channel_id=1, source_target_pairs={{0,8},{8,0},{16,24},{24,16},{1,9},{9,1},{17,25},{25,17},{2,10},{10... | collective-permute-start | bytes 3145736 | tf_op jit(solution)/shard_map/ppermute | solution.py:106
  3.0 54.9 %collective-permute-start.1 = (bf16[128,4096]{1,0:T(8,128)(2,1)}, bf16[128,4096]{1,0:T(8,128)(2,1)S(1)}, u32[]{:S(2)}, u32[]{:S(2)}) collective-permute-start(bf16[128,4096]{1,0:T(8,128)(2,1)} %refs_0_.3), channel_id=1, source_target_pairs={{0,16},{8,24},{16,0},{24,8},{1,17},{9,25},{17,1},{25,9},{2,18},{10... | collective-permute-start | bytes 3145736 | tf_op jit(solution)/shard_map/ppermute | solution.py:106
  4.5 53.4 %collective-permute-start.2 = (bf16[128,4096]{1,0:T(8,128)(2,1)}, bf16[128,4096]{1,0:T(8,128)(2,1)}, u32[]{:S(2)}, u32[]{:S(2)}) collective-permute-start(bf16[128,4096]{1,0:T(8,128)(2,1)} %refs_0_.3), channel_id=1, source_target_pairs={{0,24},{8,16},{16,8},{24,0},{1,25},{9,17},{17,9},{25,1},{2,26},{10... | collective-permute-start | bytes 3145736 | tf_op jit(solution)/shard_map/ppermute | solution.py:106
  13.3 42.6 %all-to-all-start = ((bf16[32,32,129]{2,1,0:T(8,128)(2,1)}), bf16[32,32,129]{2,1,0:T(8,128)(2,1)S(1)}, u32[]{:S(2)}, u32[]{:S(2)}) async-start(bf16[32,32,129]{2,1,0:T(8,128)(2,1)} %bitcast.8), calls=%async_computation | async-start | bytes 1048576 | tf_op jit(solution)/shard_map/all_to_all | solution.py:132
  57.8 42.4 %copy-start.4 = (bf16[128,128]{1,0:T(8,128)(2,1)S(1)}, bf16[128,128]{1,0:T(8,128)(2,1)}, u32[]{:S(2)}) copy-start(bf16[128,128]{1,0:T(8,128)(2,1)} %param.18) | copy-start | bytes 98308
  57.8 1.0 copy-start.2
  57.8 1.3 copy-start.3
  82.6 6.2 %collective-permute-start.3 = (f32[256,128]{1,0:T(8,128)S(1)}, f32[256,128]{1,0:T(8,128)S(1)}, u32[]{:S(2)}, u32[]{:S(2)}) collective-permute-start(f32[256,128]{1,0:T(8,128)S(1)} %get-tuple-element.12), channel_id=1, source_target_pairs={{0,8},{8,0},{16,24},{24,16},{1,9},{9,1},{17,25},{25,17},{2,10},{10... | collective-permute-start | bytes 393224 | tf_op jit(solution)/shard_map/ppermute | solution.py:145
  83.5 6.6 %collective-permute-start.4 = (f32[256,128]{1,0:T(8,128)S(1)}, f32[256,128]{1,0:T(8,128)S(1)}, u32[]{:S(2)}, u32[]{:S(2)}) collective-permute-start(f32[256,128]{1,0:T(8,128)S(1)} %get-tuple-element.14), channel_id=1, source_target_pairs={{0,16},{8,24},{16,0},{24,8},{1,17},{9,25},{17,1},{25,9},{2,18},{10... | collective-permute-start | bytes 393224 | tf_op jit(solution)/shard_map/ppermute | solution.py:145
  84.8 6.9 %collective-permute-start.5 = (f32[256,128]{1,0:T(8,128)S(1)}, f32[256,128]{1,0:T(8,128)S(1)}, u32[]{:S(2)}, u32[]{:S(2)}) collective-permute-start(f32[256,128]{1,0:T(8,128)S(1)} %get-tuple-element.13), channel_id=1, source_target_pairs={{0,24},{8,16},{16,8},{24,0},{1,25},{9,17},{17,9},{25,1},{2,26},{10... | collective-permute-start | bytes 393224 | tf_op jit(solution)/shard_map/ppermute | solution.py:145
  92.6 4.7 %collective-permute-start.6 = (bf16[256,128]{1,0:T(8,128)(2,1)S(1)}, bf16[256,128]{1,0:T(8,128)(2,1)S(1)}, u32[]{:S(2)}, u32[]{:S(2)}) collective-permute-start(bf16[256,128]{1,0:T(8,128)(2,1)S(1)} %fusion.14), channel_id=1, source_target_pairs={{0,8},{8,0},{16,24},{24,16},{1,9},{9,1},{17,25},{25,17},{2,10},{10... | collective-permute-start | bytes 196616 | tf_op jit(solution)/shard_map/ppermute | solution.py:150
  93.6 4.7 %collective-permute-start.7 = (bf16[256,128]{1,0:T(8,128)(2,1)S(1)}, bf16[256,128]{1,0:T(8,128)(2,1)S(1)}, u32[]{:S(2)}, u32[]{:S(2)}) collective-permute-start(bf16[256,128]{1,0:T(8,128)(2,1)S(1)} %fusion.14), channel_id=1, source_target_pairs={{0,16},{8,24},{16,0},{24,8},{1,17},{9,25},{17,1},{25,9},{2,18},{10... | collective-permute-start | bytes 196616 | tf_op jit(solution)/shard_map/ppermute | solution.py:150
  95.0 5.2 %collective-permute-start.8 = (bf16[256,128]{1,0:T(8,128)(2,1)S(1)}, bf16[256,128]{1,0:T(8,128)(2,1)S(1)}, u32[]{:S(2)}, u32[]{:S(2)}) collective-permute-start(bf16[256,128]{1,0:T(8,128)(2,1)S(1)} %fusion.14), channel_id=1, source_target_pairs={{0,24},{8,16},{16,8},{24,0},{1,25},{9,17},{17,9},{25,1},{2,26},{10... | collective-permute-start | bytes 196616 | tf_op jit(solution)/shard_map/ppermute | solution.py:150
  101.1 37.5 %copy-start.1 = (s32[128,1]{0,1:T(1,128)S(1)}, s32[128,1]{0,1:T(1,128)}, u32[]{:S(2)}) copy-start(s32[128,1]{0,1:T(1,128)} %param.13) | copy-start | bytes 1540
  124.6 5.0 %collective-permute-start.10 = (f32[256,128]{1,0:T(8,128)S(1)}, f32[256,128]{1,0:T(8,128)S(1)}, u32[]{:S(2)}, u32[]{:S(2)}) collective-permute-start(f32[256,128]{1,0:T(8,128)S(1)} %get-tuple-element.11), channel_id=1, source_target_pairs={{0,16},{8,24},{16,0},{24,8},{1,17},{9,25},{17,1},{25,9},{2,18},{10... | collective-permute-start | bytes 393224 | tf_op jit(solution)/shard_map/ppermute | solution.py:145
  125.3 5.9 %collective-permute-start.11 = (f32[256,128]{1,0:T(8,128)S(1)}, f32[256,128]{1,0:T(8,128)S(1)}, u32[]{:S(2)}, u32[]{:S(2)}) collective-permute-start(f32[256,128]{1,0:T(8,128)S(1)} %get-tuple-element.10), channel_id=1, source_target_pairs={{0,24},{8,16},{16,8},{24,0},{1,25},{9,17},{17,9},{25,1},{2,26},{10... | collective-permute-start | bytes 393224 | tf_op jit(solution)/shard_map/ppermute | solution.py:145
  126.8 5.7 %collective-permute-start.9 = (f32[256,128]{1,0:T(8,128)S(1)}, f32[256,128]{1,0:T(8,128)S(1)}, u32[]{:S(2)}, u32[]{:S(2)}) collective-permute-start(f32[256,128]{1,0:T(8,128)S(1)} %get-tuple-element.9), channel_id=1, source_target_pairs={{0,8},{8,0},{16,24},{24,16},{1,9},{9,1},{17,25},{25,17},{2,10},{10... | collective-permute-start | bytes 393224 | tf_op jit(solution)/shard_map/ppermute | solution.py:145
  134.1 11.9 %all-to-all-start.1 = ((bf16[32,8,128]{2,1,0:T(8,128)(2,1)}), bf16[32,8,128]{2,1,0:T(8,128)(2,1)S(1)}, u32[]{:S(2)}, u32[]{:S(2)}) async-start(bf16[32,8,128]{2,1,0:T(8,128)(2,1)} %fusion.15), calls=%async_computation.1 | async-start | bytes 131072 | tf_op jit(solution)/shard_map/all_to_all | solution.py:158

commit v10 on v9

--- a/solution.py
+++ b/solution.py
@@ -23,7 +23,7 @@
     return (band_values[..., None] == level_ids).astype(jnp.bfloat16)
 
 
-CHUNK = 512
+CHUNK = 2048
 
 
 def pass_kernel(x_ref, *refs):

time: 148 us -> 143 us (0.966)
  Pallas kernels: 44.9 us -> 40.1 us
    pallas_call x2, Pallas kernels: 44.9 us -> 40.1 us  [pass_values(): pl.pallas_call(pass_kernel, grid=(n_blocks,), in_specs=[pl.BlockSpec((Non...]
where the time goes in v10:
time: 143 us
  waiting for transfers between devices  55.5 us (39%)
  Pallas kernels  40.1 us (28%)
  starting transfers between devices  26 us (18%)
  other arithmetic  10.7 us (7%)
  local copies, waits for them, and re-layouts  8.98 us (6%)
    pallas_call x2, Pallas kernels, pass_values(): pl.pallas_call(pass_kernel, grid=(n_blocks,), in_specs=[pl.BlockSpec((Non...  40.1 us
    all_to_all x1, waiting for transfers between devices, per_device(): lax.all_to_all(send, ('sec', 'dev'), split_axis=0, concat_axis=0, tiled=T...  34.3 us
    ppermute x6, waiting for transfers between devices, per_device(): own_sum = own_sum + lax.ppermute(partial[k], 'sec', xor_pairs(n_sec, k))  9.8 us
    all_to_all x1, waiting for transfers between devices, per_device(): lax.all_to_all(own_values.reshape(count_all, slot_count, out_width), ('se...  7.35 us
    ppermute x6, starting transfers between devices, per_device(): own_sum = own_sum + lax.ppermute(partial[k], 'sec', xor_pairs(n_sec, k))  7.11 us
    all_to_all x1, starting transfers between devices, per_device(): lax.all_to_all(send, ('sec', 'dev'), split_axis=0, concat_axis=0, tiled=T...  6.32 us
    ppermute x3, starting transfers between devices, per_device(): lax.ppermute(first_layers, 'sec', xor_pairs(n_sec, k))  4.5 us
    all_to_all x1, starting transfers between devices, per_device(): lax.all_to_all(own_values.reshape(count_all, slot_count, out_width), ('se...  4.49 us
  transfers between devices with their start and end apart: 14, of which 11 were waited for; matrix products, arithmetic and copies ran while one was open for 9% of the time, Pallas kernels for 0%

profile of v10, /device:TPU:0, one launch (start us, length us, event | category | flops | bytes accessed | tf_op | source)
XLA Modules:
  0.0 142.6 jit_solution(1034780401694398517)
XLA Ops:
  0.0 3.0 %collective-permute-start = (bf16[128,4096]{1,0:T(8,128)(2,1)}, bf16[128,4096]{1,0:T(8,128)(2,1)S(1)}, u32[]{:S(2)}, u32[]{:S(2)}) collective-permute-start(bf16[128,4096]{1,0:T(8,128)(2,1)} %refs_0_.3), channel_id=1, source_target_pairs={{0,8},{8,0},{16,24},{24,16},{1,9},{9,1},{17,25},{25,17},{2,10},{10... | collective-permute-start | bytes 3145736 | tf_op jit(solution)/shard_map/ppermute | solution.py:106
  3.0 1.5 %collective-permute-start.1 = (bf16[128,4096]{1,0:T(8,128)(2,1)}, bf16[128,4096]{1,0:T(8,128)(2,1)S(1)}, u32[]{:S(2)}, u32[]{:S(2)}) collective-permute-start(bf16[128,4096]{1,0:T(8,128)(2,1)} %refs_0_.3), channel_id=1, source_target_pairs={{0,16},{8,24},{16,0},{24,8},{1,17},{9,25},{17,1},{25,9},{2,18},{10... | collective-permute-start | bytes 3145736 | tf_op jit(solution)/shard_map/ppermute | solution.py:106
  7.6 1.6 %gather_fusion.1 = s32[128]{0:T(128)S(1)} fusion(s32[2048]{0:T(1024)} %param.11, s32[1024]{0:T(1024)S(1)} %pad_clamp_fusion.2), kind=kCustom, calls=%fused_computation.1 | custom fusion | bytes 1536 | tf_op jit(solution)/shard_map/jit(_take)/gather | solution.py:111
  13.3 6.3 %all-to-all-start = ((bf16[32,32,129]{2,1,0:T(8,128)(2,1)}), bf16[32,32,129]{2,1,0:T(8,128)(2,1)S(1)}, u32[]{:S(2)}, u32[]{:S(2)}) async-start(bf16[32,32,129]{2,1,0:T(8,128)(2,1)} %bitcast.8), calls=%async_computation | async-start | bytes 1048576 | tf_op jit(solution)/shard_map/all_to_all | solution.py:132
  19.6 1.1 fusion.29
  21.5 34.3 %all-to-all-done = bf16[32,32,129]{2,1,0:T(8,128)(2,1)S(1)} async-done(((bf16[32,32,129]{2,1,0:T(8,128)(2,1)}), bf16[32,32,129]{2,1,0:T(8,128)(2,1)S(1)}, u32[]{:S(2)}, u32[]{:S(2)}) %all-to-all-start) | async-done | bytes 264224 | tf_op jit(solution)/shard_map/all_to_all | solution.py:132
  57.8 1.0 copy-done.2
  59.1 20.0 %shard_map.100 = f32[1024,128]{1,0:T(8,128)} custom-call(bf16[4,256,128]{2,1,0:T(8,128)(2,1)} %slice.56.x_ref, bf16[128,4096]{1,0:T(8,128)(2,1)} %refs_0_.3, bf16[128,4096]{1,0:T(8,128)(2,1)} %copy-done.2, bf16[128,4096]{1,0:T(8,128)(2,1)} %copy-done.3, bf16[128,4096]{1,0:T(8,128)(2,1)} %collective-permute-done.2.refs_3_, ...), custom_call_target="tpu_custom_call" | custom-call | flops 10334765056 | bytes 13369344 | tf_op jit(solution)/shard_map/pallas_call | solution.py:58
  79.2 1.1 fusion.28
  81.1 1.2 collective-permute-start.4
  82.3 1.4 %collective-permute-start.5 = (f32[256,128]{1,0:T(8,128)S(1)}, f32[256,128]{1,0:T(8,128)S(1)}, u32[]{:S(2)}, u32[]{:S(2)}) collective-permute-start(f32[256,128]{1,0:T(8,128)S(1)} %get-tuple-element.13), channel_id=1, source_target_pairs={{0,24},{8,16},{16,8},{24,0},{1,25},{9,17},{17,9},{25,1},{2,26},{10... | collective-permute-start | bytes 393224 | tf_op jit(solution)/shard_map/ppermute | solution.py:145
  83.8 2.6 %collective-permute-done.3 = f32[256,128]{1,0:T(8,128)S(1)} collective-permute-done((f32[256,128]{1,0:T(8,128)S(1)}, f32[256,128]{1,0:T(8,128)S(1)}, u32[]{:S(2)}, u32[]{:S(2)}) %collective-permute-start.3) | collective-permute-done | bytes 131104 | tf_op jit(solution)/shard_map/ppermute | solution.py:145
  86.4 1.4 collective-permute-done.4
  87.8 1.5 %collective-permute-done.5 = f32[256,128]{1,0:T(8,128)S(1)} collective-permute-done((f32[256,128]{1,0:T(8,128)S(1)}, f32[256,128]{1,0:T(8,128)S(1)}, u32[]{:S(2)}, u32[]{:S(2)}) %collective-permute-start.5) | collective-permute-done | bytes 131104 | tf_op jit(solution)/shard_map/ppermute | solution.py:145
  89.2 0.9 fusion.14
  90.2 1.0 collective-permute-start.6
  91.2 1.5 %collective-permute-start.7 = (bf16[256,128]{1,0:T(8,128)(2,1)S(1)}, bf16[256,128]{1,0:T(8,128)(2,1)S(1)}, u32[]{:S(2)}, u32[]{:S(2)}) collective-permute-start(bf16[256,128]{1,0:T(8,128)(2,1)S(1)} %fusion.14), channel_id=1, source_target_pairs={{0,16},{8,24},{16,0},{24,8},{1,17},{9,25},{17,1},{25,9},{2,18},{10... | collective-permute-start | bytes 196616 | tf_op jit(solution)/shard_map/ppermute | solution.py:150
  92.6 1.1 collective-permute-start.8
  93.7 1.1 collective-permute-done.6
  94.8 1.1 collective-permute-done.7
  95.9 1.9 %collective-permute-done.8 = bf16[256,128]{1,0:T(8,128)(2,1)S(1)} collective-permute-done((bf16[256,128]{1,0:T(8,128)(2,1)S(1)}, bf16[256,128]{1,0:T(8,128)(2,1)S(1)}, u32[]{:S(2)}, u32[]{:S(2)}) %collective-permute-start.8) | collective-permute-done | bytes 65568 | tf_op jit(solution)/shard_map/ppermute | solution.py:150
  97.8 0.9 fusion.x_ref
  98.7 20.1 %shard_map.101 = f32[1024,128]{1,0:T(8,128)} custom-call(bf16[4,256,128]{2,1,0:T(8,128)(2,1)} %fusion.x_ref, bf16[128,4096]{1,0:T(8,128)(2,1)} %refs_0_.3, bf16[128,4096]{1,0:T(8,128)(2,1)} %copy-done.2, bf16[128,4096]{1,0:T(8,128)(2,1)} %copy-done.3, bf16[128,4096]{1,0:T(8,128)(2,1)} %collective-permute-done.2.refs_3_, ...), custom_call_target="tpu_custom_call" | custom-call | flops 10334765056 | bytes 13369344 | tf_op jit(solution)/shard_map/pallas_call | solution.py:58
  118.8 1.1 fusion.27
  120.5 1.5 %collective-permute-start.11 = (f32[256,128]{1,0:T(8,128)S(1)}, f32[256,128]{1,0:T(8,128)S(1)}, u32[]{:S(2)}, u32[]{:S(2)}) collective-permute-start(f32[256,128]{1,0:T(8,128)S(1)} %get-tuple-element.10), channel_id=1, source_target_pairs={{0,24},{8,16},{16,8},{24,0},{1,25},{9,17},{17,9},{25,1},{2,26},{10... | collective-permute-start | bytes 393224 | tf_op jit(solution)/shard_map/ppermute | solution.py:145
  122.0 1.4 collective-permute-start.9
  123.4 1.5 %collective-permute-done.10 = f32[256,128]{1,0:T(8,128)S(1)} collective-permute-done((f32[256,128]{1,0:T(8,128)S(1)}, f32[256,128]{1,0:T(8,128)S(1)}, u32[]{:S(2)}, u32[]{:S(2)}) %collective-permute-start.10) | collective-permute-done | bytes 131104 | tf_op jit(solution)/shard_map/ppermute | solution.py:145
  124.9 1.5 %collective-permute-done.11 = f32[256,128]{1,0:T(8,128)S(1)} collective-permute-done((f32[256,128]{1,0:T(8,128)S(1)}, f32[256,128]{1,0:T(8,128)S(1)}, u32[]{:S(2)}, u32[]{:S(2)}) %collective-permute-start.11) | collective-permute-done | bytes 131104 | tf_op jit(solution)/shard_map/ppermute | solution.py:145
  126.3 1.4 collective-permute-done.9
  127.8 1.6 %fusion.15 = bf16[32,8,128]{2,1,0:T(8,128)(2,1)} fusion(f32[256,128]{1,0:T(8,128)S(1)} %collective-permute-done.11, f32[256,128]{1,0:T(8,128)S(1)} %collective-permute-done.10, f32[256,128]{1,0:T(8,128)S(1)} %collective-permute-done.9, f32[1024,128]{1,0:T(8,128)} %shard_map.101), kind=kLoop, calls=%fused_computation.30 | loop fusion | flops 131072 | bytes 589824 | tf_op jit(solution)/shard_map/reshape | solution.py:159
  129.3 4.5 %all-to-all-start.1 = ((bf16[32,8,128]{2,1,0:T(8,128)(2,1)}), bf16[32,8,128]{2,1,0:T(8,128)(2,1)S(1)}, u32[]{:S(2)}, u32[]{:S(2)}) async-start(bf16[32,8,128]{2,1,0:T(8,128)(2,1)} %fusion.15), calls=%async_computation.1 | async-start | bytes 131072 | tf_op jit(solution)/shard_map/all_to_all | solution.py:158
  133.9 7.3 %all-to-all-done.1 = bf16[32,8,128]{2,1,0:T(8,128)(2,1)S(1)} async-done(((bf16[32,8,128]{2,1,0:T(8,128)(2,1)}), bf16[32,8,128]{2,1,0:T(8,128)(2,1)S(1)}, u32[]{:S(2)}, u32[]{:S(2)}) %all-to-all-start.1) | async-done | bytes 65568 | tf_op jit(solution)/shard_map/all_to_all | solution.py:158
  (40 shorter events, 13.1 us)
Async XLA Ops:
  0.0 9.9 %copy-start = (bf16[2048,128]{1,0:T(8,128)(2,1)S(1)}, bf16[2048,128]{1,0:T(8,128)(2,1)}, u32[]{:S(2)}) copy-start(bf16[2048,128]{1,0:T(8,128)(2,1)} %param.10) | copy-start | bytes 1572868
  0.0 57.8 %collective-permute-start = (bf16[128,4096]{1,0:T(8,128)(2,1)}, bf16[128,4096]{1,0:T(8,128)(2,1)S(1)}, u32[]{:S(2)}, u32[]{:S(2)}) collective-permute-start(bf16[128,4096]{1,0:T(8,128)(2,1)} %refs_0_.3), channel_id=1, source_target_pairs={{0,8},{8,0},{16,24},{24,16},{1,9},{9,1},{17,25},{25,17},{2,10},{10... | collective-permute-start | bytes 3145736 | tf_op jit(solution)/shard_map/ppermute | solution.py:106
  3.0 54.9 %collective-permute-start.1 = (bf16[128,4096]{1,0:T(8,128)(2,1)}, bf16[128,4096]{1,0:T(8,128)(2,1)S(1)}, u32[]{:S(2)}, u32[]{:S(2)}) collective-permute-start(bf16[128,4096]{1,0:T(8,128)(2,1)} %refs_0_.3), channel_id=1, source_target_pairs={{0,16},{8,24},{16,0},{24,8},{1,17},{9,25},{17,1},{25,9},{2,18},{10... | collective-permute-start | bytes 3145736 | tf_op jit(solution)/shard_map/ppermute | solution.py:106
  4.5 53.4 %collective-permute-start.2 = (bf16[128,4096]{1,0:T(8,128)(2,1)}, bf16[128,4096]{1,0:T(8,128)(2,1)}, u32[]{:S(2)}, u32[]{:S(2)}) collective-permute-start(bf16[128,4096]{1,0:T(8,128)(2,1)} %refs_0_.3), channel_id=1, source_target_pairs={{0,24},{8,16},{16,8},{24,0},{1,25},{9,17},{17,9},{25,1},{2,26},{10... | collective-permute-start | bytes 3145736 | tf_op jit(solution)/shard_map/ppermute | solution.py:106
  13.3 42.6 %all-to-all-start = ((bf16[32,32,129]{2,1,0:T(8,128)(2,1)}), bf16[32,32,129]{2,1,0:T(8,128)(2,1)S(1)}, u32[]{:S(2)}, u32[]{:S(2)}) async-start(bf16[32,32,129]{2,1,0:T(8,128)(2,1)} %bitcast.8), calls=%async_computation | async-start | bytes 1048576 | tf_op jit(solution)/shard_map/all_to_all | solution.py:132
  57.8 40.0 %copy-start.4 = (bf16[128,128]{1,0:T(8,128)(2,1)S(1)}, bf16[128,128]{1,0:T(8,128)(2,1)}, u32[]{:S(2)}) copy-start(bf16[128,128]{1,0:T(8,128)(2,1)} %param.18) | copy-start | bytes 98308
  57.8 1.0 copy-start.2
  57.8 1.3 copy-start.3
  80.2 6.1 %collective-permute-start.3 = (f32[256,128]{1,0:T(8,128)S(1)}, f32[256,128]{1,0:T(8,128)S(1)}, u32[]{:S(2)}, u32[]{:S(2)}) collective-permute-start(f32[256,128]{1,0:T(8,128)S(1)} %get-tuple-element.12), channel_id=1, source_target_pairs={{0,8},{8,0},{16,24},{24,16},{1,9},{9,1},{17,25},{25,17},{2,10},{10... | collective-permute-start | bytes 393224 | tf_op jit(solution)/shard_map/ppermute | solution.py:145
  81.1 6.7 %collective-permute-start.4 = (f32[256,128]{1,0:T(8,128)S(1)}, f32[256,128]{1,0:T(8,128)S(1)}, u32[]{:S(2)}, u32[]{:S(2)}) collective-permute-start(f32[256,128]{1,0:T(8,128)S(1)} %get-tuple-element.14), channel_id=1, source_target_pairs={{0,16},{8,24},{16,0},{24,8},{1,17},{9,25},{17,1},{25,9},{2,18},{10... | collective-permute-start | bytes 393224 | tf_op jit(solution)/shard_map/ppermute | solution.py:145
  82.3 6.9 %collective-permute-start.5 = (f32[256,128]{1,0:T(8,128)S(1)}, f32[256,128]{1,0:T(8,128)S(1)}, u32[]{:S(2)}, u32[]{:S(2)}) collective-permute-start(f32[256,128]{1,0:T(8,128)S(1)} %get-tuple-element.13), channel_id=1, source_target_pairs={{0,24},{8,16},{16,8},{24,0},{1,25},{9,17},{17,9},{25,1},{2,26},{10... | collective-permute-start | bytes 393224 | tf_op jit(solution)/shard_map/ppermute | solution.py:145
  90.2 4.7 %collective-permute-start.6 = (bf16[256,128]{1,0:T(8,128)(2,1)S(1)}, bf16[256,128]{1,0:T(8,128)(2,1)S(1)}, u32[]{:S(2)}, u32[]{:S(2)}) collective-permute-start(bf16[256,128]{1,0:T(8,128)(2,1)S(1)} %fusion.14), channel_id=1, source_target_pairs={{0,8},{8,0},{16,24},{24,16},{1,9},{9,1},{17,25},{25,17},{2,10},{10... | collective-permute-start | bytes 196616 | tf_op jit(solution)/shard_map/ppermute | solution.py:150
  91.2 4.8 %collective-permute-start.7 = (bf16[256,128]{1,0:T(8,128)(2,1)S(1)}, bf16[256,128]{1,0:T(8,128)(2,1)S(1)}, u32[]{:S(2)}, u32[]{:S(2)}) collective-permute-start(bf16[256,128]{1,0:T(8,128)(2,1)S(1)} %fusion.14), channel_id=1, source_target_pairs={{0,16},{8,24},{16,0},{24,8},{1,17},{9,25},{17,1},{25,9},{2,18},{10... | collective-permute-start | bytes 196616 | tf_op jit(solution)/shard_map/ppermute | solution.py:150
  92.6 5.2 %collective-permute-start.8 = (bf16[256,128]{1,0:T(8,128)(2,1)S(1)}, bf16[256,128]{1,0:T(8,128)(2,1)S(1)}, u32[]{:S(2)}, u32[]{:S(2)}) collective-permute-start(bf16[256,128]{1,0:T(8,128)(2,1)S(1)} %fusion.14), channel_id=1, source_target_pairs={{0,24},{8,16},{16,8},{24,0},{1,25},{9,17},{17,9},{25,1},{2,26},{10... | collective-permute-start | bytes 196616 | tf_op jit(solution)/shard_map/ppermute | solution.py:150
  98.7 35.1 %copy-start.1 = (s32[128,1]{0,1:T(1,128)S(1)}, s32[128,1]{0,1:T(1,128)}, u32[]{:S(2)}) copy-start(s32[128,1]{0,1:T(1,128)} %param.13) | copy-start | bytes 1540
  119.9 5.0 %collective-permute-start.10 = (f32[256,128]{1,0:T(8,128)S(1)}, f32[256,128]{1,0:T(8,128)S(1)}, u32[]{:S(2)}, u32[]{:S(2)}) collective-permute-start(f32[256,128]{1,0:T(8,128)S(1)} %get-tuple-element.11), channel_id=1, source_target_pairs={{0,16},{8,24},{16,0},{24,8},{1,17},{9,25},{17,1},{25,9},{2,18},{10... | collective-permute-start | bytes 393224 | tf_op jit(solution)/shard_map/ppermute | solution.py:145
  120.5 5.9 %collective-permute-start.11 = (f32[256,128]{1,0:T(8,128)S(1)}, f32[256,128]{1,0:T(8,128)S(1)}, u32[]{:S(2)}, u32[]{:S(2)}) collective-permute-start(f32[256,128]{1,0:T(8,128)S(1)} %get-tuple-element.10), channel_id=1, source_target_pairs={{0,24},{8,16},{16,8},{24,0},{1,25},{9,17},{17,9},{25,1},{2,26},{10... | collective-permute-start | bytes 393224 | tf_op jit(solution)/shard_map/ppermute | solution.py:145
  122.0 5.7 %collective-permute-start.9 = (f32[256,128]{1,0:T(8,128)S(1)}, f32[256,128]{1,0:T(8,128)S(1)}, u32[]{:S(2)}, u32[]{:S(2)}) collective-permute-start(f32[256,128]{1,0:T(8,128)S(1)} %get-tuple-element.9), channel_id=1, source_target_pairs={{0,8},{8,0},{16,24},{24,16},{1,9},{9,1},{17,25},{25,17},{2,10},{10... | collective-permute-start | bytes 393224 | tf_op jit(solution)/shard_map/ppermute | solution.py:145
  129.3 11.9 %all-to-all-start.1 = ((bf16[32,8,128]{2,1,0:T(8,128)(2,1)}), bf16[32,8,128]{2,1,0:T(8,128)(2,1)S(1)}, u32[]{:S(2)}, u32[]{:S(2)}) async-start(bf16[32,8,128]{2,1,0:T(8,128)(2,1)} %fusion.15), calls=%async_computation.1 | async-start | bytes 131072 | tf_op jit(solution)/shard_map/all_to_all | solution.py:158

commit v11 on v10

--- a/solution.py
+++ b/solution.py
@@ -132,6 +132,7 @@
     got = lax.all_to_all(send, ("sec", "dev"), split_axis=0, concat_axis=0, tiled=True)
     got = got.reshape(count_all, n_sec, slot_count, feat_width + 1).transpose(1, 0, 2, 3)
     got = got.reshape(n_sec, count_all * slot_count, feat_width + 1)
+    sec_turn = jnp.bitwise_xor(jnp.arange(n_sec, dtype=jnp.int32), lax.axis_index("sec"))
     rows = got[:, :, :feat_width]
     picks = band_picks(got[:, :, feat_width].astype(jnp.int32), parts)
 
@@ -140,14 +141,17 @@
         partial = pass_values(rows, block_first, picks, parts, middle_weight, out_weight).reshape(
             n_sec, rows.shape[1], -1
         )
-        own_sum = partial[0]
-        for k in range(1, n_sec):
-            own_sum = own_sum + lax.ppermute(partial[k], "sec", xor_pairs(n_sec, k))
+        by_owner = jnp.take(partial, sec_turn, axis=0)
+        own_sum = jnp.sum(
+            lax.all_to_all(by_owner, "sec", split_axis=0, concat_axis=0, tiled=True), axis=0
+        )
         own_values = own_sum.astype(jnp.bfloat16)
         if segment_index + 1 < PASSES:
-            values = jnp.stack(
-                [own_values]
-                + [lax.ppermute(own_values, "sec", xor_pairs(n_sec, k)) for k in range(1, n_sec)]
+            spread = jnp.broadcast_to(own_values[None], (n_sec,) + own_values.shape)
+            values = jnp.take(
+                lax.all_to_all(spread, "sec", split_axis=0, concat_axis=0, tiled=True),
+                sec_turn,
+                axis=0,
             )
             rows = (
                 rows.astype(jnp.float32)

time: 143 us -> 149 us (1.042)
  blocking collectives: 0 us -> 20.8 us
  waiting for transfers between devices: 55.5 us -> 47 us
  starting transfers between devices: 26 us -> 18.6 us
  local copies, waits for them, and re-layouts: 8.98 us -> 11.1 us
  other arithmetic: 10.7 us -> 9.11 us
    all_to_all x0 -> x2, blocking collectives: none -> 20.8 us  [per_device(): lax.all_to_all(by_owner, 'sec', split_axis=0, concat_axis=0, tiled=True)]
    ppermute x9 -> x0, waiting for transfers between devices: 13.9 us -> none  [the longest x6 9.8 us: per_device(): own_sum = own_sum + lax.ppermute(partial[k], 'sec', xor_pairs(n_sec, k))]
    ppermute x9 -> x0, starting transfers between devices: 10.7 us -> none  [the longest x6 7.11 us: per_device(): own_sum = own_sum + lax.ppermute(partial[k], 'sec', xor_pairs(n_sec, k))]
    all_to_all x0 -> x1, waiting for transfers between devices: none -> 5.31 us  [per_device(): lax.all_to_all(spread, 'sec', split_axis=0, concat_axis=0, tiled=True)]
    gather x0 -> x3, local copies, waits for them, and re-layouts: none -> 3.83 us  [the longest x2 3.24 us: per_device(): by_owner = jnp.take(partial, sec_turn, axis=0)]
    all_to_all x0 -> x1, starting transfers between devices: none -> 3.4 us  [per_device(): lax.all_to_all(spread, 'sec', split_axis=0, concat_axis=0, tiled=True)]
    slice x2 -> x0, local copies, waits for them, and re-layouts: 2.11 us -> none  [per_device(): own_sum = own_sum + lax.ppermute(partial[k], 'sec', xor_pairs(n_sec, k))]
    reshape x1 -> x0, other arithmetic: 1.57 us -> none  [per_device(): own_values.reshape(count_all, slot_count, out_width)]
  transfers between devices with their start and end apart: 14 -> 6, of which waited for: 11 -> 3; matrix products, arithmetic and copies ran while one was open for 9% -> 8% of each run, Pallas kernels for 0% -> 0%
where the time goes in v11:
time: 149 us; the launch traced here: 148 us
  waiting for transfers between devices  47 us (32%)
  Pallas kernels  40.1 us (27%)
  blocking collectives  20.8 us (14%)
  starting transfers between devices  18.6 us (12%)
  local copies, waits for them, and re-layouts  11.1 us (7%)
  other arithmetic  9.11 us (6%)
    pallas_call x2, Pallas kernels, pass_values(): pl.pallas_call(pass_kernel, grid=(n_blocks,), in_specs=[pl.BlockSpec((Non...  40.1 us
    all_to_all x1, waiting for transfers between devices, per_device(): lax.all_to_all(send, ('sec', 'dev'), split_axis=0, concat_axis=0, tiled=T...  34.3 us
    all_to_all x2, blocking collectives, per_device(): lax.all_to_all(by_owner, 'sec', split_axis=0, concat_axis=0, tiled=True)  20.8 us
    all_to_all x1, waiting for transfers between devices, per_device(): lax.all_to_all(own_values.reshape(count_all, slot_count, out_width), ('se...  7.35 us
    all_to_all x1, starting transfers between devices, per_device(): lax.all_to_all(send, ('sec', 'dev'), split_axis=0, concat_axis=0, tiled=T...  6.31 us
    all_to_all x1, waiting for transfers between devices, per_device(): lax.all_to_all(spread, 'sec', split_axis=0, concat_axis=0, tiled=True)  5.31 us
    ppermute x3, starting transfers between devices, per_device(): lax.ppermute(first_layers, 'sec', xor_pairs(n_sec, k))  4.5 us
    all_to_all x1, starting transfers between devices, per_device(): lax.all_to_all(own_values.reshape(count_all, slot_count, out_width), ('se...  4.35 us
  transfers between devices with their start and end apart: 6, of which 3 were waited for; matrix products, arithmetic and copies ran while one was open for 8% of the time, Pallas kernels for 0%

profile of v11, /device:TPU:0, one launch (start us, length us, event | category | flops | bytes accessed | tf_op | source)
XLA Modules:
  0.0 148.0 jit_solution(4106485190445032054)
XLA Ops:
  0.0 3.0 %collective-permute-start = (bf16[128,4096]{1,0:T(8,128)(2,1)}, bf16[128,4096]{1,0:T(8,128)(2,1)S(1)}, u32[]{:S(2)}, u32[]{:S(2)}) collective-permute-start(bf16[128,4096]{1,0:T(8,128)(2,1)} %refs_0_.3), channel_id=1, source_target_pairs={{0,8},{8,0},{16,24},{24,16},{1,9},{9,1},{17,25},{25,17},{2,10},{10... | collective-permute-start | bytes 3145736 | tf_op jit(solution)/shard_map/ppermute | solution.py:106
  3.0 1.5 %collective-permute-start.1 = (bf16[128,4096]{1,0:T(8,128)(2,1)}, bf16[128,4096]{1,0:T(8,128)(2,1)}, u32[]{:S(2)}, u32[]{:S(2)}) collective-permute-start(bf16[128,4096]{1,0:T(8,128)(2,1)} %refs_0_.3), channel_id=1, source_target_pairs={{0,16},{8,24},{16,0},{24,8},{1,17},{9,25},{17,1},{25,9},{2,18},{10... | collective-permute-start | bytes 3145736 | tf_op jit(solution)/shard_map/ppermute | solution.py:106
  4.5 0.7 fusion.9
  5.4 0.8 select_reduce_fusion
  6.2 0.7 fusion.13
  6.9 0.7 compare_select_fusion.2
  7.6 1.6 %gather_fusion.1 = s32[128]{0:T(128)S(1)} fusion(s32[2048]{0:T(1024)} %param.13, s32[1024]{0:T(1024)S(1)} %pad_clamp_fusion.4), kind=kCustom, calls=%fused_computation.3 | custom fusion | bytes 1536 | tf_op jit(solution)/shard_map/jit(_take)/gather | solution.py:111
  9.2 0.7 convert_bitcast_fusion.1
  9.9 0.7 gather_fusion
  11.2 0.7 pad_clamp_fusion.3
  12.4 0.9 copy.14
  13.3 6.3 %all-to-all-start = ((bf16[32,32,129]{2,1,0:T(8,128)(2,1)}), bf16[32,32,129]{2,1,0:T(8,128)(2,1)S(1)}, u32[]{:S(2)}, u32[]{:S(2)}) async-start(bf16[32,32,129]{2,1,0:T(8,128)(2,1)} %bitcast.8), calls=%async_computation | async-start | bytes 1048576 | tf_op jit(solution)/shard_map/all_to_all | solution.py:132
  19.6 1.1 fusion.17
  20.8 0.8 pad_maximum_fusion.refs_5_
  21.6 34.3 %all-to-all-done = bf16[32,32,129]{2,1,0:T(8,128)(2,1)S(1)} async-done(((bf16[32,32,129]{2,1,0:T(8,128)(2,1)}), bf16[32,32,129]{2,1,0:T(8,128)(2,1)S(1)}, u32[]{:S(2)}, u32[]{:S(2)}) %all-to-all-start) | async-done | bytes 264224 | tf_op jit(solution)/shard_map/all_to_all | solution.py:132
  55.9 0.7 slice.22.x_ref
  56.9 0.9 compare_convert_fusion.refs_4_
  57.8 1.0 copy-done.2
  58.8 20.0 %shard_map.100 = f32[1024,128]{1,0:T(8,128)} custom-call(bf16[4,256,128]{2,1,0:T(8,128)(2,1)} %slice.22.x_ref, bf16[128,4096]{1,0:T(8,128)(2,1)} %refs_0_.3, bf16[128,4096]{1,0:T(8,128)(2,1)} %copy-done.2, bf16[128,4096]{1,0:T(8,128)(2,1)} %collective-permute-done.1.refs_2_, bf16[128,4096]{1,0:T(8,128)(2,1)} %collective-permute-done.2.refs_3_, ...), custom_call_target="tpu_custom_call" | custom-call | flops 10334765056 | bytes 13369344 | tf_op jit(solution)/shard_map/pallas_call | solution.py:58
  78.8 1.6 %gather_fusion.5 = f32[4,256,128]{2,1,0:T(8,128)S(1)} fusion(f32[4,256,128]{2,1,0:T(8,128)} %bitcast.41, s32[1024]{0:T(1024)S(1)} %pad_clamp_fusion.2), kind=kCustom, calls=%fused_computation.clone | custom fusion | bytes 1048592 | tf_op jit(solution)/shard_map/jit(_take)/gather | solution.py:144
  80.6 11.3 %all_to_all.25 = f32[4,256,128]{2,1,0:T(8,128)S(1)} all-to-all(f32[4,256,128]{2,1,0:T(8,128)S(1)} %broadcast_select_fusion.1), channel_id=1, replica_groups=mesh['sec'=4,'dev'=8] {'sec'}, dimensions={0} | all-to-all | bytes 1048576 | tf_op jit(solution)/shard_map/all_to_all | solution.py:146
  91.8 0.7 broadcast_in_dim.81
  92.6 3.4 %all-to-all-start.2 = ((bf16[4,256,128]{2,1,0:T(8,128)(2,1)}), bf16[4,256,128]{2,1,0:T(8,128)(2,1)S(1)}, u32[]{:S(2)}, u32[]{:S(2)}) async-start(bf16[4,256,128]{2,1,0:T(8,128)(2,1)} %broadcast_in_dim.81), calls=%async_computation.2 | async-start | bytes 524288 | tf_op jit(solution)/shard_map/all_to_all | solution.py:152
  96.0 5.3 %all-to-all-done.2 = bf16[4,256,128]{2,1,0:T(8,128)(2,1)S(1)} async-done(((bf16[4,256,128]{2,1,0:T(8,128)(2,1)}), bf16[4,256,128]{2,1,0:T(8,128)(2,1)S(1)}, u32[]{:S(2)}, u32[]{:S(2)}) %all-to-all-start.2) | async-done | bytes 262176 | tf_op jit(solution)/shard_map/all_to_all | solution.py:152
  101.9 1.0 fusion.x_ref
  102.9 20.1 %shard_map.101 = f32[1024,128]{1,0:T(8,128)} custom-call(bf16[4,256,128]{2,1,0:T(8,128)(2,1)} %fusion.x_ref, bf16[128,4096]{1,0:T(8,128)(2,1)} %refs_0_.3, bf16[128,4096]{1,0:T(8,128)(2,1)} %copy-done.2, bf16[128,4096]{1,0:T(8,128)(2,1)} %collective-permute-done.1.refs_2_, bf16[128,4096]{1,0:T(8,128)(2,1)} %collective-permute-done.2.refs_3_, ...), custom_call_target="tpu_custom_call" | custom-call | flops 10334765056 | bytes 13369344 | tf_op jit(solution)/shard_map/pallas_call | solution.py:58
  123.0 1.6 %gather_fusion.6 = f32[4,256,128]{2,1,0:T(8,128)S(1)} fusion(f32[4,256,128]{2,1,0:T(8,128)} %bitcast.40, s32[1024]{0:T(1024)S(1)} %pad_clamp_fusion.2), kind=kCustom, calls=%fused_computation.1.clone | custom fusion | bytes 1048592 | tf_op jit(solution)/shard_map/jit(_take)/gather | solution.py:144
  124.7 9.5 %all_to_all.26 = f32[4,256,128]{2,1,0:T(8,128)S(1)} all-to-all(f32[4,256,128]{2,1,0:T(8,128)S(1)} %broadcast_select_fusion), channel_id=1, replica_groups=mesh['sec'=4,'dev'=8] {'sec'}, dimensions={0} | all-to-all | bytes 1048576 | tf_op jit(solution)/shard_map/all_to_all | solution.py:146
  134.9 4.4 %all-to-all-start.4 = ((bf16[32,8,128]{2,1,0:T(8,128)(2,1)}), bf16[32,8,128]{2,1,0:T(8,128)(2,1)S(1)}, u32[]{:S(2)}, u32[]{:S(2)}) async-start(bf16[32,8,128]{2,1,0:T(8,128)(2,1)} %bitcast.33), calls=%async_computation.4 | async-start | bytes 131072 | tf_op jit(solution)/shard_map/all_to_all | solution.py:162
  139.3 7.3 %all-to-all-done.4 = bf16[32,8,128]{2,1,0:T(8,128)(2,1)S(1)} async-done(((bf16[32,8,128]{2,1,0:T(8,128)(2,1)}), bf16[32,8,128]{2,1,0:T(8,128)(2,1)S(1)}, u32[]{:S(2)}, u32[]{:S(2)}) %all-to-all-start.4) | async-done | bytes 65568 | tf_op jit(solution)/shard_map/all_to_all | solution.py:162
  146.6 0.7 gather_fusion.4
  147.3 0.7 broadcast_select_fusion.3
  (33 shorter events, 3.1 us)
Async XLA Ops:
  0.0 9.9 %copy-start = (bf16[2048,128]{1,0:T(8,128)(2,1)S(1)}, bf16[2048,128]{1,0:T(8,128)(2,1)}, u32[]{:S(2)}) copy-start(bf16[2048,128]{1,0:T(8,128)(2,1)} %param.12) | copy-start | bytes 1572868
  0.0 57.8 %collective-permute-start = (bf16[128,4096]{1,0:T(8,128)(2,1)}, bf16[128,4096]{1,0:T(8,128)(2,1)S(1)}, u32[]{:S(2)}, u32[]{:S(2)}) collective-permute-start(bf16[128,4096]{1,0:T(8,128)(2,1)} %refs_0_.3), channel_id=1, source_target_pairs={{0,8},{8,0},{16,24},{24,16},{1,9},{9,1},{17,25},{25,17},{2,10},{10... | collective-permute-start | bytes 3145736 | tf_op jit(solution)/shard_map/ppermute | solution.py:106
  3.0 54.8 %collective-permute-start.1 = (bf16[128,4096]{1,0:T(8,128)(2,1)}, bf16[128,4096]{1,0:T(8,128)(2,1)}, u32[]{:S(2)}, u32[]{:S(2)}) collective-permute-start(bf16[128,4096]{1,0:T(8,128)(2,1)} %refs_0_.3), channel_id=1, source_target_pairs={{0,16},{8,24},{16,0},{24,8},{1,17},{9,25},{17,1},{25,9},{2,18},{10... | collective-permute-start | bytes 3145736 | tf_op jit(solution)/shard_map/ppermute | solution.py:106
  4.5 53.3 %collective-permute-start.2 = (bf16[128,4096]{1,0:T(8,128)(2,1)}, bf16[128,4096]{1,0:T(8,128)(2,1)}, u32[]{:S(2)}, u32[]{:S(2)}) collective-permute-start(bf16[128,4096]{1,0:T(8,128)(2,1)} %refs_0_.3), channel_id=1, source_target_pairs={{0,24},{8,16},{16,8},{24,0},{1,25},{9,17},{17,9},{25,1},{2,26},{10... | collective-permute-start | bytes 3145736 | tf_op jit(solution)/shard_map/ppermute | solution.py:106
  13.3 42.6 %all-to-all-start = ((bf16[32,32,129]{2,1,0:T(8,128)(2,1)}), bf16[32,32,129]{2,1,0:T(8,128)(2,1)S(1)}, u32[]{:S(2)}, u32[]{:S(2)}) async-start(bf16[32,32,129]{2,1,0:T(8,128)(2,1)} %bitcast.8), calls=%async_computation | async-start | bytes 1048576 | tf_op jit(solution)/shard_map/all_to_all | solution.py:132
  57.8 44.1 %copy-start.3 = (bf16[128,128]{1,0:T(8,128)(2,1)S(1)}, bf16[128,128]{1,0:T(8,128)(2,1)}, u32[]{:S(2)}) copy-start(bf16[128,128]{1,0:T(8,128)(2,1)} %param.20) | copy-start | bytes 98308
  57.8 1.0 copy-start.2
  92.6 8.8 %all-to-all-start.2 = ((bf16[4,256,128]{2,1,0:T(8,128)(2,1)}), bf16[4,256,128]{2,1,0:T(8,128)(2,1)S(1)}, u32[]{:S(2)}, u32[]{:S(2)}) async-start(bf16[4,256,128]{2,1,0:T(8,128)(2,1)} %broadcast_in_dim.81), calls=%async_computation.2 | async-start | bytes 524288 | tf_op jit(solution)/shard_map/all_to_all | solution.py:152
  102.9 36.3 %copy-start.1 = (s32[128,1]{0,1:T(1,128)S(1)}, s32[128,1]{0,1:T(1,128)}, u32[]{:S(2)}) copy-start(s32[128,1]{0,1:T(1,128)} %param.15) | copy-start | bytes 1540
  134.9 11.7 %all-to-all-start.4 = ((bf16[32,8,128]{2,1,0:T(8,128)(2,1)}), bf16[32,8,128]{2,1,0:T(8,128)(2,1)S(1)}, u32[]{:S(2)}, u32[]{:S(2)}) async-start(bf16[32,8,128]{2,1,0:T(8,128)(2,1)} %bitcast.33), calls=%async_computation.4 | async-start | bytes 131072 | tf_op jit(solution)/shard_map/all_to_all | solution.py:162

commit v12 on v10

--- a/solution.py
+++ b/solution.py
@@ -128,7 +128,7 @@
     xor_table = np.bitwise_xor.outer(np.arange(n_sec), np.arange(n_sec)).reshape(-1)
     send = jnp.take(grp, jnp.asarray(xor_table, jnp.int32), axis=1)
     send = send.reshape(n_dev, n_sec, n_sec, slot_count, feat_width + 1).transpose(1, 0, 2, 3, 4)
-    send = send.reshape(count_all, group_slots, feat_width + 1)
+    send = send.reshape(count_all, group_slots * (feat_width + 1))
     got = lax.all_to_all(send, ("sec", "dev"), split_axis=0, concat_axis=0, tiled=True)
     got = got.reshape(count_all, n_sec, slot_count, feat_width + 1).transpose(1, 0, 2, 3)
     got = got.reshape(n_sec, count_all * slot_count, feat_width + 1)

time: 143 us -> 144 us (level)
  waiting for transfers between devices: 55.5 us -> 49.2 us
  other arithmetic: 10.7 us -> 14.7 us
  local copies, waits for them, and re-layouts: 8.98 us -> 12 us
    all_to_all x1, waiting for transfers between devices: 34.3 us -> 27.9 us  [per_device(): lax.all_to_all(send, ('sec', 'dev'), split_axis=0, concat_axis=0, tiled=T...]
    all_to_all x0 -> x2, other arithmetic: none -> 3.96 us  [per_device(): lax.all_to_all(send, ('sec', 'dev'), split_axis=0, concat_axis=0, tiled=T...]
    reshape x0 -> x1, local copies, waits for them, and re-layouts: none -> 1.48 us  [per_device(): got.reshape(count_all, n_sec, slot_count, feat_width + 1)]
    all_to_all x0 -> x2, local copies, waits for them, and re-layouts: none -> 1.45 us  [per_device(): lax.all_to_all(send, ('sec', 'dev'), split_axis=0, concat_axis=0, tiled=T...]
  transfers between devices with their start and end apart: 14 -> 14, of which waited for: 11 -> 11; matrix products, arithmetic and copies ran while one was open for 9% -> 13% of each run, Pallas kernels for 0% -> 0%
where the time goes in v12:
time: 144 us; the launch traced here: 143 us
  waiting for transfers between devices  49.2 us (34%)
  Pallas kernels  40.1 us (28%)
  starting transfers between devices  26.1 us (18%)
  other arithmetic  14.7 us (10%)
  local copies, waits for them, and re-layouts  12 us (8%)
    pallas_call x2, Pallas kernels, pass_values(): pl.pallas_call(pass_kernel, grid=(n_blocks,), in_specs=[pl.BlockSpec((Non...  40.1 us
    all_to_all x1, waiting for transfers between devices, per_device(): lax.all_to_all(send, ('sec', 'dev'), split_axis=0, concat_axis=0, tiled=T...  27.9 us
    ppermute x6, waiting for transfers between devices, per_device(): own_sum = own_sum + lax.ppermute(partial[k], 'sec', xor_pairs(n_sec, k))  10 us
    all_to_all x1, waiting for transfers between devices, per_device(): lax.all_to_all(own_values.reshape(count_all, slot_count, out_width), ('se...  7.35 us
    ppermute x6, starting transfers between devices, per_device(): own_sum = own_sum + lax.ppermute(partial[k], 'sec', xor_pairs(n_sec, k))  7.11 us
    all_to_all x1, starting transfers between devices, per_device(): lax.all_to_all(send, ('sec', 'dev'), split_axis=0, concat_axis=0, tiled=T...  6.31 us
    all_to_all x1, starting transfers between devices, per_device(): lax.all_to_all(own_values.reshape(count_all, slot_count, out_width), ('se...  4.59 us
    ppermute x3, starting transfers between devices, per_device(): lax.ppermute(first_layers, 'sec', xor_pairs(n_sec, k))  4.5 us
  transfers between devices with their start and end apart: 14, of which 11 were waited for; matrix products, arithmetic and copies ran while one was open for 13% of the time, Pallas kernels for 0%

profile of v12, /device:TPU:0, one launch (start us, length us, event | category | flops | bytes accessed | tf_op | source)
XLA Modules:
  0.0 143.4 jit_solution(13895839626338572593)
XLA Ops:
  0.0 3.0 %collective-permute-start = (bf16[128,4096]{1,0:T(8,128)(2,1)}, bf16[128,4096]{1,0:T(8,128)(2,1)S(1)}, u32[]{:S(2)}, u32[]{:S(2)}) collective-permute-start(bf16[128,4096]{1,0:T(8,128)(2,1)} %refs_0_.3), channel_id=1, source_target_pairs={{0,8},{8,0},{16,24},{24,16},{1,9},{9,1},{17,25},{25,17},{2,10},{10... | collective-permute-start | bytes 3145736 | tf_op jit(solution)/shard_map/ppermute | solution.py:106
  3.0 1.5 %collective-permute-start.1 = (bf16[128,4096]{1,0:T(8,128)(2,1)}, bf16[128,4096]{1,0:T(8,128)(2,1)}, u32[]{:S(2)}, u32[]{:S(2)}) collective-permute-start(bf16[128,4096]{1,0:T(8,128)(2,1)} %refs_0_.3), channel_id=1, source_target_pairs={{0,16},{8,24},{16,0},{24,8},{1,17},{9,25},{17,1},{25,9},{2,18},{10... | collective-permute-start | bytes 3145736 | tf_op jit(solution)/shard_map/ppermute | solution.py:106
  7.6 1.6 %gather_fusion.1 = s32[128]{0:T(128)S(1)} fusion(s32[2048]{0:T(1024)} %param.11, s32[1024]{0:T(1024)S(1)} %pad_clamp_fusion.2), kind=kCustom, calls=%fused_computation.1 | custom fusion | bytes 1536 | tf_op jit(solution)/shard_map/jit(_take)/gather | solution.py:111
  14.0 2.3 %reduce.3 = bf16[32,4128]{1,0:T(8,128)(2,1)S(1)} reduce(bf16[32,1,4128]{2,1,0:T(2,128)(2,1)S(1)} %all_to_all.12, bf16[]{:T(256)} %broadcast.156), dimensions={1}, to_apply=%all_to_all.12.reduce_sub_computation | reduce | bytes 528386 | tf_op jit(solution)/shard_map/all_to_all | solution.py:132
  17.2 6.3 %all-to-all-start = ((bf16[32,2,2064]{2,1,0:T(2,128)(2,1)}), bf16[32,2,2064]{2,1,0:T(2,128)(2,1)S(1)}, u32[]{:S(2)}, u32[]{:S(2)}) async-start(bf16[32,2,2064]{2,1,0:T(2,128)(2,1)} %reshape.167), calls=%async_computation | async-start | bytes 557056 | tf_op jit(solution)/shard_map/all_to_all | solution.py:132
  23.5 1.1 fusion.29
  25.4 27.9 %all-to-all-done = bf16[32,2,2064]{2,1,0:T(2,128)(2,1)S(1)} async-done(((bf16[32,2,2064]{2,1,0:T(2,128)(2,1)}), bf16[32,2,2064]{2,1,0:T(2,128)(2,1)S(1)}, u32[]{:S(2)}, u32[]{:S(2)}) %all-to-all-start) | async-done | bytes 264224 | tf_op jit(solution)/shard_map/all_to_all | solution.py:132
  53.6 1.7 %reduce = bf16[32,4128]{1,0:T(8,128)(2,1)S(1)} reduce(bf16[32,1,4128]{2,1,0:T(2,128)(2,1)S(1)} %reshape.168, bf16[]{:T(256)} %constant.121), dimensions={1}, to_apply=%all_to_all.10.reduce_sub_computation | reduce | bytes 528386 | tf_op jit(solution)/shard_map/all_to_all | solution.py:132
  55.2 1.5 %reshape.125 = bf16[32,4,8,129]{3,2,1,0:T(8,128)(2,1)S(1)} reshape(bf16[32,4128]{1,0:T(8,128)(2,1)S(1)} %reduce) | data formatting | bytes 528384 | tf_op jit(solution)/shard_map/reshape | solution.py:133
  59.6 20.1 %shard_map.100 = f32[1024,128]{1,0:T(8,128)} custom-call(bf16[4,256,128]{2,1,0:T(8,128)(2,1)} %slice.56.x_ref, bf16[128,4096]{1,0:T(8,128)(2,1)} %refs_0_.3, bf16[128,4096]{1,0:T(8,128)(2,1)} %copy-done.2, bf16[128,4096]{1,0:T(8,128)(2,1)} %collective-permute-done.1.refs_2_, bf16[128,4096]{1,0:T(8,128)(2,1)} %collective-permute-done.2.refs_3_, ...), custom_call_target="tpu_custom_call" | custom-call | flops 10334765056 | bytes 13369344 | tf_op jit(solution)/shard_map/pallas_call | solution.py:58
  79.7 1.1 fusion.28
  80.8 1.1 collective-permute-start.3
  81.9 1.0 collective-permute-start.4
  82.9 1.4 %collective-permute-start.5 = (f32[256,128]{1,0:T(8,128)S(1)}, f32[256,128]{1,0:T(8,128)S(1)}, u32[]{:S(2)}, u32[]{:S(2)}) collective-permute-start(f32[256,128]{1,0:T(8,128)S(1)} %get-tuple-element.13), channel_id=1, source_target_pairs={{0,24},{8,16},{16,8},{24,0},{1,25},{9,17},{17,9},{25,1},{2,26},{10... | collective-permute-start | bytes 393224 | tf_op jit(solution)/shard_map/ppermute | solution.py:145
  84.3 2.5 %collective-permute-done.3 = f32[256,128]{1,0:T(8,128)S(1)} collective-permute-done((f32[256,128]{1,0:T(8,128)S(1)}, f32[256,128]{1,0:T(8,128)S(1)}, u32[]{:S(2)}, u32[]{:S(2)}) %collective-permute-start.3) | collective-permute-done | bytes 131104 | tf_op jit(solution)/shard_map/ppermute | solution.py:145
  86.8 1.6 %collective-permute-done.4 = f32[256,128]{1,0:T(8,128)S(1)} collective-permute-done((f32[256,128]{1,0:T(8,128)S(1)}, f32[256,128]{1,0:T(8,128)S(1)}, u32[]{:S(2)}, u32[]{:S(2)}) %collective-permute-start.4) | collective-permute-done | bytes 131104 | tf_op jit(solution)/shard_map/ppermute | solution.py:145
  88.4 1.6 %collective-permute-done.5 = f32[256,128]{1,0:T(8,128)S(1)} collective-permute-done((f32[256,128]{1,0:T(8,128)S(1)}, f32[256,128]{1,0:T(8,128)S(1)}, u32[]{:S(2)}, u32[]{:S(2)}) %collective-permute-start.5) | collective-permute-done | bytes 131104 | tf_op jit(solution)/shard_map/ppermute | solution.py:145
  91.7 1.6 %collective-permute-start.7 = (bf16[256,128]{1,0:T(8,128)(2,1)S(1)}, bf16[256,128]{1,0:T(8,128)(2,1)S(1)}, u32[]{:S(2)}, u32[]{:S(2)}) collective-permute-start(bf16[256,128]{1,0:T(8,128)(2,1)S(1)} %fusion.14), channel_id=1, source_target_pairs={{0,16},{8,24},{16,0},{24,8},{1,17},{9,25},{17,1},{25,9},{2,18},{10... | collective-permute-start | bytes 196616 | tf_op jit(solution)/shard_map/ppermute | solution.py:150
  93.3 1.2 collective-permute-start.8
  94.5 1.0 collective-permute-done.6
  95.5 1.0 collective-permute-done.7
  96.5 2.0 %collective-permute-done.8 = bf16[256,128]{1,0:T(8,128)(2,1)S(1)} collective-permute-done((bf16[256,128]{1,0:T(8,128)(2,1)S(1)}, bf16[256,128]{1,0:T(8,128)(2,1)S(1)}, u32[]{:S(2)}, u32[]{:S(2)}) %collective-permute-start.8) | collective-permute-done | bytes 65568 | tf_op jit(solution)/shard_map/ppermute | solution.py:150
  99.4 20.1 %shard_map.101 = f32[1024,128]{1,0:T(8,128)} custom-call(bf16[4,256,128]{2,1,0:T(8,128)(2,1)} %fusion.x_ref, bf16[128,4096]{1,0:T(8,128)(2,1)} %refs_0_.3, bf16[128,4096]{1,0:T(8,128)(2,1)} %copy-done.2, bf16[128,4096]{1,0:T(8,128)(2,1)} %collective-permute-done.1.refs_2_, bf16[128,4096]{1,0:T(8,128)(2,1)} %collective-permute-done.2.refs_3_, ...), custom_call_target="tpu_custom_call" | custom-call | flops 10334765056 | bytes 13369344 | tf_op jit(solution)/shard_map/pallas_call | solution.py:58
  119.5 1.1 fusion.27
  121.1 1.6 %collective-permute-start.11 = (f32[256,128]{1,0:T(8,128)S(1)}, f32[256,128]{1,0:T(8,128)S(1)}, u32[]{:S(2)}, u32[]{:S(2)}) collective-permute-start(f32[256,128]{1,0:T(8,128)S(1)} %get-tuple-element.10), channel_id=1, source_target_pairs={{0,24},{8,16},{16,8},{24,0},{1,25},{9,17},{17,9},{25,1},{2,26},{10... | collective-permute-start | bytes 393224 | tf_op jit(solution)/shard_map/ppermute | solution.py:145
  122.6 1.5 %collective-permute-start.9 = (f32[256,128]{1,0:T(8,128)S(1)}, f32[256,128]{1,0:T(8,128)S(1)}, u32[]{:S(2)}, u32[]{:S(2)}) collective-permute-start(f32[256,128]{1,0:T(8,128)S(1)} %get-tuple-element.9), channel_id=1, source_target_pairs={{0,8},{8,0},{16,24},{24,16},{1,9},{9,1},{17,25},{25,17},{2,10},{10... | collective-permute-start | bytes 393224 | tf_op jit(solution)/shard_map/ppermute | solution.py:145
  124.1 1.5 %collective-permute-done.10 = f32[256,128]{1,0:T(8,128)S(1)} collective-permute-done((f32[256,128]{1,0:T(8,128)S(1)}, f32[256,128]{1,0:T(8,128)S(1)}, u32[]{:S(2)}, u32[]{:S(2)}) %collective-permute-start.10) | collective-permute-done | bytes 131104 | tf_op jit(solution)/shard_map/ppermute | solution.py:145
  125.6 1.4 collective-permute-done.11
  127.0 1.5 %collective-permute-done.9 = f32[256,128]{1,0:T(8,128)S(1)} collective-permute-done((f32[256,128]{1,0:T(8,128)S(1)}, f32[256,128]{1,0:T(8,128)S(1)}, u32[]{:S(2)}, u32[]{:S(2)}) %collective-permute-start.9) | collective-permute-done | bytes 131104 | tf_op jit(solution)/shard_map/ppermute | solution.py:145
  128.5 1.6 %fusion.15 = bf16[32,8,128]{2,1,0:T(8,128)(2,1)} fusion(f32[256,128]{1,0:T(8,128)S(1)} %collective-permute-done.11, f32[256,128]{1,0:T(8,128)S(1)} %collective-permute-done.10, f32[256,128]{1,0:T(8,128)S(1)} %collective-permute-done.9, f32[1024,128]{1,0:T(8,128)} %shard_map.101), kind=kLoop, calls=%fused_computation.31 | loop fusion | flops 131072 | bytes 589824 | tf_op jit(solution)/shard_map/reshape | solution.py:159
  130.0 4.6 %all-to-all-start.1 = ((bf16[32,8,128]{2,1,0:T(8,128)(2,1)}), bf16[32,8,128]{2,1,0:T(8,128)(2,1)S(1)}, u32[]{:S(2)}, u32[]{:S(2)}) async-start(bf16[32,8,128]{2,1,0:T(8,128)(2,1)} %fusion.15), calls=%async_computation.1 | async-start | bytes 131072 | tf_op jit(solution)/shard_map/all_to_all | solution.py:158
  134.7 7.3 %all-to-all-done.1 = bf16[32,8,128]{2,1,0:T(8,128)(2,1)S(1)} async-done(((bf16[32,8,128]{2,1,0:T(8,128)(2,1)}), bf16[32,8,128]{2,1,0:T(8,128)(2,1)S(1)}, u32[]{:S(2)}, u32[]{:S(2)}) %all-to-all-start.1) | async-done | bytes 65568 | tf_op jit(solution)/shard_map/all_to_all | solution.py:158
  (45 shorter events, 17.2 us)
Async XLA Ops:
  0.0 9.9 %copy-start = (bf16[2048,128]{1,0:T(8,128)(2,1)S(1)}, bf16[2048,128]{1,0:T(8,128)(2,1)}, u32[]{:S(2)}) copy-start(bf16[2048,128]{1,0:T(8,128)(2,1)} %param.10) | copy-start | bytes 1572868
  0.0 58.6 %collective-permute-start = (bf16[128,4096]{1,0:T(8,128)(2,1)}, bf16[128,4096]{1,0:T(8,128)(2,1)S(1)}, u32[]{:S(2)}, u32[]{:S(2)}) collective-permute-start(bf16[128,4096]{1,0:T(8,128)(2,1)} %refs_0_.3), channel_id=1, source_target_pairs={{0,8},{8,0},{16,24},{24,16},{1,9},{9,1},{17,25},{25,17},{2,10},{10... | collective-permute-start | bytes 3145736 | tf_op jit(solution)/shard_map/ppermute | solution.py:106
  3.0 55.7 %collective-permute-start.1 = (bf16[128,4096]{1,0:T(8,128)(2,1)}, bf16[128,4096]{1,0:T(8,128)(2,1)}, u32[]{:S(2)}, u32[]{:S(2)}) collective-permute-start(bf16[128,4096]{1,0:T(8,128)(2,1)} %refs_0_.3), channel_id=1, source_target_pairs={{0,16},{8,24},{16,0},{24,8},{1,17},{9,25},{17,1},{25,9},{2,18},{10... | collective-permute-start | bytes 3145736 | tf_op jit(solution)/shard_map/ppermute | solution.py:106
  4.5 54.2 %collective-permute-start.2 = (bf16[128,4096]{1,0:T(8,128)(2,1)}, bf16[128,4096]{1,0:T(8,128)(2,1)}, u32[]{:S(2)}, u32[]{:S(2)}) collective-permute-start(bf16[128,4096]{1,0:T(8,128)(2,1)} %refs_0_.3), channel_id=1, source_target_pairs={{0,24},{8,16},{16,8},{24,0},{1,25},{9,17},{17,9},{25,1},{2,26},{10... | collective-permute-start | bytes 3145736 | tf_op jit(solution)/shard_map/ppermute | solution.py:106
  17.2 36.1 %all-to-all-start = ((bf16[32,2,2064]{2,1,0:T(2,128)(2,1)}), bf16[32,2,2064]{2,1,0:T(2,128)(2,1)S(1)}, u32[]{:S(2)}, u32[]{:S(2)}) async-start(bf16[32,2,2064]{2,1,0:T(2,128)(2,1)} %reshape.167), calls=%async_computation | async-start | bytes 557056 | tf_op jit(solution)/shard_map/all_to_all | solution.py:132
  58.6 39.9 %copy-start.3 = (bf16[128,128]{1,0:T(8,128)(2,1)S(1)}, bf16[128,128]{1,0:T(8,128)(2,1)}, u32[]{:S(2)}) copy-start(bf16[128,128]{1,0:T(8,128)(2,1)} %param.18) | copy-start | bytes 98308
  58.6 1.0 copy-start.2
  80.8 6.1 %collective-permute-start.3 = (f32[256,128]{1,0:T(8,128)S(1)}, f32[256,128]{1,0:T(8,128)S(1)}, u32[]{:S(2)}, u32[]{:S(2)}) collective-permute-start(f32[256,128]{1,0:T(8,128)S(1)} %get-tuple-element.12), channel_id=1, source_target_pairs={{0,8},{8,0},{16,24},{24,16},{1,9},{9,1},{17,25},{25,17},{2,10},{10... | collective-permute-start | bytes 393224 | tf_op jit(solution)/shard_map/ppermute | solution.py:145
  81.9 6.5 %collective-permute-start.4 = (f32[256,128]{1,0:T(8,128)S(1)}, f32[256,128]{1,0:T(8,128)S(1)}, u32[]{:S(2)}, u32[]{:S(2)}) collective-permute-start(f32[256,128]{1,0:T(8,128)S(1)} %get-tuple-element.14), channel_id=1, source_target_pairs={{0,16},{8,24},{16,0},{24,8},{1,17},{9,25},{17,1},{25,9},{2,18},{10... | collective-permute-start | bytes 393224 | tf_op jit(solution)/shard_map/ppermute | solution.py:145
  82.9 7.1 %collective-permute-start.5 = (f32[256,128]{1,0:T(8,128)S(1)}, f32[256,128]{1,0:T(8,128)S(1)}, u32[]{:S(2)}, u32[]{:S(2)}) collective-permute-start(f32[256,128]{1,0:T(8,128)S(1)} %get-tuple-element.13), channel_id=1, source_target_pairs={{0,24},{8,16},{16,8},{24,0},{1,25},{9,17},{17,9},{25,1},{2,26},{10... | collective-permute-start | bytes 393224 | tf_op jit(solution)/shard_map/ppermute | solution.py:145
  91.0 4.6 %collective-permute-start.6 = (bf16[256,128]{1,0:T(8,128)(2,1)S(1)}, bf16[256,128]{1,0:T(8,128)(2,1)S(1)}, u32[]{:S(2)}, u32[]{:S(2)}) collective-permute-start(bf16[256,128]{1,0:T(8,128)(2,1)S(1)} %fusion.14), channel_id=1, source_target_pairs={{0,8},{8,0},{16,24},{24,16},{1,9},{9,1},{17,25},{25,17},{2,10},{10... | collective-permute-start | bytes 196616 | tf_op jit(solution)/shard_map/ppermute | solution.py:150
  91.7 4.8 %collective-permute-start.7 = (bf16[256,128]{1,0:T(8,128)(2,1)S(1)}, bf16[256,128]{1,0:T(8,128)(2,1)S(1)}, u32[]{:S(2)}, u32[]{:S(2)}) collective-permute-start(bf16[256,128]{1,0:T(8,128)(2,1)S(1)} %fusion.14), channel_id=1, source_target_pairs={{0,16},{8,24},{16,0},{24,8},{1,17},{9,25},{17,1},{25,9},{2,18},{10... | collective-permute-start | bytes 196616 | tf_op jit(solution)/shard_map/ppermute | solution.py:150
  93.3 5.2 %collective-permute-start.8 = (bf16[256,128]{1,0:T(8,128)(2,1)S(1)}, bf16[256,128]{1,0:T(8,128)(2,1)S(1)}, u32[]{:S(2)}, u32[]{:S(2)}) collective-permute-start(bf16[256,128]{1,0:T(8,128)(2,1)S(1)} %fusion.14), channel_id=1, source_target_pairs={{0,24},{8,16},{16,8},{24,0},{1,25},{9,17},{17,9},{25,1},{2,26},{10... | collective-permute-start | bytes 196616 | tf_op jit(solution)/shard_map/ppermute | solution.py:150
  99.4 35.2 %copy-start.1 = (s32[128,1]{0,1:T(1,128)S(1)}, s32[128,1]{0,1:T(1,128)}, u32[]{:S(2)}) copy-start(s32[128,1]{0,1:T(1,128)} %param.13) | copy-start | bytes 1540
  120.6 5.0 %collective-permute-start.10 = (f32[256,128]{1,0:T(8,128)S(1)}, f32[256,128]{1,0:T(8,128)S(1)}, u32[]{:S(2)}, u32[]{:S(2)}) collective-permute-start(f32[256,128]{1,0:T(8,128)S(1)} %get-tuple-element.11), channel_id=1, source_target_pairs={{0,16},{8,24},{16,0},{24,8},{1,17},{9,25},{17,1},{25,9},{2,18},{10... | collective-permute-start | bytes 393224 | tf_op jit(solution)/shard_map/ppermute | solution.py:145
  121.1 5.9 %collective-permute-start.11 = (f32[256,128]{1,0:T(8,128)S(1)}, f32[256,128]{1,0:T(8,128)S(1)}, u32[]{:S(2)}, u32[]{:S(2)}) collective-permute-start(f32[256,128]{1,0:T(8,128)S(1)} %get-tuple-element.10), channel_id=1, source_target_pairs={{0,24},{8,16},{16,8},{24,0},{1,25},{9,17},{17,9},{25,1},{2,26},{10... | collective-permute-start | bytes 393224 | tf_op jit(solution)/shard_map/ppermute | solution.py:145
  122.6 5.8 %collective-permute-start.9 = (f32[256,128]{1,0:T(8,128)S(1)}, f32[256,128]{1,0:T(8,128)S(1)}, u32[]{:S(2)}, u32[]{:S(2)}) collective-permute-start(f32[256,128]{1,0:T(8,128)S(1)} %get-tuple-element.9), channel_id=1, source_target_pairs={{0,8},{8,0},{16,24},{24,16},{1,9},{9,1},{17,25},{25,17},{2,10},{10... | collective-permute-start | bytes 393224 | tf_op jit(solution)/shard_map/ppermute | solution.py:145
  130.0 12.0 %all-to-all-start.1 = ((bf16[32,8,128]{2,1,0:T(8,128)(2,1)}), bf16[32,8,128]{2,1,0:T(8,128)(2,1)S(1)}, u32[]{:S(2)}, u32[]{:S(2)}) async-start(bf16[32,8,128]{2,1,0:T(8,128)(2,1)} %fusion.15), calls=%async_computation.1 | async-start | bytes 131072 | tf_op jit(solution)/shard_map/all_to_all | solution.py:158
